TPU v7x, 256 devices: a whole 4x4x8 slice. The times are simulated.
256 devices in a mesh: leaf: 4 (over y), row: 8 (over z), col: 8 (over x, core).
Axes of the slice: x: 4, y: 4, z: 8, core: 2. Of those that a mesh axis runs over, the one named last changes fastest.
Arguments:
- rhs: float32 [4, 4, 8, 256, 256], P('leaf', None, 'row'), may hold values from -6 to 6
- rhs_top: float32 [2, 8, 256, 256], P(None, 'row'), may hold values from -6 to 6
- factor: bfloat16 [4, 4, 8, 4, 8, 256, 256], P('leaf', None, 'row', None, 'col'), may hold values from -0.125 to 0.125
- factor_inv: bfloat16 [4, 2, 4, 8, 256, 256], P('leaf', None, None, 'row')
- lower_bridge: bfloat16 [4, 2, 8, 4, 8, 256, 256], P('leaf', None, 'row', None, 'col'), may hold values from -0.0625 to 0.0625
- upper_bridge: bfloat16 [4, 4, 8, 2, 8, 256, 256], P('leaf', None, 'row', None, 'col'), may hold values from -0.1875 to 0.1875
- top_factor: bfloat16 [2, 8, 2, 8, 256, 256], P(None, 'row', None, 'col'), may hold values from -0.1875 to 0.1875
- top_inv: bfloat16 [2, 2, 8, 256, 256], P(None, None, 'row')
- widths: int32 [4, 4, 8], P('leaf', None, 'row'), may hold values from 128 to 256, as said below
- pattern: int32 [4, 4, 8, 4, 8], P('leaf', None, 'row', None, 'col'), may hold values 0 or 1
- lower_links: int32 [4, 2, 8, 4, 8], P('leaf', None, 'row', None, 'col'), may hold values 0 or 1
- upper_links: int32 [4, 4, 8, 2, 8], P('leaf', None, 'row', None, 'col'), may hold values 0 or 1
- top_pattern: int32 [2, 8, 2, 8], P(None, 'row', None, 'col'), may hold values 0 or 1
Outputs:
- solution: float32 [4, 4, 8, 256, 256], P('leaf', None, 'row', None, 'col')
- solution_top: float32 [2, 8, 256, 256], P(None, 'row', None, 'col')
Inputs may be any that keep to these rules, and one draw needn't show every extreme that they name: widths of supernodes; the largest is 256 in every subtree.
All inputs are finite; a program needn't handle non-finite values. No bound on the sum of `pattern` or of `lower_links` or of `upper_links` or of `top_pattern` on one device may be relied on, other than what follows from the above.
Results may differ from a plain program's by a relative error of at most 0.02.
Values may be sent and summed in bfloat16 or wider, within the bound.
No kernel may reach another device: no remote copies, remote signals or barrier semaphores. Data moves between devices by JAX's collectives and lax.ppermute only.
A program may use at most 64 MiB of HBM per device.

v0:
```python
import jax
import jax.numpy as jnp
from jax import lax
from jax.sharding import PartitionSpec as P


def masked(blocks, marks):
    return blocks * marks.astype(jnp.bfloat16)[..., None, None]


def column_part(full, width):
    start = lax.axis_index("col") * width
    return lax.dynamic_slice_in_dim(full, start, width, 0)


def settle(partial_value, target, inverse, keep):
    share = lax.psum_scatter(partial_value, "col", scatter_dimension=2, tiled=True)
    resid = (target - share).astype(jnp.bfloat16)
    solved = keep * jnp.einsum("ibk,ikr->ibr", inverse, resid, preferred_element_type=jnp.float32)
    pieces = lax.all_gather(solved.astype(jnp.bfloat16)[None], ("row", "col"), axis=0, tiled=True)
    nrows = lax.axis_size("row")
    ncols = lax.axis_size("col")
    pieces = pieces.reshape((nrows, ncols) + solved.shape)
    full = jnp.transpose(pieces, (0, 2, 3, 1, 4)).reshape(
        nrows * solved.shape[0], solved.shape[1], ncols * solved.shape[2]
    )
    return (solved, full)


def shards(
    rhs,
    rhs_top,
    factor,
    factor_inv,
    lower_bridge,
    upper_bridge,
    top_factor,
    top_inv,
    widths,
    pattern,
    lower_links,
    upper_links,
    top_pattern,
):
    f32 = jnp.float32
    levels = factor.shape[1]
    tops = top_factor.shape[0]
    row_count = factor.shape[2]
    col_count = factor.shape[4]
    block = factor.shape[5]
    sides = rhs.shape[4]
    share_width = sides // lax.axis_size("col")
    col_start = lax.axis_index("col") * share_width
    local_rhs = lax.dynamic_slice_in_dim(rhs[0], col_start, share_width, 3)
    local_top = lax.dynamic_slice_in_dim(rhs_top, col_start, share_width, 3)
    fmask = masked(factor[0], pattern[0])
    lmask = masked(lower_bridge[0], lower_links[0])
    umask = masked(upper_bridge[0], upper_links[0])
    tmask = masked(top_factor, top_pattern)
    marks = lax.broadcasted_iota(jnp.int32, (levels, row_count, block, 1), 2)
    keep = (marks < widths[0][..., None, None]).astype(f32)
    ys = []
    ycols = []
    for level in range(levels):
        if level == 0:
            partial_value = jnp.zeros((row_count, block, sides), f32)
        else:
            partial_value = jnp.einsum(
                "iljbk,ljkr->ibr",
                fmask[level, :, :level],
                jnp.stack(ycols, 0),
                preferred_element_type=f32,
            )
        solved, full = settle(partial_value, local_rhs[level], factor_inv[0, 0, level], keep[level])
        ys.append(solved)
        ycols.append(column_part(full, col_count))
    coupling = jnp.einsum(
        "tiljbk,ljkr->tibr", lmask, jnp.stack(ycols, 0), preferred_element_type=f32
    )
    coupling = lax.psum(coupling, "leaf")
    yts = []
    tcols = []
    for top in range(tops):
        partial_value = coupling[top]
        if top > 0:
            partial_value = partial_value + jnp.einsum(
                "iljbk,ljkr->ibr",
                tmask[top, :, :top],
                jnp.stack(tcols, 0),
                preferred_element_type=f32,
            )
        solved, full = settle(partial_value, local_top[top], top_inv[0, top], 1.0)
        yts.append(solved)
        tcols.append(column_part(full, col_count))
    zts = [None] * tops
    zt_cols = [None] * tops
    for top in reversed(range(tops)):
        if top == tops - 1:
            partial_value = jnp.zeros((row_count, block, sides), f32)
        else:
            partial_value = jnp.einsum(
                "iljbk,ljkr->ibr",
                tmask[top, :, top + 1 :],
                jnp.stack(zt_cols[top + 1 :], 0),
                preferred_element_type=f32,
            )
        solved, full = settle(partial_value, yts[top], top_inv[1, top], 1.0)
        zts[top] = solved
        zt_cols[top] = column_part(full, col_count)
    top_stack = jnp.stack(zt_cols, 0)
    zs = [None] * levels
    zcols = [None] * levels
    for level in reversed(range(levels)):
        partial_value = jnp.einsum(
            "itjbk,tjkr->ibr", umask[level], top_stack, preferred_element_type=f32
        )
        if level < levels - 1:
            partial_value = partial_value + jnp.einsum(
                "iljbk,ljkr->ibr",
                fmask[level, :, level + 1 :],
                jnp.stack(zcols[level + 1 :], 0),
                preferred_element_type=f32,
            )
        solved, full = settle(partial_value, ys[level], factor_inv[0, 1, level], keep[level])
        zs[level] = solved
        zcols[level] = column_part(full, col_count)
    result = jnp.stack(zs, 0)
    result_top = jnp.stack(zts, 0)
    return (result[None], result_top)


def solution(mesh):
    placed = (
        P("leaf", None, "row", None, None),
        P(None, "row", None, None),
        P("leaf", None, "row", None, "col", None, None),
        P("leaf", None, None, "row", None, None),
        P("leaf", None, "row", None, "col", None, None),
        P("leaf", None, "row", None, "col", None, None),
        P(None, "row", None, "col", None, None),
        P(None, None, "row", None, None),
        P("leaf", None, "row"),
        P("leaf", None, "row", None, "col"),
        P("leaf", None, "row", None, "col"),
        P("leaf", None, "row", None, "col"),
        P(None, "row", None, "col"),
    )
    return jax.shard_map(
        shards,
        mesh=mesh,
        in_specs=placed,
        out_specs=(P("leaf", None, "row", None, "col"), P(None, "row", None, "col")),
        check_vma=False,
    )
```

profile of v0, /device:TPU:96, one launch (start us, length us, event | category | flops | bytes accessed | tf_op | source)
XLA Modules:
  0.0 1328.3 jit_solution(12221357856252894785)
XLA Ops:
  9.5 1.7 bitcast_convert_fusion.9
  12.0 1.8 bitcast_multiply_fusion
  13.8 68.9 %all-gather.21.cloned.1.call-done = bf16[16384,32]{0,1:T(8,128)(2,1)} async-done(((bf16[256,32]{0,1:T(8,128)(2,1)}), bf16[16384,32]{0,1:T(8,128)(2,1)}) %all-gather.21.cloned.1.call-update) | async-done | bytes 1048592 | tf_op jit(solution)/shard_map/all_gather | solution.py:20
  85.9 1.7 fusion.99
  87.6 1.6 copy.157
  91.1 60.1 %all-reduce.14.cloned.1.call-done = f32[1,256,256]{1,0,2:T(1,128)} async-done(((f32[1,256,256]{1,0,2:T(1,128)}), f32[1,256,256]{1,0,2:T(1,128)}) %all-reduce.14.cloned.1.call-update) | async-done | bytes 262160
  152.0 1.7 bitcast_convert_fusion.8
  154.5 68.4 %all-gather.23.cloned.1.call-done = bf16[16384,32]{0,1:T(8,128)(2,1)} async-done(((bf16[256,32]{0,1:T(8,128)(2,1)}), bf16[16384,32]{0,1:T(8,128)(2,1)}) %all-gather.23.cloned.1.call-update) | async-done | bytes 1048592 | tf_op jit(solution)/shard_map/all_gather | solution.py:20
  225.8 1.9 convolution_bitcast_fusion.8
  227.7 1.8 copy.101
  229.6 65.3 %all-reduce.16.cloned.1.call-done = f32[1,256,256]{1,0,2:T(1,128)} async-done(((f32[1,256,256]{1,0,2:T(1,128)}), f32[1,256,256]{1,0,2:T(1,128)}) %all-reduce.16.cloned.1.call-update) | async-done | bytes 262160
  295.6 1.7 bitcast_convert_fusion.7
  297.4 68.6 %all-gather.25.cloned.1.call-done = bf16[16384,32]{0,1:T(8,128)(2,1)} async-done(((bf16[256,32]{0,1:T(8,128)(2,1)}), bf16[16384,32]{0,1:T(8,128)(2,1)}) %all-gather.25.cloned.1.call-update) | async-done | bytes 1048592 | tf_op jit(solution)/shard_map/all_gather | solution.py:20
  368.9 2.0 convolution_bitcast_fusion.7
  370.9 1.8 copy.105
  372.8 65.3 %all-reduce.18.cloned.1.call-done = f32[1,256,256]{1,0,2:T(1,128)} async-done(((f32[1,256,256]{1,0,2:T(1,128)}), f32[1,256,256]{1,0,2:T(1,128)}) %all-reduce.18.cloned.1.call-update) | async-done | bytes 262160
  438.8 1.7 bitcast_convert_fusion.6
  441.8 67.4 %all-gather.27.cloned.1.call-done = bf16[16384,32]{0,1:T(8,128)(2,1)} async-done(((bf16[256,32]{0,1:T(8,128)(2,1)}), bf16[16384,32]{0,1:T(8,128)(2,1)}) %all-gather.27.cloned.1.call-update) | async-done | bytes 1048592 | tf_op jit(solution)/shard_map/all_gather | solution.py:20
  512.1 2.6 convolution_bitcast_fusion
  514.8 48.2 %all-reduce.12.cloned.1.call-done = f32[2,1,256,256]{3,2,0,1:T(8,128)} async-done(((f32[2,1,256,256]{3,2,0,1:T(8,128)}), f32[2,1,256,256]{3,2,0,1:T(8,128)}) %all-reduce.12.cloned.1.call-update) | async-done | bytes 524304 | tf_op jit(solution)/shard_map/psum | solution.py:80
  566.0 65.3 %all-reduce.20.cloned.1.call-done = f32[1,256,256]{1,0,2:T(1,128)} async-done(((f32[1,256,256]{1,0,2:T(1,128)}), f32[1,256,256]{1,0,2:T(1,128)}) %all-reduce.20.cloned.1.call-update) | async-done | bytes 262160
  632.0 1.7 bitcast_convert_fusion.5
  634.5 1.9 broadcast_multiply_fusion
  636.5 66.0 %all-gather.29.cloned.1.call-done = bf16[16384,32]{0,1:T(8,128)(2,1)} async-done(((bf16[256,32]{0,1:T(8,128)(2,1)}), bf16[16384,32]{0,1:T(8,128)(2,1)}) %all-gather.29.cloned.1.call-update) | async-done | bytes 1048592 | tf_op jit(solution)/shard_map/all_gather | solution.py:20
  702.4 1.5 copy.164
  706.7 65.3 %all-reduce.22.cloned.1.call-done = f32[1,256,256]{1,0,2:T(1,128)} async-done(((f32[1,256,256]{1,0,2:T(1,128)}), f32[1,256,256]{1,0,2:T(1,128)}) %all-reduce.22.cloned.1.call-update) | async-done | bytes 262160
  772.7 1.9 bitcast_convert_fusion.4
  774.7 68.6 %all-gather.31.cloned.1.call-done = bf16[16384,32]{0,1:T(8,128)(2,1)} async-done(((bf16[256,32]{0,1:T(8,128)(2,1)}), bf16[16384,32]{0,1:T(8,128)(2,1)}) %all-gather.31.cloned.1.call-update) | async-done | bytes 1048592 | tf_op jit(solution)/shard_map/all_gather | solution.py:20
  845.4 1.8 convolution_bitcast_fusion.9
  847.3 33.4 %reduce-scatter.6.cloned.1.call-done = f32[1,256,32]{1,2,0:T(8,128)} async-done(((f32[1,256,256]{1,2,0:T(8,128)}), f32[1,256,32]{1,2,0:T(8,128)}) %reduce-scatter.6.cloned.1.call-update) | async-done | bytes 32784 | tf_op jit(solution)/shard_map/reduce_scatter | solution.py:17
  880.7 1.7 bitcast_convert_fusion.3
  882.6 2.4 bitcast_multiply_fusion.3
  885.1 67.0 %all-gather.33.cloned.1.call-done = bf16[16384,32]{0,1:T(8,128)(2,1)} async-done(((bf16[256,32]{0,1:T(8,128)(2,1)}), bf16[16384,32]{0,1:T(8,128)(2,1)}) %all-gather.33.cloned.1.call-update) | async-done | bytes 1048592 | tf_op jit(solution)/shard_map/all_gather | solution.py:20
  954.2 1.9 convolution_bitcast_fusion.3
  956.3 33.3 %reduce-scatter.8.cloned.1.call-done = f32[1,256,32]{1,2,0:T(8,128)} async-done(((f32[1,256,256]{1,2,0:T(8,128)}), f32[1,256,32]{1,2,0:T(8,128)}) %reduce-scatter.8.cloned.1.call-update) | async-done | bytes 32784 | tf_op jit(solution)/shard_map/reduce_scatter | solution.py:17
  989.6 1.7 bitcast_convert_fusion.2
  991.6 2.0 convolution_bitcast_fusion.4
  993.5 67.5 %all-gather.35.cloned.1.call-done = bf16[16384,32]{0,1:T(8,128)(2,1)} async-done(((bf16[256,32]{0,1:T(8,128)(2,1)}), bf16[16384,32]{0,1:T(8,128)(2,1)}) %all-gather.35.cloned.1.call-update) | async-done | bytes 1048592 | tf_op jit(solution)/shard_map/all_gather | solution.py:20
  1061.0 1.5 copy.167
  1064.2 33.4 %reduce-scatter.10.cloned.1.call-done = f32[1,256,32]{1,2,0:T(8,128)} async-done(((f32[1,256,256]{1,2,0:T(8,128)}), f32[1,256,32]{1,2,0:T(8,128)}) %reduce-scatter.10.cloned.1.call-update) | async-done | bytes 32784 | tf_op jit(solution)/shard_map/reduce_scatter | solution.py:17
  1097.5 1.7 bitcast_convert_fusion.1
  1100.1 68.2 %all-gather.37.cloned.1.call-done = bf16[16384,32]{0,1:T(8,128)(2,1)} async-done(((bf16[256,32]{0,1:T(8,128)(2,1)}), bf16[16384,32]{0,1:T(8,128)(2,1)}) %all-gather.37.cloned.1.call-update) | async-done | bytes 1048592 | tf_op jit(solution)/shard_map/all_gather | solution.py:20
  1172.5 1.9 fusion.5
  1174.5 33.4 %reduce-scatter.12.cloned.1.call-done = f32[1,256,32]{1,2,0:T(8,128)} async-done(((f32[1,256,256]{1,2,0:T(8,128)}), f32[1,256,32]{1,2,0:T(8,128)}) %reduce-scatter.12.cloned.1.call-update) | async-done | bytes 32784 | tf_op jit(solution)/shard_map/reduce_scatter | solution.py:17
  1207.9 1.7 bitcast_convert_fusion
  1209.7 69.5 %all-gather.39.cloned.1.call-done = bf16[16384,32]{0,1:T(8,128)(2,1)} async-done(((bf16[256,32]{0,1:T(8,128)(2,1)}), bf16[16384,32]{0,1:T(8,128)(2,1)}) %all-gather.39.cloned.1.call-update) | async-done | bytes 1048592 | tf_op jit(solution)/shard_map/all_gather | solution.py:20
  1283.5 2.0 fusion.3
  1286.1 32.8 %reduce-scatter.14.cloned.1.call-done = f32[1,256,32]{1,2,0:T(8,128)} async-done(((f32[1,256,256]{1,2,0:T(8,128)}), f32[1,256,32]{1,2,0:T(8,128)}) %reduce-scatter.14.cloned.1.call-update) | async-done | bytes 32784 | tf_op jit(solution)/shard_map/reduce_scatter | solution.py:17
  (140 shorter events, 47.7 us)
Async XLA Ops:
  7.2 1.2 copy-start
  7.2 75.5 %all-gather.21.cloned.1.call-start = ((), (), s32[]{:S(2)}) async-start(), calls=%async_computation.11 | async-start | bytes 1064960 | tf_op jit(solution)/shard_map/all_gather | solution.py:20
  8.6 3.4 copy-start.1
  11.2 140.0 %all-reduce.14.cloned.1.call-start = ((), (), s32[]{:S(2)}) async-start(), calls=%async_computation.21 | async-start | bytes 524288
  85.8 137.1 %all-gather.23.cloned.1.call-start = ((), (), s32[]{:S(2)}) async-start(), calls=%async_computation.12 | async-start | bytes 1064960 | tf_op jit(solution)/shard_map/all_gather | solution.py:20
  153.7 141.2 %all-reduce.16.cloned.1.call-start = ((), (), s32[]{:S(2)}) async-start(), calls=%async_computation.22 | async-start | bytes 524288
  229.5 136.5 %all-gather.25.cloned.1.call-start = ((), (), s32[]{:S(2)}) async-start(), calls=%async_computation.13 | async-start | bytes 1064960 | tf_op jit(solution)/shard_map/all_gather | solution.py:20
  297.4 140.7 %all-reduce.18.cloned.1.call-start = ((), (), s32[]{:S(2)}) async-start(), calls=%async_computation.23 | async-start | bytes 524288
  366.0 2.9 copy-start.6
  372.7 136.5 %all-gather.27.cloned.1.call-start = ((), (), s32[]{:S(2)}) async-start(), calls=%async_computation.14 | async-start | bytes 1064960 | tf_op jit(solution)/shard_map/all_gather | solution.py:20
  440.6 122.4 %all-reduce.12.cloned.1.call-start = ((), (), s32[]{:S(2)}) async-start(), calls=%async_computation.5 | async-start | bytes 1048576 | tf_op jit(solution)/shard_map/psum | solution.py:80
  509.2 2.9 copy-start.7
  514.7 116.6 %all-reduce.20.cloned.1.call-start = ((), (), s32[]{:S(2)}) async-start(), calls=%async_computation.24 | async-start | bytes 524288
  564.8 137.7 %all-gather.29.cloned.1.call-start = ((), (), s32[]{:S(2)}) async-start(), calls=%async_computation.15 | async-start | bytes 1064960 | tf_op jit(solution)/shard_map/all_gather | solution.py:20
  633.8 138.2 %all-reduce.22.cloned.1.call-start = ((), (), s32[]{:S(2)}) async-start(), calls=%async_computation.25 | async-start | bytes 524288
  702.4 2.1 copy-start.2
  706.6 136.7 %all-gather.31.cloned.1.call-start = ((), (), s32[]{:S(2)}) async-start(), calls=%async_computation.16 | async-start | bytes 1064960 | tf_op jit(solution)/shard_map/all_gather | solution.py:20
  774.6 106.1 %reduce-scatter.6.cloned.1.call-start = ((), (), s32[]{:S(2)}) async-start(), calls=%async_computation.6 | async-start | bytes 294912 | tf_op jit(solution)/shard_map/reduce_scatter | solution.py:17
  844.7 35.9 %copy-start.5 = (f32[32,256]{1,0:T(8,128)S(1)}, f32[32,256]{1,0:T(8,128)}, u32[]{:S(2)}) copy-start(f32[32,256]{1,0:T(8,128)} %get-tuple-element.28) | copy-start | bytes 98308
  844.8 37.7 %copy-start.12 = (s32[1,4,1,2,1]{1,4,3,2,0:T(1,128)S(1)}, s32[1,4,1,2,1]{1,4,3,2,0:T(1,128)}, u32[]{:S(2)}) copy-start(s32[1,4,1,2,1]{1,4,3,2,0:T(1,128)} %param.24) | copy-start | bytes 100
  847.2 104.8 %all-gather.33.cloned.1.call-start = ((), (), s32[]{:S(2)}) async-start(), calls=%async_computation.17 | async-start | bytes 1064960 | tf_op jit(solution)/shard_map/all_gather | solution.py:20
  882.4 107.1 %reduce-scatter.8.cloned.1.call-start = ((), (), s32[]{:S(2)}) async-start(), calls=%async_computation.7 | async-start | bytes 294912 | tf_op jit(solution)/shard_map/reduce_scatter | solution.py:17
  956.2 104.8 %all-gather.35.cloned.1.call-start = ((), (), s32[]{:S(2)}) async-start(), calls=%async_computation.18 | async-start | bytes 1064960 | tf_op jit(solution)/shard_map/all_gather | solution.py:20
  991.4 106.2 %reduce-scatter.10.cloned.1.call-start = ((), (), s32[]{:S(2)}) async-start(), calls=%async_computation.8 | async-start | bytes 294912 | tf_op jit(solution)/shard_map/reduce_scatter | solution.py:17
  1061.0 2.1 copy-start.3
  1064.1 104.2 %all-gather.37.cloned.1.call-start = ((), (), s32[]{:S(2)}) async-start(), calls=%async_computation.19 | async-start | bytes 1064960 | tf_op jit(solution)/shard_map/all_gather | solution.py:20
  1099.3 108.6 %reduce-scatter.12.cloned.1.call-start = ((), (), s32[]{:S(2)}) async-start(), calls=%async_computation.9 | async-start | bytes 294912 | tf_op jit(solution)/shard_map/reduce_scatter | solution.py:17
  1171.2 36.7 %copy-start.4 = (f32[32,256]{1,0:T(8,128)S(1)}, f32[32,256]{1,0:T(8,128)}, u32[]{:S(2)}) copy-start(f32[32,256]{1,0:T(8,128)} %get-tuple-element.22) | copy-start | bytes 98308
  1174.4 104.8 %all-gather.39.cloned.1.call-start = ((), (), s32[]{:S(2)}) async-start(), calls=%async_computation.20 | async-start | bytes 1064960 | tf_op jit(solution)/shard_map/all_gather | solution.py:20
  1209.6 109.3 %reduce-scatter.14.cloned.1.call-start = ((), (), s32[]{:S(2)}) async-start(), calls=%async_computation.10 | async-start | bytes 294912 | tf_op jit(solution)/shard_map/reduce_scatter | solution.py:17
  1282.1 3.4 copy-start.9
  1282.1 3.4 copy-start.10
  1282.1 36.8 %copy-start.8 = (f32[32,256]{1,0:T(8,128)S(1)}, f32[32,256]{1,0:T(8,128)}, u32[]{:S(2)}) copy-start(f32[32,256]{1,0:T(8,128)} %get-tuple-element.20) | copy-start | bytes 98308
  1282.1 37.9 %copy-start.11 = (f32[32,256]{1,0:T(8,128)S(1)}, f32[32,256]{1,0:T(8,128)}, u32[]{:S(2)}) copy-start(f32[32,256]{1,0:T(8,128)} %get-tuple-element.34) | copy-start | bytes 98308
Sparse Core Ops, SparseCore 0:
  11.3 71.2 all-gather.20
  85.9 65.2 all-reduce.13
  154.4 68.4 all-gather.22
  229.6 65.2 all-reduce.15
  297.5 68.4 all-gather.24
  372.8 65.2 all-reduce.17
  440.7 68.4 all-gather.26
  514.8 48.0 all-reduce.11
  565.2 65.9 all-reduce.19
  633.9 68.4 all-gather.28
  706.7 65.2 all-reduce.21
  774.8 68.4 all-gather.30
  847.4 33.2 reduce-scatter.5
  883.8 68.2 all-gather.32
  956.3 33.1 reduce-scatter.7
  992.7 68.3 all-gather.34
  1064.2 33.2 reduce-scatter.9
  1100.0 68.2 all-gather.36
  1174.6 33.2 reduce-scatter.11
  1211.0 68.2 all-gather.38
  1285.6 33.2 reduce-scatter.13
where the time goes:
time: 1330 us
  waiting for transfers between devices  1220 us (92%)
  local copies, waits for them, and re-layouts  45.3 us (3%)
  matrix products  39.4 us (3%)
  between operations  15.4 us (1%)
    all_gather x10, waiting for transfers between devices, settle(): lax.all_gather(solved.astype(jnp.bfloat16)[None], ('row', 'col'), axis=0,...  680 us
    unnamed x26, waiting for transfers between devices  322 us
    reduce_scatter x5, waiting for transfers between devices, settle(): lax.psum_scatter(partial_value, 'col', scatter_dimension=2, tiled=True)  166 us
    psum x1, waiting for transfers between devices, shards(): coupling = lax.psum(coupling, 'leaf')  48.2 us
  transfers between devices with their start and end apart: 21, of which 21 were waited for; matrix products, arithmetic and copies ran while one was open for 1% of the time, Pallas kernels for 0%

commit v1 on v0

v1 whole, which is shorter than its diff:
```python
import jax
import jax.numpy as jnp
from jax import lax
from jax.sharding import PartitionSpec as P

GRID = ("row", "col")


def masked(blocks, marks):
    return blocks * marks.astype(jnp.bfloat16)[..., None, None]


def tree_sum(parts):
    while len(parts) > 1:
        parts = [parts[i] + parts[i + 1] for i in range(0, len(parts), 2)]
    return parts[0]


def to_columns(x, n):
    pairs = [(r * n + c, c * n + r) for r in range(n) for c in range(n)]
    return lax.ppermute(x, GRID, pairs)


def row_sum_on_columns(part, n):
    got = []
    for k in range(n):
        pairs = [(r * n + c, (c ^ k) * n + r) for r in range(n) for c in range(n)]
        got.append(lax.ppermute(part, GRID, pairs))
    return tree_sum(got)


def leaf_sum(x, n):
    got = [x] + [lax.ppermute(x, "leaf", [(g, g ^ k) for g in range(n)]) for k in range(1, n)]
    return tree_sum(got)


def products(blocks, segments):
    return jnp.einsum(
        "jbk,jkr->br", jnp.stack(blocks, 0), jnp.stack(segments, 0), preferred_element_type=jnp.float32
    )


def shards(
    rhs,
    rhs_top,
    factor,
    factor_inv,
    lower_bridge,
    upper_bridge,
    top_factor,
    top_inv,
    widths,
    pattern,
    lower_links,
    upper_links,
    top_pattern,
):
    f32 = jnp.float32
    bf16 = jnp.bfloat16
    n = lax.axis_size("row")
    leaves = lax.axis_size("leaf")
    levels = factor.shape[1]
    tops = top_factor.shape[0]
    block = factor.shape[5]
    sides = rhs.shape[4]
    share = sides // n

    fm = masked(factor[0, :, 0, :, 0], pattern[0, :, 0, :, 0])
    lm = masked(lower_bridge[0, :, 0, :, 0], lower_links[0, :, 0, :, 0])
    um = masked(upper_bridge[0, :, 0, :, 0], upper_links[0, :, 0, :, 0])
    tm = masked(top_factor[:, 0, :, 0], top_pattern[:, 0, :, 0])
    marks = lax.broadcasted_iota(jnp.int32, (levels, block, 1), 1)
    keep_own = (marks < widths[0, :, 0][:, None, None]).astype(f32)
    rhs_own = rhs[0, :, 0]
    inv_own = factor_inv[0, :, :, 0]

    seg0_own = (
        keep_own[0] * jnp.dot(inv_own[0, 0], rhs_own[0].astype(bf16), preferred_element_type=f32)
    ).astype(bf16)
    seg0 = to_columns(seg0_own, n)

    rhs_b = to_columns(rhs_own, n)
    inv_b = to_columns(inv_own, n)
    keep_b = to_columns(keep_own, n)
    top_rhs_b = to_columns(rhs_top[:, 0], n)
    top_inv_b = to_columns(top_inv[:, :, 0], n)

    ys = [keep_b[0] * jnp.dot(inv_b[0, 0], rhs_b[0].astype(bf16), preferred_element_type=f32)]
    segs = [seg0]
    for level in range(1, levels):
        part = products([fm[level, j] for j in range(level)], segs)
        full = row_sum_on_columns(part, n)
        resid = (rhs_b[level] - full).astype(bf16)
        solved = keep_b[level] * jnp.dot(inv_b[0, level], resid, preferred_element_type=f32)
        ys.append(solved)
        segs.append(solved.astype(bf16))

    coupling = jnp.stack([products([lm[t, j] for j in range(levels)], segs) for t in range(tops)], 0)
    coupling = leaf_sum(coupling, leaves)

    yts = []
    tsegs = []
    for top in range(tops):
        part = coupling[top]
        if top > 0:
            part = part + products([tm[top, j] for j in range(top)], tsegs)
        full = row_sum_on_columns(part, n)
        resid = (top_rhs_b[top] - full).astype(bf16)
        solved = jnp.dot(top_inv_b[0, top], resid, preferred_element_type=f32)
        yts.append(solved)
        tsegs.append(solved.astype(bf16))

    zts = [None] * tops
    tback = [None] * tops
    for top in reversed(range(tops)):
        if top == tops - 1:
            resid = yts[top].astype(bf16)
        else:
            part = products([tm[top, j] for j in range(top + 1, tops)], tback[top + 1 :])
            full = row_sum_on_columns(part, n)
            resid = (yts[top] - full).astype(bf16)
        solved = jnp.dot(top_inv_b[1, top], resid, preferred_element_type=f32)
        zts[top] = solved
        tback[top] = solved.astype(bf16)

    zs = [None] * levels
    back = [None] * levels
    for level in reversed(range(levels)):
        blocks = [um[level, t] for t in range(tops)] + [fm[level, j] for j in range(level + 1, levels)]
        part = products(blocks, tback + back[level + 1 :])
        full = row_sum_on_columns(part, n)
        resid = (ys[level] - full).astype(bf16)
        solved = keep_b[level] * jnp.dot(inv_b[1, level], resid, preferred_element_type=f32)
        zs[level] = solved
        back[level] = solved.astype(bf16)

    start = lax.axis_index("row") * share
    chunks = [lax.dynamic_slice_in_dim(z, start, share, 1) for z in zs]
    top_chunks = [lax.dynamic_slice_in_dim(z, start, share, 1) for z in zts]
    result = jnp.stack([to_columns(c, n) for c in chunks], 0)
    result_top = jnp.stack([to_columns(c, n) for c in top_chunks], 0)
    return (result[None, :, None], result_top[:, None])


def solution(mesh):
    assert mesh.shape["row"] == mesh.shape["col"]
    placed = (
        P("leaf", None, "row", None, None),
        P(None, "row", None, None),
        P("leaf", None, "row", None, "col", None, None),
        P("leaf", None, None, "row", None, None),
        P("leaf", None, "row", None, "col", None, None),
        P("leaf", None, "row", None, "col", None, None),
        P(None, "row", None, "col", None, None),
        P(None, None, "row", None, None),
        P("leaf", None, "row"),
        P("leaf", None, "row", None, "col"),
        P("leaf", None, "row", None, "col"),
        P("leaf", None, "row", None, "col"),
        P(None, "row", None, "col"),
    )
    return jax.shard_map(
        shards,
        mesh=mesh,
        in_specs=placed,
        out_specs=(P("leaf", None, "row", None, "col"), P(None, "row", None, "col")),
        check_vma=False,
    )
```

time: 1330 us -> 1030 us (0.77)
  the two profiles are of different devices: /device:TPU:96 before, /device:TPU:7 now
where the time goes in v1:
time: 1030 us; the launch traced here: 1020 us
  waiting for transfers between devices  728 us (71%)
  starting transfers between devices  253 us (25%)
  matrix products  16.2 us (2%)
    ppermute x80, waiting for transfers between devices, row_sum_on_columns(): got.append(lax.ppermute(part, GRID, pairs))  542 us
    ppermute x80, starting transfers between devices, row_sum_on_columns(): got.append(lax.ppermute(part, GRID, pairs))  190 us
    ppermute x12, waiting for transfers between devices, to_columns(): return lax.ppermute(x, GRID, pairs)  175 us
    ppermute x12, starting transfers between devices, to_columns(): return lax.ppermute(x, GRID, pairs)  58.9 us
  transfers between devices with their start and end apart: 95, of which 71 were waited for; matrix products, arithmetic and copies ran while one was open for 2% of the time, Pallas kernels for 0%

profile of v1, /device:TPU:7, one launch (start us, length us, event | category | flops | bytes accessed | tf_op | source)
XLA Modules:
  0.0 1016.5 jit_solution(2279182036625429616)
XLA Ops:
  0.6 8.0 collective-permute-start.1
  12.5 7.0 collective-permute-start.2
  21.9 108.9 %collective-permute-done.4 = bf16[256,256]{1,0:T(8,128)(2,1)S(1)} collective-permute-done((bf16[256,256]{1,0:T(8,128)(2,1)S(1)}, bf16[256,256]{1,0:T(8,128)(2,1)S(1)}, u32[]{:S(2)}, u32[]{:S(2)}) %collective-permute-start.4) | collective-permute-done | bytes 131104 | tf_op jit(solution)/shard_map/ppermute | solution.py:21
  137.7 15.6 %collective-permute-done = f32[4,256,1]{1,2,0:T(1,128)S(1)} collective-permute-done((f32[4,256,1]{1,2,0:T(1,128)S(1)}, f32[4,256,1]{1,2,0:T(1,128)S(1)}, u32[]{:S(2)}, u32[]{:S(2)}) %collective-permute-start) | collective-permute-done | bytes 4128 | tf_op jit(solution)/shard_map/ppermute | solution.py:21
  161.6 10.6 %collective-permute-done.12 = f32[256,256]{1,0:T(8,128)S(1)} collective-permute-done((f32[256,256]{1,0:T(8,128)S(1)}, f32[256,256]{1,0:T(8,128)S(1)}, u32[]{:S(2)}, u32[]{:S(2)}) %collective-permute-start.12) | collective-permute-done | bytes 262176 | tf_op jit(solution)/shard_map/ppermute | solution.py:28
  172.2 14.1 %collective-permute-start.7 = (f32[256,256]{1,0:T(8,128)S(1)}, f32[256,256]{1,0:T(8,128)S(1)}, u32[]{:S(2)}, u32[]{:S(2)}) collective-permute-start(f32[256,256]{1,0:T(8,128)S(1)} %fusion.95), channel_id=1, source_target_pairs={{0,16},{1,24},{2,0},{3,8},{4,48},{5,56},{6,32},{7,40},{8,17},{9,25... | collective-permute-start | bytes 786440 | tf_op jit(solution)/shard_map/ppermute | solution.py:28
  188.3 15.2 %collective-permute-done.7 = f32[256,256]{1,0:T(8,128)S(1)} collective-permute-done((f32[256,256]{1,0:T(8,128)S(1)}, f32[256,256]{1,0:T(8,128)S(1)}, u32[]{:S(2)}, u32[]{:S(2)}) %collective-permute-start.7) | collective-permute-done | bytes 262176 | tf_op jit(solution)/shard_map/ppermute | solution.py:28
  203.4 14.7 %collective-permute-done.8 = f32[256,256]{1,0:T(8,128)S(1)} collective-permute-done((f32[256,256]{1,0:T(8,128)S(1)}, f32[256,256]{1,0:T(8,128)S(1)}, u32[]{:S(2)}, u32[]{:S(2)}) %collective-permute-start.8) | collective-permute-done | bytes 262176 | tf_op jit(solution)/shard_map/ppermute | solution.py:28
  233.5 25.8 %collective-permute-done.13 = f32[256,256]{1,0:T(8,128)S(1)} collective-permute-done((f32[256,256]{1,0:T(8,128)S(1)}, f32[256,256]{1,0:T(8,128)S(1)}, u32[]{:S(2)}, u32[]{:S(2)}) %collective-permute-start.13) | collective-permute-done | bytes 262176 | tf_op jit(solution)/shard_map/ppermute | solution.py:28
  272.6 6.9 collective-permute-done.18
  279.6 10.7 %collective-permute-done.19 = f32[256,256]{1,0:T(8,128)S(1)} collective-permute-done((f32[256,256]{1,0:T(8,128)S(1)}, f32[256,256]{1,0:T(8,128)S(1)}, u32[]{:S(2)}, u32[]{:S(2)}) %collective-permute-start.19) | collective-permute-done | bytes 262176 | tf_op jit(solution)/shard_map/ppermute | solution.py:28
  300.6 12.1 %collective-permute-start.23 = (f32[256,256]{1,0:T(8,128)S(1)}, f32[256,256]{1,0:T(8,128)S(1)}, u32[]{:S(2)}, u32[]{:S(2)}) collective-permute-start(f32[256,256]{1,0:T(8,128)S(1)} %convolution_bitcast_fusion.5), channel_id=1, source_target_pairs={{0,16},{1,24},{2,0},{3,8},{4,48},{5,56},{6,32},{7,40},{8,17},{9,25... | collective-permute-start | bytes 786440 | tf_op jit(solution)/shard_map/ppermute | solution.py:28
  312.9 19.7 %collective-permute-done.21 = f32[256,256]{1,0:T(8,128)S(1)} collective-permute-done((f32[256,256]{1,0:T(8,128)S(1)}, f32[256,256]{1,0:T(8,128)S(1)}, u32[]{:S(2)}, u32[]{:S(2)}) %collective-permute-start.21) | collective-permute-done | bytes 262176 | tf_op jit(solution)/shard_map/ppermute | solution.py:28
  342.7 19.6 %collective-permute-done.26 = f32[256,256]{1,0:T(8,128)S(1)} collective-permute-done((f32[256,256]{1,0:T(8,128)S(1)}, f32[256,256]{1,0:T(8,128)S(1)}, u32[]{:S(2)}, u32[]{:S(2)}) %collective-permute-start.26) | collective-permute-done | bytes 262176 | tf_op jit(solution)/shard_map/ppermute | solution.py:28
  362.4 7.1 collective-permute-done.28
  383.9 7.3 collective-permute-done.30
  397.6 32.3 %collective-permute-start.34 = (f32[256,256]{1,0:T(8,128)S(1)}, f32[256,256]{1,0:T(8,128)S(1)}, u32[]{:S(2)}, u32[]{:S(2)}) collective-permute-start(f32[256,256]{1,0:T(8,128)S(1)} %slice_bitcast_fusion.2), channel_id=1, source_target_pairs={{0,16},{1,24},{2,0},{3,8},{4,48},{5,56},{6,32},{7,40},{8,17},{9,25... | collective-permute-start | bytes 786440 | tf_op jit(solution)/shard_map/ppermute | solution.py:28
  429.9 29.1 %collective-permute-done.40 = bf16[2,2,256,256]{3,2,1,0:T(8,128)(2,1)S(1)} collective-permute-done((bf16[2,2,256,256]{3,2,1,0:T(8,128)(2,1)S(1)}, bf16[2,2,256,256]{3,2,1,0:T(8,128)(2,1)S(1)}, u32[]{:S(2)}, u32[]{:S(2)}) %collective-permute-start.40) | collective-permute-done | bytes 524320 | tf_op jit(solution)/shard_map/ppermute | solution.py:21
  459.0 11.9 %collective-permute-done.3 = f32[2,256,256]{2,1,0:T(8,128)S(1)} collective-permute-done((f32[2,256,256]{2,1,0:T(8,128)S(1)}, f32[2,256,256]{2,1,0:T(8,128)S(1)}, u32[]{:S(2)}, u32[]{:S(2)}) %collective-permute-start.3) | collective-permute-done | bytes 524320 | tf_op jit(solution)/shard_map/ppermute | solution.py:21
  487.2 15.4 %collective-permute-done.36 = f32[256,256]{1,0:T(8,128)S(1)} collective-permute-done((f32[256,256]{1,0:T(8,128)S(1)}, f32[256,256]{1,0:T(8,128)S(1)}, u32[]{:S(2)}, u32[]{:S(2)}) %collective-permute-start.36) | collective-permute-done | bytes 262176 | tf_op jit(solution)/shard_map/ppermute | solution.py:28
  523.8 10.4 %collective-permute-start.43 = (f32[256,256]{1,0:T(8,128)S(1)}, f32[256,256]{1,0:T(8,128)S(1)}, u32[]{:S(2)}, u32[]{:S(2)}) collective-permute-start(f32[256,256]{1,0:T(8,128)S(1)} %fusion.53), channel_id=1, source_target_pairs={{0,16},{1,24},{2,0},{3,8},{4,48},{5,56},{6,32},{7,40},{8,17},{9,25... | collective-permute-start | bytes 786440 | tf_op jit(solution)/shard_map/ppermute | solution.py:28
  534.8 21.4 %collective-permute-done.41 = f32[256,256]{1,0:T(8,128)S(1)} collective-permute-done((f32[256,256]{1,0:T(8,128)S(1)}, f32[256,256]{1,0:T(8,128)S(1)}, u32[]{:S(2)}, u32[]{:S(2)}) %collective-permute-start.41) | collective-permute-done | bytes 262176 | tf_op jit(solution)/shard_map/ppermute | solution.py:28
  561.6 9.2 collective-permute-done.43
  575.8 8.2 collective-permute-done.46
  584.0 7.6 collective-permute-done.47
  606.7 9.6 collective-permute-start.51
  618.9 15.5 %collective-permute-done.49 = f32[256,256]{0,1:T(8,128)S(1)} collective-permute-done((f32[256,256]{0,1:T(8,128)}, f32[256,256]{0,1:T(8,128)S(1)}, u32[]{:S(2)}, u32[]{:S(2)}) %collective-permute-start.49) | collective-permute-done | bytes 262176 | tf_op jit(solution)/shard_map/ppermute | solution.py:28
  653.5 11.9 %collective-permute-done.54 = f32[256,256]{0,1:T(8,128)S(1)} collective-permute-done((f32[256,256]{0,1:T(8,128)}, f32[256,256]{0,1:T(8,128)S(1)}, u32[]{:S(2)}, u32[]{:S(2)}) %collective-permute-start.54) | collective-permute-done | bytes 262176 | tf_op jit(solution)/shard_map/ppermute | solution.py:28
  679.2 8.5 collective-permute-start.57
  696.9 19.5 %collective-permute-done.57 = f32[256,256]{1,0:T(8,128)S(1)} collective-permute-done((f32[256,256]{1,0:T(8,128)S(1)}, f32[256,256]{1,0:T(8,128)S(1)}, u32[]{:S(2)}, u32[]{:S(2)}) %collective-permute-start.57) | collective-permute-done | bytes 262176 | tf_op jit(solution)/shard_map/ppermute | solution.py:28
  721.8 11.4 %collective-permute-done.59 = f32[256,256]{1,0:T(8,128)S(1)} collective-permute-done((f32[256,256]{1,0:T(8,128)S(1)}, f32[256,256]{1,0:T(8,128)S(1)}, u32[]{:S(2)}, u32[]{:S(2)}) %collective-permute-start.59) | collective-permute-done | bytes 262176 | tf_op jit(solution)/shard_map/ppermute | solution.py:28
  742.8 9.9 collective-permute-done.63
  752.7 8.3 collective-permute-done.64
  765.0 8.0 collective-permute-start.67
  773.3 18.4 %collective-permute-done.65 = f32[256,256]{1,0:T(8,128)S(1)} collective-permute-done((f32[256,256]{1,0:T(8,128)S(1)}, f32[256,256]{1,0:T(8,128)S(1)}, u32[]{:S(2)}, u32[]{:S(2)}) %collective-permute-start.65) | collective-permute-done | bytes 262176 | tf_op jit(solution)/shard_map/ppermute | solution.py:28
  797.4 13.9 %collective-permute-done.67 = f32[256,256]{1,0:T(8,128)S(1)} collective-permute-done((f32[256,256]{1,0:T(8,128)S(1)}, f32[256,256]{1,0:T(8,128)S(1)}, u32[]{:S(2)}, u32[]{:S(2)}) %collective-permute-start.67) | collective-permute-done | bytes 262176 | tf_op jit(solution)/shard_map/ppermute | solution.py:28
  820.2 9.9 collective-permute-done.71
  830.1 8.3 collective-permute-done.72
  842.0 7.4 collective-permute-start.75
  851.1 18.2 %collective-permute-done.73 = f32[256,256]{1,0:T(8,128)S(1)} collective-permute-done((f32[256,256]{1,0:T(8,128)S(1)}, f32[256,256]{1,0:T(8,128)S(1)}, u32[]{:S(2)}, u32[]{:S(2)}) %collective-permute-start.73) | collective-permute-done | bytes 262176 | tf_op jit(solution)/shard_map/ppermute | solution.py:28
  874.7 14.8 %collective-permute-done.75 = f32[256,256]{1,0:T(8,128)S(1)} collective-permute-done((f32[256,256]{1,0:T(8,128)S(1)}, f32[256,256]{1,0:T(8,128)S(1)}, u32[]{:S(2)}, u32[]{:S(2)}) %collective-permute-start.75) | collective-permute-done | bytes 262176 | tf_op jit(solution)/shard_map/ppermute | solution.py:28
  897.9 9.7 collective-permute-done.79
  907.6 8.3 collective-permute-done.80
  919.5 7.5 collective-permute-start.83
  930.7 16.0 %collective-permute-done.81 = f32[256,256]{1,0:T(8,128)S(1)} collective-permute-done((f32[256,256]{1,0:T(8,128)S(1)}, f32[256,256]{1,0:T(8,128)S(1)}, u32[]{:S(2)}, u32[]{:S(2)}) %collective-permute-start.81) | collective-permute-done | bytes 262176 | tf_op jit(solution)/shard_map/ppermute | solution.py:28
  952.3 13.9 %collective-permute-done.83 = f32[256,256]{1,0:T(8,128)S(1)} collective-permute-done((f32[256,256]{1,0:T(8,128)S(1)}, f32[256,256]{1,0:T(8,128)S(1)}, u32[]{:S(2)}, u32[]{:S(2)}) %collective-permute-start.83) | collective-permute-done | bytes 262176 | tf_op jit(solution)/shard_map/ppermute | solution.py:28
  973.2 7.0 collective-permute-start.93
  998.0 7.0 collective-permute-start.89
  (288 shorter events, 302.9 us)
Async XLA Ops:
  0.6 217.5 %collective-permute-start.1 = (bf16[2,4,256,256]{3,2,1,0:T(8,128)(2,1)}, bf16[2,4,256,256]{3,2,1,0:T(8,128)(2,1)S(1)}, u32[]{:S(2)}, u32[]{:S(2)}) collective-permute-start(bf16[2,4,256,256]{3,2,1,0:T(8,128)(2,1)} %bitcast.306), channel_id=1, source_target_pairs={{0,0},{1,8},{2,16},{3,24},{4,32},{5,40},{6,48},{7,56},{8,1},{9,9},... | collective-permute-start | bytes 3145736 | tf_op jit(solution)/shard_map/ppermute | solution.py:21
  10.5 120.3 %collective-permute-start.4 = (bf16[256,256]{1,0:T(8,128)(2,1)S(1)}, bf16[256,256]{1,0:T(8,128)(2,1)S(1)}, u32[]{:S(2)}, u32[]{:S(2)}) collective-permute-start(bf16[256,256]{1,0:T(8,128)(2,1)S(1)} %fusion.3), channel_id=1, source_target_pairs={{0,0},{1,8},{2,16},{3,24},{4,32},{5,40},{6,48},{7,56},{8,1},{9,9},... | collective-permute-start | bytes 393224 | tf_op jit(solution)/shard_map/ppermute | solution.py:21
  12.5 205.6 %collective-permute-start.2 = (f32[4,256,256]{2,1,0:T(8,128)}, f32[4,256,256]{2,1,0:T(8,128)S(1)}, u32[]{:S(2)}, u32[]{:S(2)}) collective-permute-start(f32[4,256,256]{2,1,0:T(8,128)} %bitcast.302), channel_id=1, source_target_pairs={{0,0},{1,8},{2,16},{3,24},{4,32},{5,40},{6,48},{7,56},{8,1},{9,9},... | collective-permute-start | bytes 3145736 | tf_op jit(solution)/shard_map/ppermute | solution.py:21
  153.3 32.9 %collective-permute-start.5 = (f32[256,256]{1,0:T(8,128)S(1)}, f32[256,256]{1,0:T(8,128)S(1)}, u32[]{:S(2)}, u32[]{:S(2)}) collective-permute-start(f32[256,256]{1,0:T(8,128)S(1)} %fusion.95), channel_id=1, source_target_pairs={{0,0},{1,8},{2,16},{3,24},{4,32},{5,40},{6,48},{7,56},{8,1},{9,9},... | collective-permute-start | bytes 786440 | tf_op jit(solution)/shard_map/ppermute | solution.py:28
  218.7 40.7 %collective-permute-start.13 = (f32[256,256]{1,0:T(8,128)S(1)}, f32[256,256]{1,0:T(8,128)S(1)}, u32[]{:S(2)}, u32[]{:S(2)}) collective-permute-start(f32[256,256]{1,0:T(8,128)S(1)} %convolution_bitcast_fusion.6), channel_id=1, source_target_pairs={{0,0},{1,8},{2,16},{3,24},{4,32},{5,40},{6,48},{7,56},{8,1},{9,9},... | collective-permute-start | bytes 786440 | tf_op jit(solution)/shard_map/ppermute | solution.py:28
  225.2 40.7 %collective-permute-start.14 = (f32[256,256]{1,0:T(8,128)S(1)}, f32[256,256]{1,0:T(8,128)S(1)}, u32[]{:S(2)}, u32[]{:S(2)}) collective-permute-start(f32[256,256]{1,0:T(8,128)S(1)} %convolution_bitcast_fusion.6), channel_id=1, source_target_pairs={{0,8},{1,0},{2,24},{3,16},{4,40},{5,32},{6,56},{7,48},{8,9},{9,1},... | collective-permute-start | bytes 786440 | tf_op jit(solution)/shard_map/ppermute | solution.py:28
  229.0 37.4 %collective-permute-start.15 = (f32[256,256]{1,0:T(8,128)S(1)}, f32[256,256]{1,0:T(8,128)S(1)}, u32[]{:S(2)}, u32[]{:S(2)}) collective-permute-start(f32[256,256]{1,0:T(8,128)S(1)} %convolution_bitcast_fusion.6), channel_id=1, source_target_pairs={{0,16},{1,24},{2,0},{3,8},{4,48},{5,56},{6,32},{7,40},{8,17},{9,25... | collective-permute-start | bytes 786440 | tf_op jit(solution)/shard_map/ppermute | solution.py:28
  229.0 43.7 %collective-permute-start.16 = (f32[256,256]{1,0:T(8,128)S(1)}, f32[256,256]{1,0:T(8,128)S(1)}, u32[]{:S(2)}, u32[]{:S(2)}) collective-permute-start(f32[256,256]{1,0:T(8,128)S(1)} %convolution_bitcast_fusion.6), channel_id=1, source_target_pairs={{0,24},{1,16},{2,8},{3,0},{4,56},{5,48},{6,40},{7,32},{8,25},{9,17... | collective-permute-start | bytes 786440 | tf_op jit(solution)/shard_map/ppermute | solution.py:28
  233.5 39.1 %collective-permute-start.17 = (f32[256,256]{1,0:T(8,128)S(1)}, f32[256,256]{1,0:T(8,128)S(1)}, u32[]{:S(2)}, u32[]{:S(2)}) collective-permute-start(f32[256,256]{1,0:T(8,128)S(1)} %convolution_bitcast_fusion.6), channel_id=1, source_target_pairs={{0,32},{1,40},{2,48},{3,56},{4,0},{5,8},{6,16},{7,24},{8,33},{9,41... | collective-permute-start | bytes 786440 | tf_op jit(solution)/shard_map/ppermute | solution.py:28
  296.6 36.0 %collective-permute-start.21 = (f32[256,256]{1,0:T(8,128)S(1)}, f32[256,256]{1,0:T(8,128)S(1)}, u32[]{:S(2)}, u32[]{:S(2)}) collective-permute-start(f32[256,256]{1,0:T(8,128)S(1)} %convolution_bitcast_fusion.5), channel_id=1, source_target_pairs={{0,0},{1,8},{2,16},{3,24},{4,32},{5,40},{6,48},{7,56},{8,1},{9,9},... | collective-permute-start | bytes 786440 | tf_op jit(solution)/shard_map/ppermute | solution.py:28
  299.7 38.9 %collective-permute-start.22 = (f32[256,256]{1,0:T(8,128)S(1)}, f32[256,256]{1,0:T(8,128)S(1)}, u32[]{:S(2)}, u32[]{:S(2)}) collective-permute-start(f32[256,256]{1,0:T(8,128)S(1)} %convolution_bitcast_fusion.5), channel_id=1, source_target_pairs={{0,8},{1,0},{2,24},{3,16},{4,40},{5,32},{6,56},{7,48},{8,9},{9,1},... | collective-permute-start | bytes 786440 | tf_op jit(solution)/shard_map/ppermute | solution.py:28
  300.6 38.0 %collective-permute-start.23 = (f32[256,256]{1,0:T(8,128)S(1)}, f32[256,256]{1,0:T(8,128)S(1)}, u32[]{:S(2)}, u32[]{:S(2)}) collective-permute-start(f32[256,256]{1,0:T(8,128)S(1)} %convolution_bitcast_fusion.5), channel_id=1, source_target_pairs={{0,16},{1,24},{2,0},{3,8},{4,48},{5,56},{6,32},{7,40},{8,17},{9,25... | collective-permute-start | bytes 786440 | tf_op jit(solution)/shard_map/ppermute | solution.py:28
  374.9 84.0 %collective-permute-start.40 = (bf16[2,2,256,256]{3,2,1,0:T(8,128)(2,1)S(1)}, bf16[2,2,256,256]{3,2,1,0:T(8,128)(2,1)S(1)}, u32[]{:S(2)}, u32[]{:S(2)}) collective-permute-start(bf16[2,2,256,256]{3,2,1,0:T(8,128)(2,1)S(1)} %bitcast.322), channel_id=1, source_target_pairs={{0,0},{1,8},{2,16},{3,24},{4,32},{5,40},{6,48},{7,56},{8,1},{9,9},... | collective-permute-start | bytes 1572872 | tf_op jit(solution)/shard_map/ppermute | solution.py:21
  381.1 89.9 %collective-permute-start.3 = (f32[2,256,256]{2,1,0:T(8,128)S(1)}, f32[2,256,256]{2,1,0:T(8,128)S(1)}, u32[]{:S(2)}, u32[]{:S(2)}) collective-permute-start(f32[2,256,256]{2,1,0:T(8,128)S(1)} %bitcast.323), channel_id=1, source_target_pairs={{0,0},{1,8},{2,16},{3,24},{4,32},{5,40},{6,48},{7,56},{8,1},{9,9},... | collective-permute-start | bytes 1572872 | tf_op jit(solution)/shard_map/ppermute | solution.py:21
  394.4 81.4 %collective-permute-start.32 = (f32[256,256]{1,0:T(8,128)S(1)}, f32[256,256]{1,0:T(8,128)S(1)}, u32[]{:S(2)}, u32[]{:S(2)}) collective-permute-start(f32[256,256]{1,0:T(8,128)S(1)} %slice_bitcast_fusion.2), channel_id=1, source_target_pairs={{0,0},{1,8},{2,16},{3,24},{4,32},{5,40},{6,48},{7,56},{8,1},{9,9},... | collective-permute-start | bytes 786440 | tf_op jit(solution)/shard_map/ppermute | solution.py:28
  396.7 84.7 %collective-permute-start.33 = (f32[256,256]{1,0:T(8,128)S(1)}, f32[256,256]{1,0:T(8,128)S(1)}, u32[]{:S(2)}, u32[]{:S(2)}) collective-permute-start(f32[256,256]{1,0:T(8,128)S(1)} %slice_bitcast_fusion.2), channel_id=1, source_target_pairs={{0,8},{1,0},{2,24},{3,16},{4,40},{5,32},{6,56},{7,48},{8,9},{9,1},... | collective-permute-start | bytes 786440 | tf_op jit(solution)/shard_map/ppermute | solution.py:28
  397.6 83.8 %collective-permute-start.34 = (f32[256,256]{1,0:T(8,128)S(1)}, f32[256,256]{1,0:T(8,128)S(1)}, u32[]{:S(2)}, u32[]{:S(2)}) collective-permute-start(f32[256,256]{1,0:T(8,128)S(1)} %slice_bitcast_fusion.2), channel_id=1, source_target_pairs={{0,16},{1,24},{2,0},{3,8},{4,48},{5,56},{6,32},{7,40},{8,17},{9,25... | collective-permute-start | bytes 786440 | tf_op jit(solution)/shard_map/ppermute | solution.py:28
  475.8 32.8 %collective-permute-start.37 = (f32[256,256]{1,0:T(8,128)S(1)}, f32[256,256]{1,0:T(8,128)S(1)}, u32[]{:S(2)}, u32[]{:S(2)}) collective-permute-start(f32[256,256]{1,0:T(8,128)S(1)} %slice_bitcast_fusion.2), channel_id=1, source_target_pairs={{0,40},{1,32},{2,56},{3,48},{4,8},{5,0},{6,24},{7,16},{8,41},{9,33... | collective-permute-start | bytes 786440 | tf_op jit(solution)/shard_map/ppermute | solution.py:28
  481.4 35.3 %collective-permute-start.39 = (f32[256,256]{1,0:T(8,128)S(1)}, f32[256,256]{1,0:T(8,128)S(1)}, u32[]{:S(2)}, u32[]{:S(2)}) collective-permute-start(f32[256,256]{1,0:T(8,128)S(1)} %slice_bitcast_fusion.2), channel_id=1, source_target_pairs={{0,56},{1,48},{2,40},{3,32},{4,24},{5,16},{6,8},{7,0},{8,57},{9,49... | collective-permute-start | bytes 786440 | tf_op jit(solution)/shard_map/ppermute | solution.py:28
  517.3 38.9 %collective-permute-start.41 = (f32[256,256]{1,0:T(8,128)S(1)}, f32[256,256]{1,0:T(8,128)S(1)}, u32[]{:S(2)}, u32[]{:S(2)}) collective-permute-start(f32[256,256]{1,0:T(8,128)S(1)} %fusion.53), channel_id=1, source_target_pairs={{0,0},{1,8},{2,16},{3,24},{4,32},{5,40},{6,48},{7,56},{8,1},{9,9},... | collective-permute-start | bytes 786440 | tf_op jit(solution)/shard_map/ppermute | solution.py:28
  523.7 37.9 %collective-permute-start.42 = (f32[256,256]{1,0:T(8,128)S(1)}, f32[256,256]{1,0:T(8,128)S(1)}, u32[]{:S(2)}, u32[]{:S(2)}) collective-permute-start(f32[256,256]{1,0:T(8,128)S(1)} %fusion.53), channel_id=1, source_target_pairs={{0,8},{1,0},{2,24},{3,16},{4,40},{5,32},{6,56},{7,48},{8,9},{9,1},... | collective-permute-start | bytes 786440 | tf_op jit(solution)/shard_map/ppermute | solution.py:28
  523.8 47.0 %collective-permute-start.43 = (f32[256,256]{1,0:T(8,128)S(1)}, f32[256,256]{1,0:T(8,128)S(1)}, u32[]{:S(2)}, u32[]{:S(2)}) collective-permute-start(f32[256,256]{1,0:T(8,128)S(1)} %fusion.53), channel_id=1, source_target_pairs={{0,16},{1,24},{2,0},{3,8},{4,48},{5,56},{6,32},{7,40},{8,17},{9,25... | collective-permute-start | bytes 786440 | tf_op jit(solution)/shard_map/ppermute | solution.py:28
  534.1 41.6 %collective-permute-start.44 = (f32[256,256]{1,0:T(8,128)S(1)}, f32[256,256]{1,0:T(8,128)S(1)}, u32[]{:S(2)}, u32[]{:S(2)}) collective-permute-start(f32[256,256]{1,0:T(8,128)S(1)} %fusion.53), channel_id=1, source_target_pairs={{0,24},{1,16},{2,8},{3,0},{4,56},{5,48},{6,40},{7,32},{8,25},{9,17... | collective-permute-start | bytes 786440 | tf_op jit(solution)/shard_map/ppermute | solution.py:28
  534.1 41.6 %collective-permute-start.45 = (f32[256,256]{1,0:T(8,128)S(1)}, f32[256,256]{1,0:T(8,128)S(1)}, u32[]{:S(2)}, u32[]{:S(2)}) collective-permute-start(f32[256,256]{1,0:T(8,128)S(1)} %fusion.53), channel_id=1, source_target_pairs={{0,32},{1,40},{2,48},{3,56},{4,0},{5,8},{6,16},{7,24},{8,33},{9,41... | collective-permute-start | bytes 786440 | tf_op jit(solution)/shard_map/ppermute | solution.py:28
  600.4 34.0 %collective-permute-start.49 = (f32[256,256]{0,1:T(8,128)}, f32[256,256]{0,1:T(8,128)S(1)}, u32[]{:S(2)}, u32[]{:S(2)}) collective-permute-start(f32[256,256]{0,1:T(8,128)} %fusion.94), channel_id=1, source_target_pairs={{0,0},{1,8},{2,16},{3,24},{4,32},{5,40},{6,48},{7,56},{8,1},{9,9},... | collective-permute-start | bytes 786440 | tf_op jit(solution)/shard_map/ppermute | solution.py:28
  606.4 33.8 %collective-permute-start.50 = (f32[256,256]{0,1:T(8,128)}, f32[256,256]{0,1:T(8,128)S(1)}, u32[]{:S(2)}, u32[]{:S(2)}) collective-permute-start(f32[256,256]{0,1:T(8,128)} %fusion.94), channel_id=1, source_target_pairs={{0,8},{1,0},{2,24},{3,16},{4,40},{5,32},{6,56},{7,48},{8,9},{9,1},... | collective-permute-start | bytes 786440 | tf_op jit(solution)/shard_map/ppermute | solution.py:28
  606.7 37.2 %collective-permute-start.51 = (f32[256,256]{0,1:T(8,128)}, f32[256,256]{0,1:T(8,128)S(1)}, u32[]{:S(2)}, u32[]{:S(2)}) collective-permute-start(f32[256,256]{0,1:T(8,128)} %fusion.94), channel_id=1, source_target_pairs={{0,16},{1,24},{2,0},{3,8},{4,48},{5,56},{6,32},{7,40},{8,17},{9,25... | collective-permute-start | bytes 786440 | tf_op jit(solution)/shard_map/ppermute | solution.py:28
  618.9 34.6 %collective-permute-start.52 = (f32[256,256]{0,1:T(8,128)}, f32[256,256]{0,1:T(8,128)S(1)}, u32[]{:S(2)}, u32[]{:S(2)}) collective-permute-start(f32[256,256]{0,1:T(8,128)} %fusion.94), channel_id=1, source_target_pairs={{0,24},{1,16},{2,8},{3,0},{4,56},{5,48},{6,40},{7,32},{8,25},{9,17... | collective-permute-start | bytes 786440 | tf_op jit(solution)/shard_map/ppermute | solution.py:28
  618.9 34.6 %collective-permute-start.53 = (f32[256,256]{0,1:T(8,128)}, f32[256,256]{0,1:T(8,128)S(1)}, u32[]{:S(2)}, u32[]{:S(2)}) collective-permute-start(f32[256,256]{0,1:T(8,128)} %fusion.94), channel_id=1, source_target_pairs={{0,32},{1,40},{2,48},{3,56},{4,0},{5,8},{6,16},{7,24},{8,33},{9,41... | collective-permute-start | bytes 786440 | tf_op jit(solution)/shard_map/ppermute | solution.py:28
  679.2 37.2 %collective-permute-start.57 = (f32[256,256]{1,0:T(8,128)S(1)}, f32[256,256]{1,0:T(8,128)S(1)}, u32[]{:S(2)}, u32[]{:S(2)}) collective-permute-start(f32[256,256]{1,0:T(8,128)S(1)} %convolution_bitcast_fusion.2), channel_id=1, source_target_pairs={{0,0},{1,8},{2,16},{3,24},{4,32},{5,40},{6,48},{7,56},{8,1},{9,9},... | collective-permute-start | bytes 786440 | tf_op jit(solution)/shard_map/ppermute | solution.py:28
  687.7 34.1 %collective-permute-start.58 = (f32[256,256]{1,0:T(8,128)S(1)}, f32[256,256]{1,0:T(8,128)S(1)}, u32[]{:S(2)}, u32[]{:S(2)}) collective-permute-start(f32[256,256]{1,0:T(8,128)S(1)} %convolution_bitcast_fusion.2), channel_id=1, source_target_pairs={{0,8},{1,0},{2,24},{3,16},{4,40},{5,32},{6,56},{7,48},{8,9},{9,1},... | collective-permute-start | bytes 786440 | tf_op jit(solution)/shard_map/ppermute | solution.py:28
  687.8 45.4 %collective-permute-start.59 = (f32[256,256]{1,0:T(8,128)S(1)}, f32[256,256]{1,0:T(8,128)S(1)}, u32[]{:S(2)}, u32[]{:S(2)}) collective-permute-start(f32[256,256]{1,0:T(8,128)S(1)} %convolution_bitcast_fusion.2), channel_id=1, source_target_pairs={{0,16},{1,24},{2,0},{3,8},{4,48},{5,56},{6,32},{7,40},{8,17},{9,25... | collective-permute-start | bytes 786440 | tf_op jit(solution)/shard_map/ppermute | solution.py:28
  693.4 45.0 %collective-permute-start.60 = (f32[256,256]{1,0:T(8,128)S(1)}, f32[256,256]{1,0:T(8,128)S(1)}, u32[]{:S(2)}, u32[]{:S(2)}) collective-permute-start(f32[256,256]{1,0:T(8,128)S(1)} %convolution_bitcast_fusion.2), channel_id=1, source_target_pairs={{0,24},{1,16},{2,8},{3,0},{4,56},{5,48},{6,40},{7,32},{8,25},{9,17... | collective-permute-start | bytes 786440 | tf_op jit(solution)/shard_map/ppermute | solution.py:28
  693.4 45.0 %collective-permute-start.61 = (f32[256,256]{1,0:T(8,128)S(1)}, f32[256,256]{1,0:T(8,128)S(1)}, u32[]{:S(2)}, u32[]{:S(2)}) collective-permute-start(f32[256,256]{1,0:T(8,128)S(1)} %convolution_bitcast_fusion.2), channel_id=1, source_target_pairs={{0,32},{1,40},{2,48},{3,56},{4,0},{5,8},{6,16},{7,24},{8,33},{9,41... | collective-permute-start | bytes 786440 | tf_op jit(solution)/shard_map/ppermute | solution.py:28
  765.0 46.3 %collective-permute-start.67 = (f32[256,256]{1,0:T(8,128)S(1)}, f32[256,256]{1,0:T(8,128)S(1)}, u32[]{:S(2)}, u32[]{:S(2)}) collective-permute-start(f32[256,256]{1,0:T(8,128)S(1)} %convolution_bitcast_fusion.1), channel_id=1, source_target_pairs={{0,16},{1,24},{2,0},{3,8},{4,48},{5,56},{6,32},{7,40},{8,17},{9,25... | collective-permute-start | bytes 786440 | tf_op jit(solution)/shard_map/ppermute | solution.py:28
  773.0 43.1 %collective-permute-start.68 = (f32[256,256]{1,0:T(8,128)S(1)}, f32[256,256]{1,0:T(8,128)S(1)}, u32[]{:S(2)}, u32[]{:S(2)}) collective-permute-start(f32[256,256]{1,0:T(8,128)S(1)} %convolution_bitcast_fusion.1), channel_id=1, source_target_pairs={{0,24},{1,16},{2,8},{3,0},{4,56},{5,48},{6,40},{7,32},{8,25},{9,17... | collective-permute-start | bytes 786440 | tf_op jit(solution)/shard_map/ppermute | solution.py:28
  773.1 43.0 %collective-permute-start.69 = (f32[256,256]{1,0:T(8,128)S(1)}, f32[256,256]{1,0:T(8,128)S(1)}, u32[]{:S(2)}, u32[]{:S(2)}) collective-permute-start(f32[256,256]{1,0:T(8,128)S(1)} %convolution_bitcast_fusion.1), channel_id=1, source_target_pairs={{0,32},{1,40},{2,48},{3,56},{4,0},{5,8},{6,16},{7,24},{8,33},{9,41... | collective-permute-start | bytes 786440 | tf_op jit(solution)/shard_map/ppermute | solution.py:28
  841.9 32.8 %collective-permute-start.74 = (f32[256,256]{1,0:T(8,128)S(1)}, f32[256,256]{1,0:T(8,128)S(1)}, u32[]{:S(2)}, u32[]{:S(2)}) collective-permute-start(f32[256,256]{1,0:T(8,128)S(1)} %convolution_bitcast_fusion), channel_id=1, source_target_pairs={{0,8},{1,0},{2,24},{3,16},{4,40},{5,32},{6,56},{7,48},{8,9},{9,1},... | collective-permute-start | bytes 786440 | tf_op jit(solution)/shard_map/ppermute | solution.py:28
  842.0 47.5 %collective-permute-start.75 = (f32[256,256]{1,0:T(8,128)S(1)}, f32[256,256]{1,0:T(8,128)S(1)}, u32[]{:S(2)}, u32[]{:S(2)}) collective-permute-start(f32[256,256]{1,0:T(8,128)S(1)} %convolution_bitcast_fusion), channel_id=1, source_target_pairs={{0,16},{1,24},{2,0},{3,8},{4,48},{5,56},{6,32},{7,40},{8,17},{9,25... | collective-permute-start | bytes 786440 | tf_op jit(solution)/shard_map/ppermute | solution.py:28
  849.4 45.3 %collective-permute-start.76 = (f32[256,256]{1,0:T(8,128)S(1)}, f32[256,256]{1,0:T(8,128)S(1)}, u32[]{:S(2)}, u32[]{:S(2)}) collective-permute-start(f32[256,256]{1,0:T(8,128)S(1)} %convolution_bitcast_fusion), channel_id=1, source_target_pairs={{0,24},{1,16},{2,8},{3,0},{4,56},{5,48},{6,40},{7,32},{8,25},{9,17... | collective-permute-start | bytes 786440 | tf_op jit(solution)/shard_map/ppermute | solution.py:28
  849.5 45.2 %collective-permute-start.77 = (f32[256,256]{1,0:T(8,128)S(1)}, f32[256,256]{1,0:T(8,128)S(1)}, u32[]{:S(2)}, u32[]{:S(2)}) collective-permute-start(f32[256,256]{1,0:T(8,128)S(1)} %convolution_bitcast_fusion), channel_id=1, source_target_pairs={{0,32},{1,40},{2,48},{3,56},{4,0},{5,8},{6,16},{7,24},{8,33},{9,41... | collective-permute-start | bytes 786440 | tf_op jit(solution)/shard_map/ppermute | solution.py:28
  874.7 32.8 %collective-permute-start.79 = (f32[256,256]{1,0:T(8,128)S(1)}, f32[256,256]{1,0:T(8,128)S(1)}, u32[]{:S(2)}, u32[]{:S(2)}) collective-permute-start(f32[256,256]{1,0:T(8,128)S(1)} %convolution_bitcast_fusion), channel_id=1, source_target_pairs={{0,48},{1,56},{2,32},{3,40},{4,16},{5,24},{6,0},{7,8},{8,49},{9,57... | collective-permute-start | bytes 786440 | tf_op jit(solution)/shard_map/ppermute | solution.py:28
  919.4 32.9 %collective-permute-start.82 = (f32[256,256]{1,0:T(8,128)S(1)}, f32[256,256]{1,0:T(8,128)S(1)}, u32[]{:S(2)}, u32[]{:S(2)}) collective-permute-start(f32[256,256]{1,0:T(8,128)S(1)} %convolution_bitcast_fusion.7), channel_id=1, source_target_pairs={{0,8},{1,0},{2,24},{3,16},{4,40},{5,32},{6,56},{7,48},{8,9},{9,1},... | collective-permute-start | bytes 786440 | tf_op jit(solution)/shard_map/ppermute | solution.py:28
  919.5 46.8 %collective-permute-start.83 = (f32[256,256]{1,0:T(8,128)S(1)}, f32[256,256]{1,0:T(8,128)S(1)}, u32[]{:S(2)}, u32[]{:S(2)}) collective-permute-start(f32[256,256]{1,0:T(8,128)S(1)} %convolution_bitcast_fusion.7), channel_id=1, source_target_pairs={{0,16},{1,24},{2,0},{3,8},{4,48},{5,56},{6,32},{7,40},{8,17},{9,25... | collective-permute-start | bytes 786440 | tf_op jit(solution)/shard_map/ppermute | solution.py:28
  929.8 41.5 %collective-permute-start.84 = (f32[256,256]{1,0:T(8,128)S(1)}, f32[256,256]{1,0:T(8,128)S(1)}, u32[]{:S(2)}, u32[]{:S(2)}) collective-permute-start(f32[256,256]{1,0:T(8,128)S(1)} %convolution_bitcast_fusion.7), channel_id=1, source_target_pairs={{0,24},{1,16},{2,8},{3,0},{4,56},{5,48},{6,40},{7,32},{8,25},{9,17... | collective-permute-start | bytes 786440 | tf_op jit(solution)/shard_map/ppermute | solution.py:28
  929.8 43.5 %collective-permute-start.85 = (f32[256,256]{1,0:T(8,128)S(1)}, f32[256,256]{1,0:T(8,128)S(1)}, u32[]{:S(2)}, u32[]{:S(2)}) collective-permute-start(f32[256,256]{1,0:T(8,128)S(1)} %convolution_bitcast_fusion.7), channel_id=1, source_target_pairs={{0,32},{1,40},{2,48},{3,56},{4,0},{5,8},{6,16},{7,24},{8,33},{9,41... | collective-permute-start | bytes 786440 | tf_op jit(solution)/shard_map/ppermute | solution.py:28
  946.7 33.5 %collective-permute-start.86 = (f32[256,256]{1,0:T(8,128)S(1)}, f32[256,256]{1,0:T(8,128)S(1)}, u32[]{:S(2)}, u32[]{:S(2)}) collective-permute-start(f32[256,256]{1,0:T(8,128)S(1)} %convolution_bitcast_fusion.7), channel_id=1, source_target_pairs={{0,40},{1,32},{2,56},{3,48},{4,8},{5,0},{6,24},{7,16},{8,41},{9,33... | collective-permute-start | bytes 786440 | tf_op jit(solution)/shard_map/ppermute | solution.py:28
  952.3 33.6 %collective-permute-start.87 = (f32[256,256]{1,0:T(8,128)S(1)}, f32[256,256]{1,0:T(8,128)S(1)}, u32[]{:S(2)}, u32[]{:S(2)}) collective-permute-start(f32[256,256]{1,0:T(8,128)S(1)} %convolution_bitcast_fusion.7), channel_id=1, source_target_pairs={{0,48},{1,56},{2,32},{3,40},{4,16},{5,24},{6,0},{7,8},{8,49},{9,57... | collective-permute-start | bytes 786440 | tf_op jit(solution)/shard_map/ppermute | solution.py:28
  (85 other events, 3149.7 us)

commit v2 on v1

v2 whole, which is shorter than its diff:
```python
import jax
import jax.numpy as jnp
from jax import lax
from jax.sharding import PartitionSpec as P

GRID = ("row", "col")


def masked(blocks, marks):
    return blocks * marks.astype(jnp.bfloat16)[..., None, None]


def to_columns(x, n):
    pairs = [(r * n + c, c * n + r) for r in range(n) for c in range(n)]
    return lax.ppermute(x, GRID, pairs)


def butterfly(x, axis, n):
    k = 1
    while k < n:
        x = x + lax.ppermute(x, axis, [(i, i ^ k) for i in range(n)])
        k *= 2
    return x


def products(blocks, segments):
    return jnp.einsum(
        "jbk,jkr->br", jnp.stack(blocks, 0), jnp.stack(segments, 0), preferred_element_type=jnp.float32
    )


def shards(
    rhs,
    rhs_top,
    factor,
    factor_inv,
    lower_bridge,
    upper_bridge,
    top_factor,
    top_inv,
    widths,
    pattern,
    lower_links,
    upper_links,
    top_pattern,
):
    f32 = jnp.float32
    bf16 = jnp.bfloat16
    n = lax.axis_size("row")
    ncol = lax.axis_size("col")
    leaves = lax.axis_size("leaf")
    levels = factor.shape[1]
    tops = top_factor.shape[0]
    block = factor.shape[5]
    sides = rhs.shape[4]
    share = sides // ncol

    fm = masked(factor[0, :, 0, :, 0], pattern[0, :, 0, :, 0])
    lm = masked(lower_bridge[0, :, 0, :, 0], lower_links[0, :, 0, :, 0])
    um = masked(upper_bridge[0, :, 0, :, 0], upper_links[0, :, 0, :, 0])
    tm = masked(top_factor[:, 0, :, 0], top_pattern[:, 0, :, 0])
    marks = lax.broadcasted_iota(jnp.int32, (levels, block, 1), 1)
    keep = (marks < widths[0, :, 0][:, None, None]).astype(f32)
    own_rhs = rhs[0, :, 0]
    inv = factor_inv[0, :, :, 0]
    top_rhs = rhs_top[:, 0]
    tinv = top_inv[:, :, 0]

    ys = []
    segs = []
    for level in range(levels):
        if level == 0:
            resid = own_rhs[0].astype(bf16)
        else:
            part = products([fm[level, j] for j in range(level)], segs)
            resid = (own_rhs[level] - butterfly(part, "col", ncol)).astype(bf16)
        solved = keep[level] * jnp.dot(inv[0, level], resid, preferred_element_type=f32)
        ys.append(solved)
        segs.append(to_columns(solved.astype(bf16), n))

    coupling = jnp.stack([products([lm[t, j] for j in range(levels)], segs) for t in range(tops)], 0)
    coupling = butterfly(butterfly(coupling, "col", ncol), "leaf", leaves)

    yts = []
    tsegs = []
    for top in range(tops):
        summed = coupling[top]
        if top > 0:
            part = products([tm[top, j] for j in range(top)], tsegs)
            summed = summed + butterfly(part, "col", ncol)
        resid = (top_rhs[top] - summed).astype(bf16)
        solved = jnp.dot(tinv[0, top], resid, preferred_element_type=f32)
        yts.append(solved)
        tsegs.append(to_columns(solved.astype(bf16), n))

    zts = [None] * tops
    tback = [None] * tops
    for top in reversed(range(tops)):
        if top == tops - 1:
            resid = yts[top].astype(bf16)
        else:
            part = products([tm[top, j] for j in range(top + 1, tops)], tback[top + 1 :])
            resid = (yts[top] - butterfly(part, "col", ncol)).astype(bf16)
        solved = jnp.dot(tinv[1, top], resid, preferred_element_type=f32)
        zts[top] = solved
        tback[top] = to_columns(solved.astype(bf16), n)

    zs = [None] * levels
    back = [None] * levels
    for level in reversed(range(levels)):
        blocks = [um[level, t] for t in range(tops)] + [fm[level, j] for j in range(level + 1, levels)]
        part = products(blocks, tback + back[level + 1 :])
        resid = (ys[level] - butterfly(part, "col", ncol)).astype(bf16)
        solved = keep[level] * jnp.dot(inv[1, level], resid, preferred_element_type=f32)
        zs[level] = solved
        if level > 0:
            back[level] = to_columns(solved.astype(bf16), n)

    start = lax.axis_index("col") * share
    result = lax.dynamic_slice_in_dim(jnp.stack(zs, 0), start, share, 2)
    result_top = lax.dynamic_slice_in_dim(jnp.stack(zts, 0), start, share, 2)
    return (result[None, :, None], result_top[:, None])


def solution(mesh):
    assert mesh.shape["row"] == mesh.shape["col"]
    placed = (
        P("leaf", None, "row", None, None),
        P(None, "row", None, None),
        P("leaf", None, "row", None, "col", None, None),
        P("leaf", None, None, "row", None, None),
        P("leaf", None, "row", None, "col", None, None),
        P("leaf", None, "row", None, "col", None, None),
        P(None, "row", None, "col", None, None),
        P(None, None, "row", None, None),
        P("leaf", None, "row"),
        P("leaf", None, "row", None, "col"),
        P("leaf", None, "row", None, "col"),
        P("leaf", None, "row", None, "col"),
        P(None, "row", None, "col"),
    )
    return jax.shard_map(
        shards,
        mesh=mesh,
        in_specs=placed,
        out_specs=(P("leaf", None, "row", None, "col"), P(None, "row", None, "col")),
        check_vma=False,
    )
```

time: 1030 us -> 406 us (0.39)
  the two profiles are of different devices: /device:TPU:7 before, /device:TPU:192 now
where the time goes in v2:
time: 406 us; the launch traced here: 405 us
  waiting for transfers between devices  345 us (85%)
  starting transfers between devices  30.6 us (8%)
  matrix products  17.8 us (4%)
  other arithmetic  6.87 us (2%)
    ppermute x32, waiting for transfers between devices, butterfly(): x = x + lax.ppermute(x, axis, [(i, i ^ k) for i in range(n)])  218 us
    ppermute x10, waiting for transfers between devices, to_columns(): return lax.ppermute(x, GRID, pairs)  128 us
    ppermute x10, starting transfers between devices, to_columns(): return lax.ppermute(x, GRID, pairs)  22.7 us
  transfers between devices with their start and end apart: 42, of which 42 were waited for; matrix products, arithmetic and copies ran while one was open for 2% of the time, Pallas kernels for 0%

profile of v2, /device:TPU:192, one launch (start us, length us, event | category | flops | bytes accessed | tf_op | source)
XLA Modules:
  0.0 404.9 jit_solution(1372191007092117799)
XLA Ops:
  1.4 1.9 fusion.104
  3.3 1.9 collective-permute-start
  7.7 12.6 %collective-permute-done = bf16[256,256]{1,0:T(8,128)(2,1)S(1)} collective-permute-done((bf16[256,256]{1,0:T(8,128)(2,1)S(1)}, bf16[256,256]{1,0:T(8,128)(2,1)S(1)}, u32[]{:S(2)}, u32[]{:S(2)}) %collective-permute-start) | collective-permute-done | bytes 131104 | tf_op jit(solution)/shard_map/ppermute | solution.py:15
  22.3 8.3 %collective-permute-done.2 = f32[256,256]{1,0:T(8,128)S(1)} collective-permute-done((f32[256,256]{1,0:T(8,128)S(1)}, f32[256,256]{1,0:T(8,128)S(1)}, u32[]{:S(2)}, u32[]{:S(2)}) %collective-permute-start.2) | collective-permute-done | bytes 262176 | tf_op jit(solution)/shard_map/ppermute | solution.py:21
  30.8 9.0 %collective-permute-done.3 = f32[256,256]{1,0:T(8,128)S(1)} collective-permute-done((f32[256,256]{1,0:T(8,128)S(1)}, f32[256,256]{1,0:T(8,128)S(1)}, u32[]{:S(2)}, u32[]{:S(2)}) %collective-permute-start.3) | collective-permute-done | bytes 262176 | tf_op jit(solution)/shard_map/ppermute | solution.py:21
  41.6 2.2 collective-permute-start.4
  44.5 12.2 %collective-permute-done.4 = bf16[256,256]{1,0:T(8,128)(2,1)S(1)} collective-permute-done((bf16[256,256]{1,0:T(8,128)(2,1)S(1)}, bf16[256,256]{1,0:T(8,128)(2,1)S(1)}, u32[]{:S(2)}, u32[]{:S(2)}) %collective-permute-start.4) | collective-permute-done | bytes 131104 | tf_op jit(solution)/shard_map/ppermute | solution.py:15
  58.7 8.3 %collective-permute-done.6 = f32[256,256]{1,0:T(8,128)S(1)} collective-permute-done((f32[256,256]{1,0:T(8,128)S(1)}, f32[256,256]{1,0:T(8,128)S(1)}, u32[]{:S(2)}, u32[]{:S(2)}) %collective-permute-start.6) | collective-permute-done | bytes 262176 | tf_op jit(solution)/shard_map/ppermute | solution.py:21
  67.2 9.0 %collective-permute-done.7 = f32[256,256]{1,0:T(8,128)S(1)} collective-permute-done((f32[256,256]{1,0:T(8,128)S(1)}, f32[256,256]{1,0:T(8,128)S(1)}, u32[]{:S(2)}, u32[]{:S(2)}) %collective-permute-start.7) | collective-permute-done | bytes 262176 | tf_op jit(solution)/shard_map/ppermute | solution.py:21
  76.2 1.8 fusion.106
  78.0 2.7 collective-permute-start.8
  80.7 12.5 %collective-permute-done.8 = bf16[256,256]{1,0:T(8,128)(2,1)S(1)} collective-permute-done((bf16[256,256]{1,0:T(8,128)(2,1)S(1)}, bf16[256,256]{1,0:T(8,128)(2,1)S(1)}, u32[]{:S(2)}, u32[]{:S(2)}) %collective-permute-start.8) | collective-permute-done | bytes 131104 | tf_op jit(solution)/shard_map/ppermute | solution.py:15
  95.2 8.3 %collective-permute-done.10 = f32[256,256]{1,0:T(8,128)S(1)} collective-permute-done((f32[256,256]{1,0:T(8,128)S(1)}, f32[256,256]{1,0:T(8,128)S(1)}, u32[]{:S(2)}, u32[]{:S(2)}) %collective-permute-start.10) | collective-permute-done | bytes 262176 | tf_op jit(solution)/shard_map/ppermute | solution.py:21
  103.8 8.8 %collective-permute-done.11 = f32[256,256]{1,0:T(8,128)S(1)} collective-permute-done((f32[256,256]{1,0:T(8,128)S(1)}, f32[256,256]{1,0:T(8,128)S(1)}, u32[]{:S(2)}, u32[]{:S(2)}) %collective-permute-start.11) | collective-permute-done | bytes 262176 | tf_op jit(solution)/shard_map/ppermute | solution.py:21
  114.5 2.4 collective-permute-start.12
  116.9 12.5 %collective-permute-done.12 = bf16[256,256]{1,0:T(8,128)(2,1)S(1)} collective-permute-done((bf16[256,256]{1,0:T(8,128)(2,1)S(1)}, bf16[256,256]{1,0:T(8,128)(2,1)S(1)}, u32[]{:S(2)}, u32[]{:S(2)}) %collective-permute-start.12) | collective-permute-done | bytes 131104 | tf_op jit(solution)/shard_map/ppermute | solution.py:15
  130.2 1.9 collective-permute-done.13
  132.3 14.0 %collective-permute-done.14 = f32[2,256,256]{2,1,0:T(8,128)S(1)} collective-permute-done((f32[2,256,256]{2,1,0:T(8,128)S(1)}, f32[2,256,256]{2,1,0:T(8,128)S(1)}, u32[]{:S(2)}, u32[]{:S(2)}) %collective-permute-start.14) | collective-permute-done | bytes 524320 | tf_op jit(solution)/shard_map/ppermute | solution.py:21
  146.5 14.6 %collective-permute-done.15 = f32[2,256,256]{2,1,0:T(8,128)S(1)} collective-permute-done((f32[2,256,256]{2,1,0:T(8,128)S(1)}, f32[2,256,256]{2,1,0:T(8,128)S(1)}, u32[]{:S(2)}, u32[]{:S(2)}) %collective-permute-start.15) | collective-permute-done | bytes 524320 | tf_op jit(solution)/shard_map/ppermute | solution.py:21
  162.8 10.7 %collective-permute-done.16 = f32[2,256,256]{2,1,0:T(8,128)S(1)} collective-permute-done((f32[2,256,256]{2,1,0:T(8,128)S(1)}, f32[2,256,256]{2,1,0:T(8,128)S(1)}, u32[]{:S(2)}, u32[]{:S(2)}) %collective-permute-start.16) | collective-permute-done | bytes 524320 | tf_op jit(solution)/shard_map/ppermute | solution.py:21
  173.6 3.3 collective-permute-start.17
  176.9 10.3 %collective-permute-done.17 = f32[2,256,256]{2,1,0:T(8,128)S(1)} collective-permute-done((f32[2,256,256]{2,1,0:T(8,128)S(1)}, f32[2,256,256]{2,1,0:T(8,128)S(1)}, u32[]{:S(2)}, u32[]{:S(2)}) %collective-permute-start.17) | collective-permute-done | bytes 524320 | tf_op jit(solution)/shard_map/ppermute | solution.py:21
  187.3 1.8 fusion.108
  189.1 3.1 collective-permute-start.18
  192.3 11.3 %collective-permute-done.18 = bf16[256,256]{0,1:T(8,128)(2,1)S(1)} collective-permute-done((bf16[256,256]{0,1:T(8,128)(2,1)S(1)}, bf16[256,256]{0,1:T(8,128)(2,1)S(1)}, u32[]{:S(2)}, u32[]{:S(2)}) %collective-permute-start.18) | collective-permute-done | bytes 131104 | tf_op jit(solution)/shard_map/ppermute | solution.py:15
  205.8 8.3 %collective-permute-done.20 = f32[256,256]{1,0:T(8,128)S(1)} collective-permute-done((f32[256,256]{1,0:T(8,128)S(1)}, f32[256,256]{1,0:T(8,128)S(1)}, u32[]{:S(2)}, u32[]{:S(2)}) %collective-permute-start.20) | collective-permute-done | bytes 262176 | tf_op jit(solution)/shard_map/ppermute | solution.py:21
  214.2 9.1 %collective-permute-done.21 = f32[256,256]{1,0:T(8,128)} collective-permute-done((f32[256,256]{1,0:T(8,128)S(1)}, f32[256,256]{1,0:T(8,128)}, u32[]{:S(2)}, u32[]{:S(2)}) %collective-permute-start.21) | collective-permute-done | bytes 262176 | tf_op jit(solution)/shard_map/ppermute | solution.py:21
  223.3 2.3 bitcast_convert_fusion.4
  225.6 2.4 collective-permute-start.22
  228.0 13.3 %collective-permute-done.22 = bf16[256,256]{1,0:T(8,128)(2,1)S(1)} collective-permute-done((bf16[256,256]{1,0:T(8,128)(2,1)}, bf16[256,256]{1,0:T(8,128)(2,1)S(1)}, u32[]{:S(2)}, u32[]{:S(2)}) %collective-permute-start.22) | collective-permute-done | bytes 131104 | tf_op jit(solution)/shard_map/ppermute | solution.py:15
  244.1 7.5 %collective-permute-done.24 = f32[256,256]{0,1:T(8,128)S(1)} collective-permute-done((f32[256,256]{0,1:T(8,128)S(1)}, f32[256,256]{0,1:T(8,128)S(1)}, u32[]{:S(2)}, u32[]{:S(2)}) %collective-permute-start.24) | collective-permute-done | bytes 262176 | tf_op jit(solution)/shard_map/ppermute | solution.py:21
  253.1 7.6 %collective-permute-done.25 = f32[256,256]{0,1:T(8,128)S(1)} collective-permute-done((f32[256,256]{0,1:T(8,128)S(1)}, f32[256,256]{0,1:T(8,128)S(1)}, u32[]{:S(2)}, u32[]{:S(2)}) %collective-permute-start.25) | collective-permute-done | bytes 262176 | tf_op jit(solution)/shard_map/ppermute | solution.py:21
  262.0 2.1 collective-permute-start.26
  264.1 13.4 %collective-permute-done.26 = bf16[256,256]{1,0:T(8,128)(2,1)S(1)} collective-permute-done((bf16[256,256]{1,0:T(8,128)(2,1)S(1)}, bf16[256,256]{1,0:T(8,128)(2,1)S(1)}, u32[]{:S(2)}, u32[]{:S(2)}) %collective-permute-start.26) | collective-permute-done | bytes 131104 | tf_op jit(solution)/shard_map/ppermute | solution.py:15
  279.5 8.3 %collective-permute-done.28 = f32[256,256]{1,0:T(8,128)S(1)} collective-permute-done((f32[256,256]{1,0:T(8,128)S(1)}, f32[256,256]{1,0:T(8,128)S(1)}, u32[]{:S(2)}, u32[]{:S(2)}) %collective-permute-start.28) | collective-permute-done | bytes 262176 | tf_op jit(solution)/shard_map/ppermute | solution.py:21
  287.9 9.0 %collective-permute-done.29 = f32[256,256]{1,0:T(8,128)S(1)} collective-permute-done((f32[256,256]{1,0:T(8,128)S(1)}, f32[256,256]{1,0:T(8,128)S(1)}, u32[]{:S(2)}, u32[]{:S(2)}) %collective-permute-start.29) | collective-permute-done | bytes 262176 | tf_op jit(solution)/shard_map/ppermute | solution.py:21
  297.8 2.0 collective-permute-start.30
  299.9 13.4 %collective-permute-done.30 = bf16[256,256]{1,0:T(8,128)(2,1)S(1)} collective-permute-done((bf16[256,256]{1,0:T(8,128)(2,1)S(1)}, bf16[256,256]{1,0:T(8,128)(2,1)S(1)}, u32[]{:S(2)}, u32[]{:S(2)}) %collective-permute-start.30) | collective-permute-done | bytes 131104 | tf_op jit(solution)/shard_map/ppermute | solution.py:15
  315.3 8.3 %collective-permute-done.32 = f32[256,256]{1,0:T(8,128)S(1)} collective-permute-done((f32[256,256]{1,0:T(8,128)S(1)}, f32[256,256]{1,0:T(8,128)S(1)}, u32[]{:S(2)}, u32[]{:S(2)}) %collective-permute-start.32) | collective-permute-done | bytes 262176 | tf_op jit(solution)/shard_map/ppermute | solution.py:21
  323.8 9.0 %collective-permute-done.33 = f32[256,256]{1,0:T(8,128)S(1)} collective-permute-done((f32[256,256]{1,0:T(8,128)S(1)}, f32[256,256]{1,0:T(8,128)S(1)}, u32[]{:S(2)}, u32[]{:S(2)}) %collective-permute-start.33) | collective-permute-done | bytes 262176 | tf_op jit(solution)/shard_map/ppermute | solution.py:21
  333.7 1.9 collective-permute-start.34
  335.6 13.3 %collective-permute-done.34 = bf16[256,256]{1,0:T(8,128)(2,1)S(1)} collective-permute-done((bf16[256,256]{1,0:T(8,128)(2,1)S(1)}, bf16[256,256]{1,0:T(8,128)(2,1)S(1)}, u32[]{:S(2)}, u32[]{:S(2)}) %collective-permute-start.34) | collective-permute-done | bytes 131104 | tf_op jit(solution)/shard_map/ppermute | solution.py:15
  351.0 8.3 %collective-permute-done.36 = f32[256,256]{1,0:T(8,128)S(1)} collective-permute-done((f32[256,256]{1,0:T(8,128)S(1)}, f32[256,256]{1,0:T(8,128)S(1)}, u32[]{:S(2)}, u32[]{:S(2)}) %collective-permute-start.36) | collective-permute-done | bytes 262176 | tf_op jit(solution)/shard_map/ppermute | solution.py:21
  359.5 8.9 %collective-permute-done.37 = f32[256,256]{1,0:T(8,128)S(1)} collective-permute-done((f32[256,256]{1,0:T(8,128)S(1)}, f32[256,256]{1,0:T(8,128)S(1)}, u32[]{:S(2)}, u32[]{:S(2)}) %collective-permute-start.37) | collective-permute-done | bytes 262176 | tf_op jit(solution)/shard_map/ppermute | solution.py:21
  368.7 2.1 collective-permute-start.38
  370.7 13.2 %collective-permute-done.38 = bf16[256,256]{1,0:T(8,128)(2,1)S(1)} collective-permute-done((bf16[256,256]{1,0:T(8,128)(2,1)S(1)}, bf16[256,256]{1,0:T(8,128)(2,1)S(1)}, u32[]{:S(2)}, u32[]{:S(2)}) %collective-permute-start.38) | collective-permute-done | bytes 131104 | tf_op jit(solution)/shard_map/ppermute | solution.py:15
  386.2 8.3 %collective-permute-done.40 = f32[256,256]{1,0:T(8,128)S(1)} collective-permute-done((f32[256,256]{1,0:T(8,128)S(1)}, f32[256,256]{1,0:T(8,128)S(1)}, u32[]{:S(2)}, u32[]{:S(2)}) %collective-permute-start.40) | collective-permute-done | bytes 262176 | tf_op jit(solution)/shard_map/ppermute | solution.py:21
  395.5 8.1 %collective-permute-done.41 = f32[256,256]{1,0:T(8,128)S(1)} collective-permute-done((f32[256,256]{1,0:T(8,128)S(1)}, f32[256,256]{1,0:T(8,128)S(1)}, u32[]{:S(2)}, u32[]{:S(2)}) %collective-permute-start.41) | collective-permute-done | bytes 262176 | tf_op jit(solution)/shard_map/ppermute | solution.py:21
  (147 shorter events, 37.9 us)
Async XLA Ops:
  3.3 17.1 %collective-permute-start = (bf16[256,256]{1,0:T(8,128)(2,1)S(1)}, bf16[256,256]{1,0:T(8,128)(2,1)S(1)}, u32[]{:S(2)}, u32[]{:S(2)}) collective-permute-start(bf16[256,256]{1,0:T(8,128)(2,1)S(1)} %get-tuple-element.28), channel_id=1, source_target_pairs={{0,0},{1,8},{2,16},{3,24},{4,32},{5,40},{6,48},{7,56},{8,1},{9,9},... | collective-permute-start | bytes 393224 | tf_op jit(solution)/shard_map/ppermute | solution.py:15
  20.5 1.6 collective-permute-start.1
  22.2 8.4 %collective-permute-start.2 = (f32[256,256]{1,0:T(8,128)S(1)}, f32[256,256]{1,0:T(8,128)S(1)}, u32[]{:S(2)}, u32[]{:S(2)}) collective-permute-start(f32[256,256]{1,0:T(8,128)S(1)} %add.103), channel_id=1, source_target_pairs={{0,2},{1,3},{2,0},{3,1},{4,6},{5,7},{6,4},{7,5},{8,10},{9,11},{10,... | collective-permute-start | bytes 786440 | tf_op jit(solution)/shard_map/ppermute | solution.py:21
  30.7 9.1 %collective-permute-start.3 = (f32[256,256]{1,0:T(8,128)S(1)}, f32[256,256]{1,0:T(8,128)S(1)}, u32[]{:S(2)}, u32[]{:S(2)}) collective-permute-start(f32[256,256]{1,0:T(8,128)S(1)} %add.104), channel_id=1, source_target_pairs={{0,4},{1,5},{2,6},{3,7},{4,0},{5,1},{6,2},{7,3},{8,12},{9,13},{10,... | collective-permute-start | bytes 786440 | tf_op jit(solution)/shard_map/ppermute | solution.py:21
  41.6 15.1 %collective-permute-start.4 = (bf16[256,256]{1,0:T(8,128)(2,1)S(1)}, bf16[256,256]{1,0:T(8,128)(2,1)S(1)}, u32[]{:S(2)}, u32[]{:S(2)}) collective-permute-start(bf16[256,256]{1,0:T(8,128)(2,1)S(1)} %get-tuple-element.30), channel_id=1, source_target_pairs={{0,0},{1,8},{2,16},{3,24},{4,32},{5,40},{6,48},{7,56},{8,1},{9,9},... | collective-permute-start | bytes 393224 | tf_op jit(solution)/shard_map/ppermute | solution.py:15
  56.9 1.6 collective-permute-start.5
  58.6 8.4 %collective-permute-start.6 = (f32[256,256]{1,0:T(8,128)S(1)}, f32[256,256]{1,0:T(8,128)S(1)}, u32[]{:S(2)}, u32[]{:S(2)}) collective-permute-start(f32[256,256]{1,0:T(8,128)S(1)} %add.106), channel_id=1, source_target_pairs={{0,2},{1,3},{2,0},{3,1},{4,6},{5,7},{6,4},{7,5},{8,10},{9,11},{10,... | collective-permute-start | bytes 786440 | tf_op jit(solution)/shard_map/ppermute | solution.py:21
  67.1 9.1 %collective-permute-start.7 = (f32[256,256]{1,0:T(8,128)S(1)}, f32[256,256]{1,0:T(8,128)S(1)}, u32[]{:S(2)}, u32[]{:S(2)}) collective-permute-start(f32[256,256]{1,0:T(8,128)S(1)} %add.107), channel_id=1, source_target_pairs={{0,4},{1,5},{2,6},{3,7},{4,0},{5,1},{6,2},{7,3},{8,12},{9,13},{10,... | collective-permute-start | bytes 786440 | tf_op jit(solution)/shard_map/ppermute | solution.py:21
  78.0 15.2 %collective-permute-start.8 = (bf16[256,256]{1,0:T(8,128)(2,1)S(1)}, bf16[256,256]{1,0:T(8,128)(2,1)S(1)}, u32[]{:S(2)}, u32[]{:S(2)}) collective-permute-start(bf16[256,256]{1,0:T(8,128)(2,1)S(1)} %get-tuple-element.32), channel_id=1, source_target_pairs={{0,0},{1,8},{2,16},{3,24},{4,32},{5,40},{6,48},{7,56},{8,1},{9,9},... | collective-permute-start | bytes 393224 | tf_op jit(solution)/shard_map/ppermute | solution.py:15
  93.4 1.6 collective-permute-start.9
  95.1 8.4 %collective-permute-start.10 = (f32[256,256]{1,0:T(8,128)S(1)}, f32[256,256]{1,0:T(8,128)S(1)}, u32[]{:S(2)}, u32[]{:S(2)}) collective-permute-start(f32[256,256]{1,0:T(8,128)S(1)} %add.109), channel_id=1, source_target_pairs={{0,2},{1,3},{2,0},{3,1},{4,6},{5,7},{6,4},{7,5},{8,10},{9,11},{10,... | collective-permute-start | bytes 786440 | tf_op jit(solution)/shard_map/ppermute | solution.py:21
  103.6 9.1 %collective-permute-start.11 = (f32[256,256]{1,0:T(8,128)S(1)}, f32[256,256]{1,0:T(8,128)S(1)}, u32[]{:S(2)}, u32[]{:S(2)}) collective-permute-start(f32[256,256]{1,0:T(8,128)S(1)} %add.110), channel_id=1, source_target_pairs={{0,4},{1,5},{2,6},{3,7},{4,0},{5,1},{6,2},{7,3},{8,12},{9,13},{10,... | collective-permute-start | bytes 786440 | tf_op jit(solution)/shard_map/ppermute | solution.py:21
  114.5 15.0 %collective-permute-start.12 = (bf16[256,256]{1,0:T(8,128)(2,1)S(1)}, bf16[256,256]{1,0:T(8,128)(2,1)S(1)}, u32[]{:S(2)}, u32[]{:S(2)}) collective-permute-start(bf16[256,256]{1,0:T(8,128)(2,1)S(1)} %get-tuple-element.34), channel_id=1, source_target_pairs={{0,0},{1,8},{2,16},{3,24},{4,32},{5,40},{6,48},{7,56},{8,1},{9,9},... | collective-permute-start | bytes 393224 | tf_op jit(solution)/shard_map/ppermute | solution.py:15
  130.1 2.0 collective-permute-start.13
  132.2 14.1 %collective-permute-start.14 = (f32[2,256,256]{2,1,0:T(8,128)S(1)}, f32[2,256,256]{2,1,0:T(8,128)S(1)}, u32[]{:S(2)}, u32[]{:S(2)}) collective-permute-start(f32[2,256,256]{2,1,0:T(8,128)S(1)} %fusion.102), channel_id=1, source_target_pairs={{0,2},{1,3},{2,0},{3,1},{4,6},{5,7},{6,4},{7,5},{8,10},{9,11},{10,... | collective-permute-start | bytes 1572872 | tf_op jit(solution)/shard_map/ppermute | solution.py:21
  146.4 40.9 %copy-start.11 = (f32[2,1,256,256]{3,2,1,0:T(8,128)S(1)}, f32[2,1,256,256]{3,2,1,0:T(8,128)}, u32[]{:S(2)}) copy-start(f32[2,1,256,256]{3,2,1,0:T(8,128)} %param.14) | copy-start | bytes 1572868
  146.4 14.7 %collective-permute-start.15 = (f32[2,256,256]{2,1,0:T(8,128)S(1)}, f32[2,256,256]{2,1,0:T(8,128)S(1)}, u32[]{:S(2)}, u32[]{:S(2)}) collective-permute-start(f32[2,256,256]{2,1,0:T(8,128)S(1)} %fusion.116), channel_id=1, source_target_pairs={{0,4},{1,5},{2,6},{3,7},{4,0},{5,1},{6,2},{7,3},{8,12},{9,13},{10,... | collective-permute-start | bytes 1572872 | tf_op jit(solution)/shard_map/ppermute | solution.py:21
  161.2 12.3 %collective-permute-start.16 = (f32[2,256,256]{2,1,0:T(8,128)S(1)}, f32[2,256,256]{2,1,0:T(8,128)S(1)}, u32[]{:S(2)}, u32[]{:S(2)}) collective-permute-start(f32[2,256,256]{2,1,0:T(8,128)S(1)} %add.114), channel_id=1, source_target_pairs={{0,64},{64,0},{128,192},{192,128},{1,65},{65,1},{129,193},{193,129... | collective-permute-start | bytes 1572872 | tf_op jit(solution)/shard_map/ppermute | solution.py:21
  173.6 13.6 %collective-permute-start.17 = (f32[2,256,256]{2,1,0:T(8,128)S(1)}, f32[2,256,256]{2,1,0:T(8,128)S(1)}, u32[]{:S(2)}, u32[]{:S(2)}) collective-permute-start(f32[2,256,256]{2,1,0:T(8,128)S(1)} %add.115), channel_id=1, source_target_pairs={{0,128},{64,192},{128,0},{192,64},{1,129},{65,193},{129,1},{193,65... | collective-permute-start | bytes 1572872 | tf_op jit(solution)/shard_map/ppermute | solution.py:21
  189.1 14.5 %collective-permute-start.18 = (bf16[256,256]{0,1:T(8,128)(2,1)S(1)}, bf16[256,256]{0,1:T(8,128)(2,1)S(1)}, u32[]{:S(2)}, u32[]{:S(2)}) collective-permute-start(bf16[256,256]{0,1:T(8,128)(2,1)S(1)} %get-tuple-element.36), channel_id=1, source_target_pairs={{0,0},{1,8},{2,16},{3,24},{4,32},{5,40},{6,48},{7,56},{8,1},{9,9},... | collective-permute-start | bytes 393224 | tf_op jit(solution)/shard_map/ppermute | solution.py:15
  203.8 1.6 collective-permute-start.19
  205.5 8.6 %collective-permute-start.20 = (f32[256,256]{1,0:T(8,128)S(1)}, f32[256,256]{1,0:T(8,128)S(1)}, u32[]{:S(2)}, u32[]{:S(2)}) collective-permute-start(f32[256,256]{1,0:T(8,128)S(1)} %add.117), channel_id=1, source_target_pairs={{0,2},{1,3},{2,0},{3,1},{4,6},{5,7},{6,4},{7,5},{8,10},{9,11},{10,... | collective-permute-start | bytes 786440 | tf_op jit(solution)/shard_map/ppermute | solution.py:21
  214.1 9.2 %collective-permute-start.21 = (f32[256,256]{1,0:T(8,128)S(1)}, f32[256,256]{1,0:T(8,128)}, u32[]{:S(2)}, u32[]{:S(2)}) collective-permute-start(f32[256,256]{1,0:T(8,128)S(1)} %add.118), channel_id=1, source_target_pairs={{0,4},{1,5},{2,6},{3,7},{4,0},{5,1},{6,2},{7,3},{8,12},{9,13},{10,... | collective-permute-start | bytes 786440 | tf_op jit(solution)/shard_map/ppermute | solution.py:21
  225.6 15.7 %collective-permute-start.22 = (bf16[256,256]{1,0:T(8,128)(2,1)}, bf16[256,256]{1,0:T(8,128)(2,1)S(1)}, u32[]{:S(2)}, u32[]{:S(2)}) collective-permute-start(bf16[256,256]{1,0:T(8,128)(2,1)} %get-tuple-element.38), channel_id=1, source_target_pairs={{0,0},{1,8},{2,16},{3,24},{4,32},{5,40},{6,48},{7,56},{8,1},{9,9},... | collective-permute-start | bytes 393224 | tf_op jit(solution)/shard_map/ppermute | solution.py:15
  241.5 1.6 collective-permute-start.23
  243.2 8.4 %collective-permute-start.24 = (f32[256,256]{0,1:T(8,128)S(1)}, f32[256,256]{0,1:T(8,128)S(1)}, u32[]{:S(2)}, u32[]{:S(2)}) collective-permute-start(f32[256,256]{0,1:T(8,128)S(1)} %add.121), channel_id=1, source_target_pairs={{0,2},{1,3},{2,0},{3,1},{4,6},{5,7},{6,4},{7,5},{8,10},{9,11},{10,... | collective-permute-start | bytes 786440 | tf_op jit(solution)/shard_map/ppermute | solution.py:21
  251.6 9.1 %collective-permute-start.25 = (f32[256,256]{0,1:T(8,128)S(1)}, f32[256,256]{0,1:T(8,128)S(1)}, u32[]{:S(2)}, u32[]{:S(2)}) collective-permute-start(f32[256,256]{0,1:T(8,128)S(1)} %add.122), channel_id=1, source_target_pairs={{0,4},{1,5},{2,6},{3,7},{4,0},{5,1},{6,2},{7,3},{8,12},{9,13},{10,... | collective-permute-start | bytes 786440 | tf_op jit(solution)/shard_map/ppermute | solution.py:21
  261.9 35.0 %copy-start.1 = (bf16[1,2,4,1,256,256]{5,4,3,2,1,0:T(8,128)(2,1)S(1)}, bf16[1,2,4,1,256,256]{5,4,3,2,1,0:T(8,128)(2,1)}, u32[]{:S(2)}) copy-start(bf16[1,2,4,1,256,256]{5,4,3,2,1,0:T(8,128)(2,1)} %param.16) | copy-start | bytes 3145732
  262.0 35.0 %copy-start.7 = (f32[256,256]{1,0:T(8,128)S(1)}, f32[256,256]{1,0:T(8,128)}, u32[]{:S(2)}) copy-start(f32[256,256]{1,0:T(8,128)} %get-tuple-element.35) | copy-start | bytes 786436
  262.0 15.5 %collective-permute-start.26 = (bf16[256,256]{1,0:T(8,128)(2,1)S(1)}, bf16[256,256]{1,0:T(8,128)(2,1)S(1)}, u32[]{:S(2)}, u32[]{:S(2)}) collective-permute-start(bf16[256,256]{1,0:T(8,128)(2,1)S(1)} %get-tuple-element.40), channel_id=1, source_target_pairs={{0,0},{1,8},{2,16},{3,24},{4,32},{5,40},{6,48},{7,56},{8,1},{9,9},... | collective-permute-start | bytes 393224 | tf_op jit(solution)/shard_map/ppermute | solution.py:15
  264.1 49.2 %copy-start.14 = (bf16[1,256,256]{2,1,0:T(8,128)(2,1)S(1)}, bf16[1,256,256]{2,1,0:T(8,128)(2,1)}, u32[]{:S(2)}) copy-start(bf16[1,256,256]{2,1,0:T(8,128)(2,1)} %get-tuple-element.2) | copy-start | bytes 393220
  277.7 1.6 collective-permute-start.27
  279.4 8.4 %collective-permute-start.28 = (f32[256,256]{1,0:T(8,128)S(1)}, f32[256,256]{1,0:T(8,128)S(1)}, u32[]{:S(2)}, u32[]{:S(2)}) collective-permute-start(f32[256,256]{1,0:T(8,128)S(1)} %add.124), channel_id=1, source_target_pairs={{0,2},{1,3},{2,0},{3,1},{4,6},{5,7},{6,4},{7,5},{8,10},{9,11},{10,... | collective-permute-start | bytes 786440 | tf_op jit(solution)/shard_map/ppermute | solution.py:21
  287.8 9.1 %collective-permute-start.29 = (f32[256,256]{1,0:T(8,128)S(1)}, f32[256,256]{1,0:T(8,128)S(1)}, u32[]{:S(2)}, u32[]{:S(2)}) collective-permute-start(f32[256,256]{1,0:T(8,128)S(1)} %add.125), channel_id=1, source_target_pairs={{0,4},{1,5},{2,6},{3,7},{4,0},{5,1},{6,2},{7,3},{8,12},{9,13},{10,... | collective-permute-start | bytes 786440 | tf_op jit(solution)/shard_map/ppermute | solution.py:21
  297.8 15.4 %collective-permute-start.30 = (bf16[256,256]{1,0:T(8,128)(2,1)S(1)}, bf16[256,256]{1,0:T(8,128)(2,1)S(1)}, u32[]{:S(2)}, u32[]{:S(2)}) collective-permute-start(bf16[256,256]{1,0:T(8,128)(2,1)S(1)} %get-tuple-element.42), channel_id=1, source_target_pairs={{0,0},{1,8},{2,16},{3,24},{4,32},{5,40},{6,48},{7,56},{8,1},{9,9},... | collective-permute-start | bytes 393224 | tf_op jit(solution)/shard_map/ppermute | solution.py:15
  313.3 35.6 %copy-start.12 = (bf16[1,256,256]{2,1,0:T(8,128)(2,1)S(1)}, bf16[1,256,256]{2,1,0:T(8,128)(2,1)}, u32[]{:S(2)}) copy-start(bf16[1,256,256]{2,1,0:T(8,128)(2,1)} %get-tuple-element.3) | copy-start | bytes 393220
  313.3 35.6 %copy-start.13 = (bf16[1,256,256]{2,1,0:T(8,128)(2,1)S(1)}, bf16[1,256,256]{2,1,0:T(8,128)(2,1)}, u32[]{:S(2)}) copy-start(bf16[1,256,256]{2,1,0:T(8,128)(2,1)} %get-tuple-element.4) | copy-start | bytes 393220
  313.6 1.6 collective-permute-start.31
  315.2 8.4 %collective-permute-start.32 = (f32[256,256]{1,0:T(8,128)S(1)}, f32[256,256]{1,0:T(8,128)S(1)}, u32[]{:S(2)}, u32[]{:S(2)}) collective-permute-start(f32[256,256]{1,0:T(8,128)S(1)} %add.127), channel_id=1, source_target_pairs={{0,2},{1,3},{2,0},{3,1},{4,6},{5,7},{6,4},{7,5},{8,10},{9,11},{10,... | collective-permute-start | bytes 786440 | tf_op jit(solution)/shard_map/ppermute | solution.py:21
  323.7 9.1 %collective-permute-start.33 = (f32[256,256]{1,0:T(8,128)S(1)}, f32[256,256]{1,0:T(8,128)S(1)}, u32[]{:S(2)}, u32[]{:S(2)}) collective-permute-start(f32[256,256]{1,0:T(8,128)S(1)} %add.128), channel_id=1, source_target_pairs={{0,4},{1,5},{2,6},{3,7},{4,0},{5,1},{6,2},{7,3},{8,12},{9,13},{10,... | collective-permute-start | bytes 786440 | tf_op jit(solution)/shard_map/ppermute | solution.py:21
  333.7 15.2 %collective-permute-start.34 = (bf16[256,256]{1,0:T(8,128)(2,1)S(1)}, bf16[256,256]{1,0:T(8,128)(2,1)S(1)}, u32[]{:S(2)}, u32[]{:S(2)}) collective-permute-start(bf16[256,256]{1,0:T(8,128)(2,1)S(1)} %get-tuple-element.44), channel_id=1, source_target_pairs={{0,0},{1,8},{2,16},{3,24},{4,32},{5,40},{6,48},{7,56},{8,1},{9,9},... | collective-permute-start | bytes 393224 | tf_op jit(solution)/shard_map/ppermute | solution.py:15
  349.2 1.6 collective-permute-start.35
  350.9 8.4 %collective-permute-start.36 = (f32[256,256]{1,0:T(8,128)S(1)}, f32[256,256]{1,0:T(8,128)S(1)}, u32[]{:S(2)}, u32[]{:S(2)}) collective-permute-start(f32[256,256]{1,0:T(8,128)S(1)} %add.130), channel_id=1, source_target_pairs={{0,2},{1,3},{2,0},{3,1},{4,6},{5,7},{6,4},{7,5},{8,10},{9,11},{10,... | collective-permute-start | bytes 786440 | tf_op jit(solution)/shard_map/ppermute | solution.py:21
  359.4 9.1 %collective-permute-start.37 = (f32[256,256]{1,0:T(8,128)S(1)}, f32[256,256]{1,0:T(8,128)S(1)}, u32[]{:S(2)}, u32[]{:S(2)}) collective-permute-start(f32[256,256]{1,0:T(8,128)S(1)} %add.131), channel_id=1, source_target_pairs={{0,4},{1,5},{2,6},{3,7},{4,0},{5,1},{6,2},{7,3},{8,12},{9,13},{10,... | collective-permute-start | bytes 786440 | tf_op jit(solution)/shard_map/ppermute | solution.py:21
  368.7 15.3 %collective-permute-start.38 = (bf16[256,256]{1,0:T(8,128)(2,1)S(1)}, bf16[256,256]{1,0:T(8,128)(2,1)S(1)}, u32[]{:S(2)}, u32[]{:S(2)}) collective-permute-start(bf16[256,256]{1,0:T(8,128)(2,1)S(1)} %get-tuple-element.46), channel_id=1, source_target_pairs={{0,0},{1,8},{2,16},{3,24},{4,32},{5,40},{6,48},{7,56},{8,1},{9,9},... | collective-permute-start | bytes 393224 | tf_op jit(solution)/shard_map/ppermute | solution.py:15
  384.4 1.6 collective-permute-start.39
  386.1 8.4 %collective-permute-start.40 = (f32[256,256]{1,0:T(8,128)S(1)}, f32[256,256]{1,0:T(8,128)S(1)}, u32[]{:S(2)}, u32[]{:S(2)}) collective-permute-start(f32[256,256]{1,0:T(8,128)S(1)} %add.133), channel_id=1, source_target_pairs={{0,2},{1,3},{2,0},{3,1},{4,6},{5,7},{6,4},{7,5},{8,10},{9,11},{10,... | collective-permute-start | bytes 786440 | tf_op jit(solution)/shard_map/ppermute | solution.py:21
  394.5 9.1 %collective-permute-start.41 = (f32[256,256]{1,0:T(8,128)S(1)}, f32[256,256]{1,0:T(8,128)S(1)}, u32[]{:S(2)}, u32[]{:S(2)}) collective-permute-start(f32[256,256]{1,0:T(8,128)S(1)} %add.134), channel_id=1, source_target_pairs={{0,4},{1,5},{2,6},{3,7},{4,0},{5,1},{6,2},{7,3},{8,12},{9,13},{10,... | collective-permute-start | bytes 786440 | tf_op jit(solution)/shard_map/ppermute | solution.py:21
  (11 other events, 277.0 us)

commit v3 on v2

--- a/solution.py
+++ b/solution.py
@@ -10,17 +10,34 @@
     return blocks * marks.astype(jnp.bfloat16)[..., None, None]
 
 
+def ring_distance(a, b, size):
+    d = abs(a - b) % size
+    return min(d, size - d)
+
+
 def to_columns(x, n):
-    pairs = [(r * n + c, c * n + r) for r in range(n) for c in range(n)]
+    pairs = []
+    for c in range(n):
+        targets = sorted(range(n), key=lambda r: (-ring_distance(r, c, n), r))
+        sources = sorted(range(n), key=lambda s: (ring_distance(s // 2, c // 2, n // 2), s % 2 != c % 2, s))
+        pairs += [(c * n + s, r * n + c) for r, s in zip(targets, sources)]
     return lax.ppermute(x, GRID, pairs)
 
 
-def butterfly(x, axis, n):
-    k = 1
-    while k < n:
-        x = x + lax.ppermute(x, axis, [(i, i ^ k) for i in range(n)])
-        k *= 2
-    return x
+def tree_sum(parts):
+    while len(parts) > 1:
+        parts = [parts[i] + parts[i + 1] for i in range(0, len(parts), 2)]
+    return parts[0]
+
+
+def group_sum(x, axis, n, step=1):
+    got = [x] + [lax.ppermute(x, axis, [(i, i ^ (step * k)) for i in range(n)]) for k in range(1, n // step)]
+    return tree_sum(got)
+
+
+def column_total(x, n):
+    x = x + lax.ppermute(x, "col", [(i, i ^ 1) for i in range(n)])
+    return group_sum(x, "col", n, 2)
 
 
 def products(blocks, segments):
@@ -73,13 +90,13 @@
             resid = own_rhs[0].astype(bf16)
         else:
             part = products([fm[level, j] for j in range(level)], segs)
-            resid = (own_rhs[level] - butterfly(part, "col", ncol)).astype(bf16)
+            resid = (own_rhs[level] - column_total(part, ncol)).astype(bf16)
         solved = keep[level] * jnp.dot(inv[0, level], resid, preferred_element_type=f32)
         ys.append(solved)
         segs.append(to_columns(solved.astype(bf16), n))
 
     coupling = jnp.stack([products([lm[t, j] for j in range(levels)], segs) for t in range(tops)], 0)
-    coupling = butterfly(butterfly(coupling, "col", ncol), "leaf", leaves)
+    coupling = group_sum(column_total(coupling, ncol), "leaf", leaves)
 
     yts = []
     tsegs = []
@@ -87,7 +104,7 @@
         summed = coupling[top]
         if top > 0:
             part = products([tm[top, j] for j in range(top)], tsegs)
-            summed = summed + butterfly(part, "col", ncol)
+            summed = summed + column_total(part, ncol)
         resid = (top_rhs[top] - summed).astype(bf16)
         solved = jnp.dot(tinv[0, top], resid, preferred_element_type=f32)
         yts.append(solved)
@@ -100,7 +117,7 @@
             resid = yts[top].astype(bf16)
         else:
             part = products([tm[top, j] for j in range(top + 1, tops)], tback[top + 1 :])
-            resid = (yts[top] - butterfly(part, "col", ncol)).astype(bf16)
+            resid = (yts[top] - column_total(part, ncol)).astype(bf16)
         solved = jnp.dot(tinv[1, top], resid, preferred_element_type=f32)
         zts[top] = solved
         tback[top] = to_columns(solved.astype(bf16), n)
@@ -110,7 +127,7 @@
     for level in reversed(range(levels)):
         blocks = [um[level, t] for t in range(tops)] + [fm[level, j] for j in range(level + 1, levels)]
         part = products(blocks, tback + back[level + 1 :])
-        resid = (ys[level] - butterfly(part, "col", ncol)).astype(bf16)
+        resid = (ys[level] - column_total(part, ncol)).astype(bf16)
         solved = keep[level] * jnp.dot(inv[1, level], resid, preferred_element_type=f32)
         zs[level] = solved
         if level > 0:

time: 406 us -> 366 us (0.901)
  the two profiles are of different devices: /device:TPU:192 before, /device:TPU:96 now
where the time goes in v3:
time: 366 us; the launch traced here: 362 us
  waiting for transfers between devices  234 us (64%)
  starting transfers between devices  96.9 us (26%)
  matrix products  19.3 us (5%)
  other arithmetic  6.64 us (2%)
  local copies, waits for them, and re-layouts  4.05 us (1%)
    ppermute x33, waiting for transfers between devices, group_sum(): lax.ppermute(x, axis, [(i, i ^ step * k) for i in range(n)])  150 us
    ppermute x33, starting transfers between devices, group_sum(): lax.ppermute(x, axis, [(i, i ^ step * k) for i in range(n)])  73.3 us
    ppermute x10, waiting for transfers between devices, to_columns(): return lax.ppermute(x, GRID, pairs)  71.4 us
    ppermute x10, starting transfers between devices, to_columns(): return lax.ppermute(x, GRID, pairs)  14.1 us
    ppermute x10, waiting for transfers between devices, column_total(): x = x + lax.ppermute(x, 'col', [(i, i ^ 1) for i in range(n)])  11.9 us
    ppermute x10, starting transfers between devices, column_total(): x = x + lax.ppermute(x, 'col', [(i, i ^ 1) for i in range(n)])  9.5 us
  transfers between devices with their start and end apart: 53, of which 52 were waited for; matrix products, arithmetic and copies ran while one was open for 2% of the time, Pallas kernels for 0%

profile of v3, /device:TPU:96, one launch (start us, length us, event | category | flops | bytes accessed | tf_op | source)
XLA Modules:
  0.0 361.7 jit_solution(15307219155174409037)
XLA Ops:
  3.3 4.0 %collective-permute-start = (bf16[256,256]{1,0:T(8,128)(2,1)S(1)}, bf16[256,256]{1,0:T(8,128)(2,1)S(1)}, u32[]{:S(2)}, u32[]{:S(2)}) collective-permute-start(bf16[256,256]{1,0:T(8,128)(2,1)S(1)} %get-tuple-element.28), channel_id=1, source_target_pairs={{0,32},{1,24},{2,40},{6,16},{3,48},{7,8},{4,56},{5,0},{9,41},{8,33... | collective-permute-start | bytes 393224 | tf_op jit(solution)/shard_map/ppermute | solution.py:24
  9.8 5.4 %collective-permute-done = bf16[256,256]{1,0:T(8,128)(2,1)S(1)} collective-permute-done((bf16[256,256]{1,0:T(8,128)(2,1)S(1)}, bf16[256,256]{1,0:T(8,128)(2,1)S(1)}, u32[]{:S(2)}, u32[]{:S(2)}) %collective-permute-start) | collective-permute-done | bytes 131104 | tf_op jit(solution)/shard_map/ppermute | solution.py:24
  18.7 4.9 %collective-permute-start.4 = (f32[256,256]{1,0:T(8,128)S(1)}, f32[256,256]{1,0:T(8,128)S(1)}, u32[]{:S(2)}, u32[]{:S(2)}) collective-permute-start(f32[256,256]{1,0:T(8,128)S(1)} %add.136), channel_id=1, source_target_pairs={{0,6},{1,7},{2,4},{3,5},{4,2},{5,3},{6,0},{7,1},{8,14},{9,15},{10,... | collective-permute-start | bytes 786440 | tf_op jit(solution)/shard_map/ppermute | solution.py:34
  24.4 2.8 collective-permute-done.3
  27.2 8.0 %collective-permute-done.4 = f32[256,256]{1,0:T(8,128)S(1)} collective-permute-done((f32[256,256]{1,0:T(8,128)S(1)}, f32[256,256]{1,0:T(8,128)S(1)}, u32[]{:S(2)}, u32[]{:S(2)}) %collective-permute-start.4) | collective-permute-done | bytes 262176 | tf_op jit(solution)/shard_map/ppermute | solution.py:34
  38.4 6.7 %collective-permute-done.5 = bf16[256,256]{1,0:T(8,128)(2,1)S(1)} collective-permute-done((bf16[256,256]{1,0:T(8,128)(2,1)S(1)}, bf16[256,256]{1,0:T(8,128)(2,1)S(1)}, u32[]{:S(2)}, u32[]{:S(2)}) %collective-permute-start.5) | collective-permute-done | bytes 131104 | tf_op jit(solution)/shard_map/ppermute | solution.py:24
  50.0 3.8 %collective-permute-start.9 = (f32[256,256]{1,0:T(8,128)S(1)}, f32[256,256]{1,0:T(8,128)S(1)}, u32[]{:S(2)}, u32[]{:S(2)}) collective-permute-start(f32[256,256]{1,0:T(8,128)S(1)} %add.140), channel_id=1, source_target_pairs={{0,6},{1,7},{2,4},{3,5},{4,2},{5,3},{6,0},{7,1},{8,14},{9,15},{10,... | collective-permute-start | bytes 786440 | tf_op jit(solution)/shard_map/ppermute | solution.py:34
  54.6 4.0 %collective-permute-done.8 = f32[256,256]{1,0:T(8,128)S(1)} collective-permute-done((f32[256,256]{1,0:T(8,128)S(1)}, f32[256,256]{1,0:T(8,128)S(1)}, u32[]{:S(2)}, u32[]{:S(2)}) %collective-permute-start.8) | collective-permute-done | bytes 262176 | tf_op jit(solution)/shard_map/ppermute | solution.py:34
  58.5 6.8 %collective-permute-done.9 = f32[256,256]{1,0:T(8,128)S(1)} collective-permute-done((f32[256,256]{1,0:T(8,128)S(1)}, f32[256,256]{1,0:T(8,128)S(1)}, u32[]{:S(2)}, u32[]{:S(2)}) %collective-permute-start.9) | collective-permute-done | bytes 262176 | tf_op jit(solution)/shard_map/ppermute | solution.py:34
  68.5 7.4 %collective-permute-done.10 = bf16[256,256]{1,0:T(8,128)(2,1)S(1)} collective-permute-done((bf16[256,256]{1,0:T(8,128)(2,1)S(1)}, bf16[256,256]{1,0:T(8,128)(2,1)S(1)}, u32[]{:S(2)}, u32[]{:S(2)}) %collective-permute-start.10) | collective-permute-done | bytes 131104 | tf_op jit(solution)/shard_map/ppermute | solution.py:24
  80.8 3.6 collective-permute-start.14
  85.3 4.5 %collective-permute-done.13 = f32[256,256]{1,0:T(8,128)S(1)} collective-permute-done((f32[256,256]{1,0:T(8,128)S(1)}, f32[256,256]{1,0:T(8,128)S(1)}, u32[]{:S(2)}, u32[]{:S(2)}) %collective-permute-start.13) | collective-permute-done | bytes 262176 | tf_op jit(solution)/shard_map/ppermute | solution.py:34
  89.9 6.0 %collective-permute-done.14 = f32[256,256]{1,0:T(8,128)S(1)} collective-permute-done((f32[256,256]{1,0:T(8,128)S(1)}, f32[256,256]{1,0:T(8,128)S(1)}, u32[]{:S(2)}, u32[]{:S(2)}) %collective-permute-start.14) | collective-permute-done | bytes 262176 | tf_op jit(solution)/shard_map/ppermute | solution.py:34
  99.3 7.0 %collective-permute-done.15 = bf16[256,256]{1,0:T(8,128)(2,1)S(1)} collective-permute-done((bf16[256,256]{1,0:T(8,128)(2,1)S(1)}, bf16[256,256]{1,0:T(8,128)(2,1)S(1)}, u32[]{:S(2)}, u32[]{:S(2)}) %collective-permute-start.15) | collective-permute-done | bytes 131104 | tf_op jit(solution)/shard_map/ppermute | solution.py:24
  112.5 3.9 %collective-permute-start.19 = (f32[2,256,256]{2,1,0:T(8,128)S(1)}, f32[2,256,256]{2,1,0:T(8,128)S(1)}, u32[]{:S(2)}, u32[]{:S(2)}) collective-permute-start(f32[2,256,256]{2,1,0:T(8,128)S(1)} %fusion.102), channel_id=1, source_target_pairs={{0,6},{1,7},{2,4},{3,5},{4,2},{5,3},{6,0},{7,1},{8,14},{9,15},{10,... | collective-permute-start | bytes 1572872 | tf_op jit(solution)/shard_map/ppermute | solution.py:34
  117.1 10.0 %collective-permute-done.18 = f32[2,256,256]{2,1,0:T(8,128)S(1)} collective-permute-done((f32[2,256,256]{2,1,0:T(8,128)S(1)}, f32[2,256,256]{2,1,0:T(8,128)S(1)}, u32[]{:S(2)}, u32[]{:S(2)}) %collective-permute-start.18) | collective-permute-done | bytes 524320 | tf_op jit(solution)/shard_map/ppermute | solution.py:34
  127.1 12.0 %collective-permute-done.19 = f32[2,256,256]{2,1,0:T(8,128)S(1)} collective-permute-done((f32[2,256,256]{2,1,0:T(8,128)S(1)}, f32[2,256,256]{2,1,0:T(8,128)S(1)}, u32[]{:S(2)}, u32[]{:S(2)}) %collective-permute-start.19) | collective-permute-done | bytes 524320 | tf_op jit(solution)/shard_map/ppermute | solution.py:34
  140.5 3.3 collective-permute-start.21
  144.9 12.1 %collective-permute-done.21 = f32[2,256,256]{2,1,0:T(8,128)S(1)} collective-permute-done((f32[2,256,256]{2,1,0:T(8,128)S(1)}, f32[2,256,256]{2,1,0:T(8,128)S(1)}, u32[]{:S(2)}, u32[]{:S(2)}) %collective-permute-start.21) | collective-permute-done | bytes 524320 | tf_op jit(solution)/shard_map/ppermute | solution.py:34
  157.0 9.5 %collective-permute-done.22 = f32[2,256,256]{2,1,0:T(8,128)S(1)} collective-permute-done((f32[2,256,256]{2,1,0:T(8,128)S(1)}, f32[2,256,256]{2,1,0:T(8,128)S(1)}, u32[]{:S(2)}, u32[]{:S(2)}) %collective-permute-start.22) | collective-permute-done | bytes 524320 | tf_op jit(solution)/shard_map/ppermute | solution.py:34
  169.0 7.4 %collective-permute-done.23 = bf16[256,256]{0,1:T(8,128)(2,1)S(1)} collective-permute-done((bf16[256,256]{0,1:T(8,128)(2,1)S(1)}, bf16[256,256]{0,1:T(8,128)(2,1)S(1)}, u32[]{:S(2)}, u32[]{:S(2)}) %collective-permute-start.23) | collective-permute-done | bytes 131104 | tf_op jit(solution)/shard_map/ppermute | solution.py:24
  178.8 2.7 collective-permute-start.26
  181.5 3.8 %collective-permute-start.27 = (f32[256,256]{1,0:T(8,128)S(1)}, f32[256,256]{1,0:T(8,128)S(1)}, u32[]{:S(2)}, u32[]{:S(2)}) collective-permute-start(f32[256,256]{1,0:T(8,128)S(1)} %add.155), channel_id=1, source_target_pairs={{0,6},{1,7},{2,4},{3,5},{4,2},{5,3},{6,0},{7,1},{8,14},{9,15},{10,... | collective-permute-start | bytes 786440 | tf_op jit(solution)/shard_map/ppermute | solution.py:34
  186.1 3.4 collective-permute-done.26
  189.5 7.3 %collective-permute-done.27 = f32[256,256]{1,0:T(8,128)S(1)} collective-permute-done((f32[256,256]{1,0:T(8,128)S(1)}, f32[256,256]{1,0:T(8,128)S(1)}, u32[]{:S(2)}, u32[]{:S(2)}) %collective-permute-start.27) | collective-permute-done | bytes 262176 | tf_op jit(solution)/shard_map/ppermute | solution.py:34
  198.1 2.6 bitcast_convert_fusion.4
  200.7 7.6 %collective-permute-done.28 = bf16[256,256]{1,0:T(8,128)(2,1)S(1)} collective-permute-done((bf16[256,256]{1,0:T(8,128)(2,1)}, bf16[256,256]{1,0:T(8,128)(2,1)S(1)}, u32[]{:S(2)}, u32[]{:S(2)}) %collective-permute-start.28) | collective-permute-done | bytes 131104 | tf_op jit(solution)/shard_map/ppermute | solution.py:24
  210.7 2.7 collective-permute-start.31
  213.4 4.1 %collective-permute-start.32 = (f32[256,256]{0,1:T(8,128)S(1)}, f32[256,256]{0,1:T(8,128)S(1)}, u32[]{:S(2)}, u32[]{:S(2)}) collective-permute-start(f32[256,256]{0,1:T(8,128)S(1)} %add.160), channel_id=1, source_target_pairs={{0,6},{1,7},{2,4},{3,5},{4,2},{5,3},{6,0},{7,1},{8,14},{9,15},{10,... | collective-permute-start | bytes 786440 | tf_op jit(solution)/shard_map/ppermute | solution.py:34
  220.8 8.4 %collective-permute-done.32 = f32[256,256]{0,1:T(8,128)S(1)} collective-permute-done((f32[256,256]{0,1:T(8,128)S(1)}, f32[256,256]{0,1:T(8,128)S(1)}, u32[]{:S(2)}, u32[]{:S(2)}) %collective-permute-start.32) | collective-permute-done | bytes 262176 | tf_op jit(solution)/shard_map/ppermute | solution.py:34
  232.3 9.7 %collective-permute-start.33 = (bf16[256,256]{1,0:T(8,128)(2,1)S(1)}, bf16[256,256]{1,0:T(8,128)(2,1)S(1)}, u32[]{:S(2)}, u32[]{:S(2)}) collective-permute-start(bf16[256,256]{1,0:T(8,128)(2,1)S(1)} %get-tuple-element.40), channel_id=1, source_target_pairs={{0,32},{1,24},{2,40},{6,16},{3,48},{7,8},{4,56},{5,0},{9,41},{8,33... | collective-permute-start | bytes 393224 | tf_op jit(solution)/shard_map/ppermute | solution.py:24
  242.1 7.2 %collective-permute-done.33 = bf16[256,256]{1,0:T(8,128)(2,1)S(1)} collective-permute-done((bf16[256,256]{1,0:T(8,128)(2,1)S(1)}, bf16[256,256]{1,0:T(8,128)(2,1)S(1)}, u32[]{:S(2)}, u32[]{:S(2)}) %collective-permute-start.33) | collective-permute-done | bytes 131104 | tf_op jit(solution)/shard_map/ppermute | solution.py:24
  251.3 3.2 collective-permute-start.36
  254.4 3.7 %collective-permute-start.37 = (f32[256,256]{1,0:T(8,128)S(1)}, f32[256,256]{1,0:T(8,128)S(1)}, u32[]{:S(2)}, u32[]{:S(2)}) collective-permute-start(f32[256,256]{1,0:T(8,128)S(1)} %add.164), channel_id=1, source_target_pairs={{0,6},{1,7},{2,4},{3,5},{4,2},{5,3},{6,0},{7,1},{8,14},{9,15},{10,... | collective-permute-start | bytes 786440 | tf_op jit(solution)/shard_map/ppermute | solution.py:34
  258.9 2.4 collective-permute-done.36
  261.3 8.3 %collective-permute-done.37 = f32[256,256]{1,0:T(8,128)S(1)} collective-permute-done((f32[256,256]{1,0:T(8,128)S(1)}, f32[256,256]{1,0:T(8,128)S(1)}, u32[]{:S(2)}, u32[]{:S(2)}) %collective-permute-start.37) | collective-permute-done | bytes 262176 | tf_op jit(solution)/shard_map/ppermute | solution.py:34
  271.8 7.7 %collective-permute-done.38 = bf16[256,256]{1,0:T(8,128)(2,1)S(1)} collective-permute-done((bf16[256,256]{1,0:T(8,128)(2,1)S(1)}, bf16[256,256]{1,0:T(8,128)(2,1)S(1)}, u32[]{:S(2)}, u32[]{:S(2)}) %collective-permute-start.38) | collective-permute-done | bytes 131104 | tf_op jit(solution)/shard_map/ppermute | solution.py:24
  284.3 3.3 collective-permute-start.42
  288.4 4.6 %collective-permute-done.41 = f32[256,256]{1,0:T(8,128)S(1)} collective-permute-done((f32[256,256]{1,0:T(8,128)S(1)}, f32[256,256]{1,0:T(8,128)S(1)}, u32[]{:S(2)}, u32[]{:S(2)}) %collective-permute-start.41) | collective-permute-done | bytes 262176 | tf_op jit(solution)/shard_map/ppermute | solution.py:34
  293.0 6.1 %collective-permute-done.42 = f32[256,256]{1,0:T(8,128)S(1)} collective-permute-done((f32[256,256]{1,0:T(8,128)S(1)}, f32[256,256]{1,0:T(8,128)S(1)}, u32[]{:S(2)}, u32[]{:S(2)}) %collective-permute-start.42) | collective-permute-done | bytes 262176 | tf_op jit(solution)/shard_map/ppermute | solution.py:34
  301.3 7.6 %collective-permute-done.43 = bf16[256,256]{1,0:T(8,128)(2,1)S(1)} collective-permute-done((bf16[256,256]{1,0:T(8,128)(2,1)S(1)}, bf16[256,256]{1,0:T(8,128)(2,1)S(1)}, u32[]{:S(2)}, u32[]{:S(2)}) %collective-permute-start.43) | collective-permute-done | bytes 131104 | tf_op jit(solution)/shard_map/ppermute | solution.py:24
  313.8 3.3 collective-permute-start.47
  317.9 4.7 %collective-permute-done.46 = f32[256,256]{1,0:T(8,128)S(1)} collective-permute-done((f32[256,256]{1,0:T(8,128)S(1)}, f32[256,256]{1,0:T(8,128)S(1)}, u32[]{:S(2)}, u32[]{:S(2)}) %collective-permute-start.46) | collective-permute-done | bytes 262176 | tf_op jit(solution)/shard_map/ppermute | solution.py:34
  322.6 6.0 %collective-permute-done.47 = f32[256,256]{1,0:T(8,128)S(1)} collective-permute-done((f32[256,256]{1,0:T(8,128)S(1)}, f32[256,256]{1,0:T(8,128)S(1)}, u32[]{:S(2)}, u32[]{:S(2)}) %collective-permute-start.47) | collective-permute-done | bytes 262176 | tf_op jit(solution)/shard_map/ppermute | solution.py:34
  330.2 7.4 %collective-permute-done.48 = bf16[256,256]{1,0:T(8,128)(2,1)S(1)} collective-permute-done((bf16[256,256]{1,0:T(8,128)(2,1)S(1)}, bf16[256,256]{1,0:T(8,128)(2,1)S(1)}, u32[]{:S(2)}, u32[]{:S(2)}) %collective-permute-start.48) | collective-permute-done | bytes 131104 | tf_op jit(solution)/shard_map/ppermute | solution.py:24
  339.7 3.2 collective-permute-start.51
  342.8 3.5 collective-permute-start.52
  349.7 8.1 %collective-permute-done.52 = f32[256,256]{1,0:T(8,128)} collective-permute-done((f32[256,256]{1,0:T(8,128)S(1)}, f32[256,256]{1,0:T(8,128)}, u32[]{:S(2)}, u32[]{:S(2)}) %collective-permute-start.52) | collective-permute-done | bytes 262176 | tf_op jit(solution)/shard_map/ppermute | solution.py:34
  (166 shorter events, 84.8 us)
Async XLA Ops:
  3.3 11.9 %collective-permute-start = (bf16[256,256]{1,0:T(8,128)(2,1)S(1)}, bf16[256,256]{1,0:T(8,128)(2,1)S(1)}, u32[]{:S(2)}, u32[]{:S(2)}) collective-permute-start(bf16[256,256]{1,0:T(8,128)(2,1)S(1)} %get-tuple-element.28), channel_id=1, source_target_pairs={{0,32},{1,24},{2,40},{6,16},{3,48},{7,8},{4,56},{5,0},{9,41},{8,33... | collective-permute-start | bytes 393224 | tf_op jit(solution)/shard_map/ppermute | solution.py:24
  17.1 10.1 %collective-permute-start.3 = (f32[256,256]{1,0:T(8,128)S(1)}, f32[256,256]{1,0:T(8,128)S(1)}, u32[]{:S(2)}, u32[]{:S(2)}) collective-permute-start(f32[256,256]{1,0:T(8,128)S(1)} %add.136), channel_id=1, source_target_pairs={{0,4},{1,5},{2,6},{3,7},{4,0},{5,1},{6,2},{7,3},{8,12},{9,13},{10,... | collective-permute-start | bytes 786440 | tf_op jit(solution)/shard_map/ppermute | solution.py:34
  18.7 16.4 %collective-permute-start.4 = (f32[256,256]{1,0:T(8,128)S(1)}, f32[256,256]{1,0:T(8,128)S(1)}, u32[]{:S(2)}, u32[]{:S(2)}) collective-permute-start(f32[256,256]{1,0:T(8,128)S(1)} %add.136), channel_id=1, source_target_pairs={{0,6},{1,7},{2,4},{3,5},{4,2},{5,3},{6,0},{7,1},{8,14},{9,15},{10,... | collective-permute-start | bytes 786440 | tf_op jit(solution)/shard_map/ppermute | solution.py:34
  23.6 12.7 %collective-permute-start.2 = (f32[256,256]{1,0:T(8,128)S(1)}, f32[256,256]{1,0:T(8,128)S(1)}, u32[]{:S(2)}, u32[]{:S(2)}) collective-permute-start(f32[256,256]{1,0:T(8,128)S(1)} %add.136), channel_id=1, source_target_pairs={{0,2},{1,3},{2,0},{3,1},{4,6},{5,7},{6,4},{7,5},{8,10},{9,11},{10,... | collective-permute-start | bytes 786440 | tf_op jit(solution)/shard_map/ppermute | solution.py:34
  37.5 7.5 %collective-permute-start.5 = (bf16[256,256]{1,0:T(8,128)(2,1)S(1)}, bf16[256,256]{1,0:T(8,128)(2,1)S(1)}, u32[]{:S(2)}, u32[]{:S(2)}) collective-permute-start(bf16[256,256]{1,0:T(8,128)(2,1)S(1)} %get-tuple-element.30), channel_id=1, source_target_pairs={{0,32},{1,24},{2,40},{6,16},{3,48},{7,8},{4,56},{5,0},{9,41},{8,33... | collective-permute-start | bytes 393224 | tf_op jit(solution)/shard_map/ppermute | solution.py:24
  45.3 2.3 collective-permute-start.6
  47.7 10.8 %collective-permute-start.8 = (f32[256,256]{1,0:T(8,128)S(1)}, f32[256,256]{1,0:T(8,128)S(1)}, u32[]{:S(2)}, u32[]{:S(2)}) collective-permute-start(f32[256,256]{1,0:T(8,128)S(1)} %add.140), channel_id=1, source_target_pairs={{0,4},{1,5},{2,6},{3,7},{4,0},{5,1},{6,2},{7,3},{8,12},{9,13},{10,... | collective-permute-start | bytes 786440 | tf_op jit(solution)/shard_map/ppermute | solution.py:34
  50.0 15.3 %collective-permute-start.9 = (f32[256,256]{1,0:T(8,128)S(1)}, f32[256,256]{1,0:T(8,128)S(1)}, u32[]{:S(2)}, u32[]{:S(2)}) collective-permute-start(f32[256,256]{1,0:T(8,128)S(1)} %add.140), channel_id=1, source_target_pairs={{0,6},{1,7},{2,4},{3,5},{4,2},{5,3},{6,0},{7,1},{8,14},{9,15},{10,... | collective-permute-start | bytes 786440 | tf_op jit(solution)/shard_map/ppermute | solution.py:34
  53.8 12.7 %collective-permute-start.7 = (f32[256,256]{1,0:T(8,128)S(1)}, f32[256,256]{1,0:T(8,128)S(1)}, u32[]{:S(2)}, u32[]{:S(2)}) collective-permute-start(f32[256,256]{1,0:T(8,128)S(1)} %add.140), channel_id=1, source_target_pairs={{0,2},{1,3},{2,0},{3,1},{4,6},{5,7},{6,4},{7,5},{8,10},{9,11},{10,... | collective-permute-start | bytes 786440 | tf_op jit(solution)/shard_map/ppermute | solution.py:34
  68.5 7.4 %collective-permute-start.10 = (bf16[256,256]{1,0:T(8,128)(2,1)S(1)}, bf16[256,256]{1,0:T(8,128)(2,1)S(1)}, u32[]{:S(2)}, u32[]{:S(2)}) collective-permute-start(bf16[256,256]{1,0:T(8,128)(2,1)S(1)} %get-tuple-element.32), channel_id=1, source_target_pairs={{0,32},{1,24},{2,40},{6,16},{3,48},{7,8},{4,56},{5,0},{9,41},{8,33... | collective-permute-start | bytes 393224 | tf_op jit(solution)/shard_map/ppermute | solution.py:24
  76.1 2.9 collective-permute-start.11
  79.1 10.8 %collective-permute-start.13 = (f32[256,256]{1,0:T(8,128)S(1)}, f32[256,256]{1,0:T(8,128)S(1)}, u32[]{:S(2)}, u32[]{:S(2)}) collective-permute-start(f32[256,256]{1,0:T(8,128)S(1)} %add.144), channel_id=1, source_target_pairs={{0,4},{1,5},{2,6},{3,7},{4,0},{5,1},{6,2},{7,3},{8,12},{9,13},{10,... | collective-permute-start | bytes 786440 | tf_op jit(solution)/shard_map/ppermute | solution.py:34
  80.8 15.1 %collective-permute-start.14 = (f32[256,256]{1,0:T(8,128)S(1)}, f32[256,256]{1,0:T(8,128)S(1)}, u32[]{:S(2)}, u32[]{:S(2)}) collective-permute-start(f32[256,256]{1,0:T(8,128)S(1)} %add.144), channel_id=1, source_target_pairs={{0,6},{1,7},{2,4},{3,5},{4,2},{5,3},{6,0},{7,1},{8,14},{9,15},{10,... | collective-permute-start | bytes 786440 | tf_op jit(solution)/shard_map/ppermute | solution.py:34
  84.4 12.7 %collective-permute-start.12 = (f32[256,256]{1,0:T(8,128)S(1)}, f32[256,256]{1,0:T(8,128)S(1)}, u32[]{:S(2)}, u32[]{:S(2)}) collective-permute-start(f32[256,256]{1,0:T(8,128)S(1)} %add.144), channel_id=1, source_target_pairs={{0,2},{1,3},{2,0},{3,1},{4,6},{5,7},{6,4},{7,5},{8,10},{9,11},{10,... | collective-permute-start | bytes 786440 | tf_op jit(solution)/shard_map/ppermute | solution.py:34
  99.0 7.4 %collective-permute-start.15 = (bf16[256,256]{1,0:T(8,128)(2,1)S(1)}, bf16[256,256]{1,0:T(8,128)(2,1)S(1)}, u32[]{:S(2)}, u32[]{:S(2)}) collective-permute-start(bf16[256,256]{1,0:T(8,128)(2,1)S(1)} %get-tuple-element.34), channel_id=1, source_target_pairs={{0,32},{1,24},{2,40},{6,16},{3,48},{7,8},{4,56},{5,0},{9,41},{8,33... | collective-permute-start | bytes 393224 | tf_op jit(solution)/shard_map/ppermute | solution.py:24
  107.1 3.5 collective-permute-start.16
  110.7 16.4 %collective-permute-start.18 = (f32[2,256,256]{2,1,0:T(8,128)S(1)}, f32[2,256,256]{2,1,0:T(8,128)S(1)}, u32[]{:S(2)}, u32[]{:S(2)}) collective-permute-start(f32[2,256,256]{2,1,0:T(8,128)S(1)} %fusion.102), channel_id=1, source_target_pairs={{0,4},{1,5},{2,6},{3,7},{4,0},{5,1},{6,2},{7,3},{8,12},{9,13},{10,... | collective-permute-start | bytes 1572872 | tf_op jit(solution)/shard_map/ppermute | solution.py:34
  112.5 26.6 %collective-permute-start.19 = (f32[2,256,256]{2,1,0:T(8,128)S(1)}, f32[2,256,256]{2,1,0:T(8,128)S(1)}, u32[]{:S(2)}, u32[]{:S(2)}) collective-permute-start(f32[2,256,256]{2,1,0:T(8,128)S(1)} %fusion.102), channel_id=1, source_target_pairs={{0,6},{1,7},{2,4},{3,5},{4,2},{5,3},{6,0},{7,1},{8,14},{9,15},{10,... | collective-permute-start | bytes 1572872 | tf_op jit(solution)/shard_map/ppermute | solution.py:34
  116.4 24.0 %collective-permute-start.17 = (f32[2,256,256]{2,1,0:T(8,128)S(1)}, f32[2,256,256]{2,1,0:T(8,128)S(1)}, u32[]{:S(2)}, u32[]{:S(2)}) collective-permute-start(f32[2,256,256]{2,1,0:T(8,128)S(1)} %fusion.102), channel_id=1, source_target_pairs={{0,2},{1,3},{2,0},{3,1},{4,6},{5,7},{6,4},{7,5},{8,10},{9,11},{10,... | collective-permute-start | bytes 1572872 | tf_op jit(solution)/shard_map/ppermute | solution.py:34
  140.5 16.4 %collective-permute-start.21 = (f32[2,256,256]{2,1,0:T(8,128)S(1)}, f32[2,256,256]{2,1,0:T(8,128)S(1)}, u32[]{:S(2)}, u32[]{:S(2)}) collective-permute-start(f32[2,256,256]{2,1,0:T(8,128)S(1)} %add_add_fusion.1), channel_id=1, source_target_pairs={{0,128},{64,192},{128,0},{192,64},{1,129},{65,193},{129,1},{193,65... | collective-permute-start | bytes 1572872 | tf_op jit(solution)/shard_map/ppermute | solution.py:34
  143.8 22.7 %collective-permute-start.22 = (f32[2,256,256]{2,1,0:T(8,128)S(1)}, f32[2,256,256]{2,1,0:T(8,128)S(1)}, u32[]{:S(2)}, u32[]{:S(2)}) collective-permute-start(f32[2,256,256]{2,1,0:T(8,128)S(1)} %add_add_fusion.1), channel_id=1, source_target_pairs={{0,192},{64,128},{128,64},{192,0},{1,193},{65,129},{129,65},{193,1... | collective-permute-start | bytes 1572872 | tf_op jit(solution)/shard_map/ppermute | solution.py:34
  144.9 22.0 %collective-permute-start.20 = (f32[2,256,256]{2,1,0:T(8,128)S(1)}, f32[2,256,256]{2,1,0:T(8,128)S(1)}, u32[]{:S(2)}, u32[]{:S(2)}) collective-permute-start(f32[2,256,256]{2,1,0:T(8,128)S(1)} %add_add_fusion.1), channel_id=1, source_target_pairs={{0,64},{64,0},{128,192},{192,128},{1,65},{65,1},{129,193},{193,129... | collective-permute-start | bytes 1572872 | tf_op jit(solution)/shard_map/ppermute | solution.py:34
  168.8 7.6 %collective-permute-start.23 = (bf16[256,256]{0,1:T(8,128)(2,1)S(1)}, bf16[256,256]{0,1:T(8,128)(2,1)S(1)}, u32[]{:S(2)}, u32[]{:S(2)}) collective-permute-start(bf16[256,256]{0,1:T(8,128)(2,1)S(1)} %get-tuple-element.36), channel_id=1, source_target_pairs={{0,32},{1,24},{2,40},{6,16},{3,48},{7,8},{4,56},{5,0},{9,41},{8,33... | collective-permute-start | bytes 393224 | tf_op jit(solution)/shard_map/ppermute | solution.py:24
  178.8 10.7 %collective-permute-start.26 = (f32[256,256]{1,0:T(8,128)S(1)}, f32[256,256]{1,0:T(8,128)S(1)}, u32[]{:S(2)}, u32[]{:S(2)}) collective-permute-start(f32[256,256]{1,0:T(8,128)S(1)} %add.155), channel_id=1, source_target_pairs={{0,4},{1,5},{2,6},{3,7},{4,0},{5,1},{6,2},{7,3},{8,12},{9,13},{10,... | collective-permute-start | bytes 786440 | tf_op jit(solution)/shard_map/ppermute | solution.py:34
  181.5 15.3 %collective-permute-start.27 = (f32[256,256]{1,0:T(8,128)S(1)}, f32[256,256]{1,0:T(8,128)S(1)}, u32[]{:S(2)}, u32[]{:S(2)}) collective-permute-start(f32[256,256]{1,0:T(8,128)S(1)} %add.155), channel_id=1, source_target_pairs={{0,6},{1,7},{2,4},{3,5},{4,2},{5,3},{6,0},{7,1},{8,14},{9,15},{10,... | collective-permute-start | bytes 786440 | tf_op jit(solution)/shard_map/ppermute | solution.py:34
  185.3 12.8 %collective-permute-start.25 = (f32[256,256]{1,0:T(8,128)S(1)}, f32[256,256]{1,0:T(8,128)}, u32[]{:S(2)}, u32[]{:S(2)}) collective-permute-start(f32[256,256]{1,0:T(8,128)S(1)} %add.155), channel_id=1, source_target_pairs={{0,2},{1,3},{2,0},{3,1},{4,6},{5,7},{6,4},{7,5},{8,10},{9,11},{10,... | collective-permute-start | bytes 786440 | tf_op jit(solution)/shard_map/ppermute | solution.py:34
  200.7 7.6 %collective-permute-start.28 = (bf16[256,256]{1,0:T(8,128)(2,1)}, bf16[256,256]{1,0:T(8,128)(2,1)S(1)}, u32[]{:S(2)}, u32[]{:S(2)}) collective-permute-start(bf16[256,256]{1,0:T(8,128)(2,1)} %get-tuple-element.38), channel_id=1, source_target_pairs={{0,32},{1,24},{2,40},{6,16},{3,48},{7,8},{4,56},{5,0},{9,41},{8,33... | collective-permute-start | bytes 393224 | tf_op jit(solution)/shard_map/ppermute | solution.py:24
  210.7 10.1 %collective-permute-start.31 = (f32[256,256]{0,1:T(8,128)S(1)}, f32[256,256]{0,1:T(8,128)S(1)}, u32[]{:S(2)}, u32[]{:S(2)}) collective-permute-start(f32[256,256]{0,1:T(8,128)S(1)} %add.160), channel_id=1, source_target_pairs={{0,4},{1,5},{2,6},{3,7},{4,0},{5,1},{6,2},{7,3},{8,12},{9,13},{10,... | collective-permute-start | bytes 786440 | tf_op jit(solution)/shard_map/ppermute | solution.py:34
  213.4 15.8 %collective-permute-start.32 = (f32[256,256]{0,1:T(8,128)S(1)}, f32[256,256]{0,1:T(8,128)S(1)}, u32[]{:S(2)}, u32[]{:S(2)}) collective-permute-start(f32[256,256]{0,1:T(8,128)S(1)} %add.160), channel_id=1, source_target_pairs={{0,6},{1,7},{2,4},{3,5},{4,2},{5,3},{6,0},{7,1},{8,14},{9,15},{10,... | collective-permute-start | bytes 786440 | tf_op jit(solution)/shard_map/ppermute | solution.py:34
  217.6 12.9 %collective-permute-start.30 = (f32[256,256]{0,1:T(8,128)S(1)}, f32[256,256]{0,1:T(8,128)S(1)}, u32[]{:S(2)}, u32[]{:S(2)}) collective-permute-start(f32[256,256]{0,1:T(8,128)S(1)} %add.160), channel_id=1, source_target_pairs={{0,2},{1,3},{2,0},{3,1},{4,6},{5,7},{6,4},{7,5},{8,10},{9,11},{10,... | collective-permute-start | bytes 786440 | tf_op jit(solution)/shard_map/ppermute | solution.py:34
  232.3 17.0 %collective-permute-start.33 = (bf16[256,256]{1,0:T(8,128)(2,1)S(1)}, bf16[256,256]{1,0:T(8,128)(2,1)S(1)}, u32[]{:S(2)}, u32[]{:S(2)}) collective-permute-start(bf16[256,256]{1,0:T(8,128)(2,1)S(1)} %get-tuple-element.40), channel_id=1, source_target_pairs={{0,32},{1,24},{2,40},{6,16},{3,48},{7,8},{4,56},{5,0},{9,41},{8,33... | collective-permute-start | bytes 393224 | tf_op jit(solution)/shard_map/ppermute | solution.py:24
  251.3 10.0 %collective-permute-start.36 = (f32[256,256]{1,0:T(8,128)S(1)}, f32[256,256]{1,0:T(8,128)S(1)}, u32[]{:S(2)}, u32[]{:S(2)}) collective-permute-start(f32[256,256]{1,0:T(8,128)S(1)} %add.164), channel_id=1, source_target_pairs={{0,4},{1,5},{2,6},{3,7},{4,0},{5,1},{6,2},{7,3},{8,12},{9,13},{10,... | collective-permute-start | bytes 786440 | tf_op jit(solution)/shard_map/ppermute | solution.py:34
  254.4 15.2 %collective-permute-start.37 = (f32[256,256]{1,0:T(8,128)S(1)}, f32[256,256]{1,0:T(8,128)S(1)}, u32[]{:S(2)}, u32[]{:S(2)}) collective-permute-start(f32[256,256]{1,0:T(8,128)S(1)} %add.164), channel_id=1, source_target_pairs={{0,6},{1,7},{2,4},{3,5},{4,2},{5,3},{6,0},{7,1},{8,14},{9,15},{10,... | collective-permute-start | bytes 786440 | tf_op jit(solution)/shard_map/ppermute | solution.py:34
  258.1 12.7 %collective-permute-start.35 = (f32[256,256]{1,0:T(8,128)S(1)}, f32[256,256]{1,0:T(8,128)S(1)}, u32[]{:S(2)}, u32[]{:S(2)}) collective-permute-start(f32[256,256]{1,0:T(8,128)S(1)} %add.164), channel_id=1, source_target_pairs={{0,2},{1,3},{2,0},{3,1},{4,6},{5,7},{6,4},{7,5},{8,10},{9,11},{10,... | collective-permute-start | bytes 786440 | tf_op jit(solution)/shard_map/ppermute | solution.py:34
  271.8 7.7 %collective-permute-start.38 = (bf16[256,256]{1,0:T(8,128)(2,1)S(1)}, bf16[256,256]{1,0:T(8,128)(2,1)S(1)}, u32[]{:S(2)}, u32[]{:S(2)}) collective-permute-start(bf16[256,256]{1,0:T(8,128)(2,1)S(1)} %get-tuple-element.42), channel_id=1, source_target_pairs={{0,32},{1,24},{2,40},{6,16},{3,48},{7,8},{4,56},{5,0},{9,41},{8,33... | collective-permute-start | bytes 393224 | tf_op jit(solution)/shard_map/ppermute | solution.py:24
  279.8 2.4 collective-permute-start.39
  282.2 10.8 %collective-permute-start.41 = (f32[256,256]{1,0:T(8,128)S(1)}, f32[256,256]{1,0:T(8,128)S(1)}, u32[]{:S(2)}, u32[]{:S(2)}) collective-permute-start(f32[256,256]{1,0:T(8,128)S(1)} %add.168), channel_id=1, source_target_pairs={{0,4},{1,5},{2,6},{3,7},{4,0},{5,1},{6,2},{7,3},{8,12},{9,13},{10,... | collective-permute-start | bytes 786440 | tf_op jit(solution)/shard_map/ppermute | solution.py:34
  284.3 14.8 %collective-permute-start.42 = (f32[256,256]{1,0:T(8,128)S(1)}, f32[256,256]{1,0:T(8,128)S(1)}, u32[]{:S(2)}, u32[]{:S(2)}) collective-permute-start(f32[256,256]{1,0:T(8,128)S(1)} %add.168), channel_id=1, source_target_pairs={{0,6},{1,7},{2,4},{3,5},{4,2},{5,3},{6,0},{7,1},{8,14},{9,15},{10,... | collective-permute-start | bytes 786440 | tf_op jit(solution)/shard_map/ppermute | solution.py:34
  287.6 12.7 %collective-permute-start.40 = (f32[256,256]{1,0:T(8,128)S(1)}, f32[256,256]{1,0:T(8,128)S(1)}, u32[]{:S(2)}, u32[]{:S(2)}) collective-permute-start(f32[256,256]{1,0:T(8,128)S(1)} %add.168), channel_id=1, source_target_pairs={{0,2},{1,3},{2,0},{3,1},{4,6},{5,7},{6,4},{7,5},{8,10},{9,11},{10,... | collective-permute-start | bytes 786440 | tf_op jit(solution)/shard_map/ppermute | solution.py:34
  301.3 7.6 %collective-permute-start.43 = (bf16[256,256]{1,0:T(8,128)(2,1)S(1)}, bf16[256,256]{1,0:T(8,128)(2,1)S(1)}, u32[]{:S(2)}, u32[]{:S(2)}) collective-permute-start(bf16[256,256]{1,0:T(8,128)(2,1)S(1)} %get-tuple-element.44), channel_id=1, source_target_pairs={{0,32},{1,24},{2,40},{6,16},{3,48},{7,8},{4,56},{5,0},{9,41},{8,33... | collective-permute-start | bytes 393224 | tf_op jit(solution)/shard_map/ppermute | solution.py:24
  309.2 2.6 collective-permute-start.44
  311.8 10.8 %collective-permute-start.46 = (f32[256,256]{1,0:T(8,128)S(1)}, f32[256,256]{1,0:T(8,128)S(1)}, u32[]{:S(2)}, u32[]{:S(2)}) collective-permute-start(f32[256,256]{1,0:T(8,128)S(1)} %add.172), channel_id=1, source_target_pairs={{0,4},{1,5},{2,6},{3,7},{4,0},{5,1},{6,2},{7,3},{8,12},{9,13},{10,... | collective-permute-start | bytes 786440 | tf_op jit(solution)/shard_map/ppermute | solution.py:34
  313.8 14.8 %collective-permute-start.47 = (f32[256,256]{1,0:T(8,128)S(1)}, f32[256,256]{1,0:T(8,128)S(1)}, u32[]{:S(2)}, u32[]{:S(2)}) collective-permute-start(f32[256,256]{1,0:T(8,128)S(1)} %add.172), channel_id=1, source_target_pairs={{0,6},{1,7},{2,4},{3,5},{4,2},{5,3},{6,0},{7,1},{8,14},{9,15},{10,... | collective-permute-start | bytes 786440 | tf_op jit(solution)/shard_map/ppermute | solution.py:34
  317.1 12.7 %collective-permute-start.45 = (f32[256,256]{1,0:T(8,128)S(1)}, f32[256,256]{1,0:T(8,128)S(1)}, u32[]{:S(2)}, u32[]{:S(2)}) collective-permute-start(f32[256,256]{1,0:T(8,128)S(1)} %add.172), channel_id=1, source_target_pairs={{0,2},{1,3},{2,0},{3,1},{4,6},{5,7},{6,4},{7,5},{8,10},{9,11},{10,... | collective-permute-start | bytes 786440 | tf_op jit(solution)/shard_map/ppermute | solution.py:34
  330.1 7.5 %collective-permute-start.48 = (bf16[256,256]{1,0:T(8,128)(2,1)S(1)}, bf16[256,256]{1,0:T(8,128)(2,1)S(1)}, u32[]{:S(2)}, u32[]{:S(2)}) collective-permute-start(bf16[256,256]{1,0:T(8,128)(2,1)S(1)} %get-tuple-element.46), channel_id=1, source_target_pairs={{0,32},{1,24},{2,40},{6,16},{3,48},{7,8},{4,56},{5,0},{9,41},{8,33... | collective-permute-start | bytes 393224 | tf_op jit(solution)/shard_map/ppermute | solution.py:24
  339.7 10.1 %collective-permute-start.51 = (f32[256,256]{1,0:T(8,128)S(1)}, f32[256,256]{1,0:T(8,128)S(1)}, u32[]{:S(2)}, u32[]{:S(2)}) collective-permute-start(f32[256,256]{1,0:T(8,128)S(1)} %add.176), channel_id=1, source_target_pairs={{0,4},{1,5},{2,6},{3,7},{4,0},{5,1},{6,2},{7,3},{8,12},{9,13},{10,... | collective-permute-start | bytes 786440 | tf_op jit(solution)/shard_map/ppermute | solution.py:34
  342.8 15.0 %collective-permute-start.52 = (f32[256,256]{1,0:T(8,128)S(1)}, f32[256,256]{1,0:T(8,128)}, u32[]{:S(2)}, u32[]{:S(2)}) collective-permute-start(f32[256,256]{1,0:T(8,128)S(1)} %add.176), channel_id=1, source_target_pairs={{0,6},{1,7},{2,4},{3,5},{4,2},{5,3},{6,0},{7,1},{8,14},{9,15},{10,... | collective-permute-start | bytes 786440 | tf_op jit(solution)/shard_map/ppermute | solution.py:34
  346.3 12.8 %collective-permute-start.50 = (f32[256,256]{1,0:T(8,128)S(1)}, f32[256,256]{1,0:T(8,128)}, u32[]{:S(2)}, u32[]{:S(2)}) collective-permute-start(f32[256,256]{1,0:T(8,128)S(1)} %add.176), channel_id=1, source_target_pairs={{0,2},{1,3},{2,0},{3,1},{4,6},{5,7},{6,4},{7,5},{8,10},{9,11},{10,... | collective-permute-start | bytes 786440 | tf_op jit(solution)/shard_map/ppermute | solution.py:34
  (26 other events, 532.4 us)

commit v4 on v3

--- a/solution.py
+++ b/solution.py
@@ -41,9 +41,11 @@
 
 
 def products(blocks, segments):
-    return jnp.einsum(
-        "jbk,jkr->br", jnp.stack(blocks, 0), jnp.stack(segments, 0), preferred_element_type=jnp.float32
-    )
+    total = None
+    for block, segment in zip(blocks, segments):
+        term = jnp.dot(block, segment, preferred_element_type=jnp.float32)
+        total = term if total is None else total + term
+    return total
 
 
 def shards(
@@ -108,7 +110,8 @@
         resid = (top_rhs[top] - summed).astype(bf16)
         solved = jnp.dot(tinv[0, top], resid, preferred_element_type=f32)
         yts.append(solved)
-        tsegs.append(to_columns(solved.astype(bf16), n))
+        if top < tops - 1:
+            tsegs.append(to_columns(solved.astype(bf16), n))
 
     zts = [None] * tops
     tback = [None] * tops
@@ -116,7 +119,8 @@
         if top == tops - 1:
             resid = yts[top].astype(bf16)
         else:
-            part = products([tm[top, j] for j in range(top + 1, tops)], tback[top + 1 :])
+            later = list(reversed(range(top + 1, tops)))
+            part = products([tm[top, j] for j in later], [tback[j] for j in later])
             resid = (yts[top] - column_total(part, ncol)).astype(bf16)
         solved = jnp.dot(tinv[1, top], resid, preferred_element_type=f32)
         zts[top] = solved
@@ -125,8 +129,10 @@
     zs = [None] * levels
     back = [None] * levels
     for level in reversed(range(levels)):
-        blocks = [um[level, t] for t in range(tops)] + [fm[level, j] for j in range(level + 1, levels)]
-        part = products(blocks, tback + back[level + 1 :])
+        later = list(reversed(range(level + 1, levels)))
+        earlier_tops = list(reversed(range(tops)))
+        blocks = [um[level, t] for t in earlier_tops] + [fm[level, j] for j in later]
+        part = products(blocks, [tback[t] for t in earlier_tops] + [back[j] for j in later])
         resid = (ys[level] - column_total(part, ncol)).astype(bf16)
         solved = keep[level] * jnp.dot(inv[1, level], resid, preferred_element_type=f32)
         zs[level] = solved

time: 366 us -> 384 us (1.049)
  waiting for transfers between devices: 234 us -> 256 us
  starting transfers between devices: 96.9 us -> 88.2 us
  matrix products: 19.3 us -> 23.6 us
    ppermute x33, waiting for transfers between devices: 150 us -> 175 us  [group_sum(): lax.ppermute(x, axis, [(i, i ^ step * k) for i in range(n)])]
    ppermute x33, starting transfers between devices: 73.3 us -> 63.8 us  [group_sum(): lax.ppermute(x, axis, [(i, i ^ step * k) for i in range(n)])]
  transfers between devices with their start and end apart: 53 -> 53, of which waited for: 52 -> 53; matrix products, arithmetic and copies ran while one was open for 2% -> 3% of each run, Pallas kernels for 0% -> 0%
where the time goes in v4:
time: 384 us; the launch traced here: 380 us
  waiting for transfers between devices  256 us (67%)
  starting transfers between devices  88.2 us (23%)
  matrix products  23.6 us (6%)
  other arithmetic  8.49 us (2%)
    ppermute x33, waiting for transfers between devices, group_sum(): lax.ppermute(x, axis, [(i, i ^ step * k) for i in range(n)])  175 us
    ppermute x10, waiting for transfers between devices, to_columns(): return lax.ppermute(x, GRID, pairs)  68 us
    ppermute x33, starting transfers between devices, group_sum(): lax.ppermute(x, axis, [(i, i ^ step * k) for i in range(n)])  63.8 us
    ppermute x10, starting transfers between devices, to_columns(): return lax.ppermute(x, GRID, pairs)  13.5 us
    ppermute x10, waiting for transfers between devices, column_total(): x = x + lax.ppermute(x, 'col', [(i, i ^ 1) for i in range(n)])  12.7 us
    ppermute x10, starting transfers between devices, column_total(): x = x + lax.ppermute(x, 'col', [(i, i ^ 1) for i in range(n)])  10.9 us
  transfers between devices with their start and end apart: 53, of which 53 were waited for; matrix products, arithmetic and copies ran while one was open for 3% of the time, Pallas kernels for 0%

profile of v4, /device:TPU:96, one launch (start us, length us, event | category | flops | bytes accessed | tf_op | source)
XLA Modules:
  0.0 380.0 jit_solution(13757202931269834334)
XLA Ops:
  3.3 4.0 %collective-permute-start = (bf16[256,256]{1,0:T(8,128)(2,1)S(1)}, bf16[256,256]{1,0:T(8,128)(2,1)S(1)}, u32[]{:S(2)}, u32[]{:S(2)}) collective-permute-start(bf16[256,256]{1,0:T(8,128)(2,1)S(1)} %get-tuple-element.6), channel_id=1, source_target_pairs={{0,32},{1,24},{2,40},{6,16},{3,48},{7,8},{4,56},{5,0},{9,41},{8,33... | collective-permute-start | bytes 393224 | tf_op jit(solution)/shard_map/ppermute | solution.py:24
  9.8 5.4 %collective-permute-done = bf16[256,256]{1,0:T(8,128)(2,1)S(1)} collective-permute-done((bf16[256,256]{1,0:T(8,128)(2,1)S(1)}, bf16[256,256]{1,0:T(8,128)(2,1)S(1)}, u32[]{:S(2)}, u32[]{:S(2)}) %collective-permute-start) | collective-permute-done | bytes 131104 | tf_op jit(solution)/shard_map/ppermute | solution.py:24
  17.2 7.9 %collective-permute-start.3 = (f32[256,256]{1,0:T(8,128)S(1)}, f32[256,256]{1,0:T(8,128)S(1)}, u32[]{:S(2)}, u32[]{:S(2)}) collective-permute-start(f32[256,256]{1,0:T(8,128)S(1)} %add.193), channel_id=1, source_target_pairs={{0,4},{1,5},{2,6},{3,7},{4,0},{5,1},{6,2},{7,3},{8,12},{9,13},{10,... | collective-permute-start | bytes 786440 | tf_op jit(solution)/shard_map/ppermute | solution.py:34
  25.8 11.3 %collective-permute-done.3 = f32[256,256]{1,0:T(8,128)S(1)} collective-permute-done((f32[256,256]{1,0:T(8,128)S(1)}, f32[256,256]{1,0:T(8,128)S(1)}, u32[]{:S(2)}, u32[]{:S(2)}) %collective-permute-start.3) | collective-permute-done | bytes 262176 | tf_op jit(solution)/shard_map/ppermute | solution.py:34
  37.1 2.6 collective-permute-done.4
  41.0 7.1 %collective-permute-done.5 = bf16[256,256]{0,1:T(8,128)(2,1)S(1)} collective-permute-done((bf16[256,256]{0,1:T(8,128)(2,1)S(1)}, bf16[256,256]{0,1:T(8,128)(2,1)S(1)}, u32[]{:S(2)}, u32[]{:S(2)}) %collective-permute-start.5) | collective-permute-done | bytes 131104 | tf_op jit(solution)/shard_map/ppermute | solution.py:24
  50.4 7.2 %collective-permute-start.8 = (f32[256,256]{1,0:T(8,128)S(1)}, f32[256,256]{1,0:T(8,128)S(1)}, u32[]{:S(2)}, u32[]{:S(2)}) collective-permute-start(f32[256,256]{1,0:T(8,128)S(1)} %add.199), channel_id=1, source_target_pairs={{0,4},{1,5},{2,6},{3,7},{4,0},{5,1},{6,2},{7,3},{8,12},{9,13},{10,... | collective-permute-start | bytes 786440 | tf_op jit(solution)/shard_map/ppermute | solution.py:34
  59.4 10.2 %collective-permute-done.8 = f32[256,256]{1,0:T(8,128)S(1)} collective-permute-done((f32[256,256]{1,0:T(8,128)S(1)}, f32[256,256]{1,0:T(8,128)S(1)}, u32[]{:S(2)}, u32[]{:S(2)}) %collective-permute-start.8) | collective-permute-done | bytes 262176 | tf_op jit(solution)/shard_map/ppermute | solution.py:34
  69.7 2.6 collective-permute-done.9
  74.4 7.0 %collective-permute-done.10 = bf16[256,256]{0,1:T(8,128)(2,1)S(1)} collective-permute-done((bf16[256,256]{0,1:T(8,128)(2,1)S(1)}, bf16[256,256]{0,1:T(8,128)(2,1)S(1)}, u32[]{:S(2)}, u32[]{:S(2)}) %collective-permute-start.10) | collective-permute-done | bytes 131104 | tf_op jit(solution)/shard_map/ppermute | solution.py:24
  83.8 6.5 %collective-permute-start.13 = (f32[256,256]{1,0:T(8,128)S(1)}, f32[256,256]{1,0:T(8,128)S(1)}, u32[]{:S(2)}, u32[]{:S(2)}) collective-permute-start(f32[256,256]{1,0:T(8,128)S(1)} %add.206), channel_id=1, source_target_pairs={{0,4},{1,5},{2,6},{3,7},{4,0},{5,1},{6,2},{7,3},{8,12},{9,13},{10,... | collective-permute-start | bytes 786440 | tf_op jit(solution)/shard_map/ppermute | solution.py:34
  92.9 9.4 %collective-permute-done.13 = f32[256,256]{1,0:T(8,128)S(1)} collective-permute-done((f32[256,256]{1,0:T(8,128)S(1)}, f32[256,256]{1,0:T(8,128)S(1)}, u32[]{:S(2)}, u32[]{:S(2)}) %collective-permute-start.13) | collective-permute-done | bytes 262176 | tf_op jit(solution)/shard_map/ppermute | solution.py:34
  102.3 2.6 collective-permute-done.14
  107.3 6.9 %collective-permute-done.15 = bf16[256,256]{0,1:T(8,128)(2,1)S(1)} collective-permute-done((bf16[256,256]{0,1:T(8,128)(2,1)S(1)}, bf16[256,256]{0,1:T(8,128)(2,1)S(1)}, u32[]{:S(2)}, u32[]{:S(2)}) %collective-permute-start.15) | collective-permute-done | bytes 131104 | tf_op jit(solution)/shard_map/ppermute | solution.py:24
  117.7 5.4 %collective-permute-start.18 = (f32[2,256,256]{2,1,0:T(8,128)S(1)}, f32[2,256,256]{2,1,0:T(8,128)S(1)}, u32[]{:S(2)}, u32[]{:S(2)}) collective-permute-start(f32[2,256,256]{2,1,0:T(8,128)S(1)} %fusion.64), channel_id=1, source_target_pairs={{0,4},{1,5},{2,6},{3,7},{4,0},{5,1},{6,2},{7,3},{8,12},{9,13},{10,... | collective-permute-start | bytes 1572872 | tf_op jit(solution)/shard_map/ppermute | solution.py:34
  123.1 9.4 %collective-permute-done.17 = f32[2,256,256]{2,1,0:T(8,128)S(1)} collective-permute-done((f32[2,256,256]{2,1,0:T(8,128)S(1)}, f32[2,256,256]{2,1,0:T(8,128)S(1)}, u32[]{:S(2)}, u32[]{:S(2)}) %collective-permute-start.17) | collective-permute-done | bytes 524320 | tf_op jit(solution)/shard_map/ppermute | solution.py:34
  132.5 13.9 %collective-permute-done.18 = f32[2,256,256]{2,1,0:T(8,128)S(1)} collective-permute-done((f32[2,256,256]{2,1,0:T(8,128)S(1)}, f32[2,256,256]{2,1,0:T(8,128)S(1)}, u32[]{:S(2)}, u32[]{:S(2)}) %collective-permute-start.18) | collective-permute-done | bytes 524320 | tf_op jit(solution)/shard_map/ppermute | solution.py:34
  146.4 2.6 collective-permute-done.19
  150.9 2.9 collective-permute-start.21
  154.0 10.1 %collective-permute-done.20 = f32[2,256,256]{2,1,0:T(8,128)S(1)} collective-permute-done((f32[2,256,256]{2,1,0:T(8,128)S(1)}, f32[2,256,256]{2,1,0:T(8,128)S(1)}, u32[]{:S(2)}, u32[]{:S(2)}) %collective-permute-start.20) | collective-permute-done | bytes 524320 | tf_op jit(solution)/shard_map/ppermute | solution.py:34
  164.1 11.5 %collective-permute-done.21 = f32[2,256,256]{2,1,0:T(8,128)S(1)} collective-permute-done((f32[2,256,256]{2,1,0:T(8,128)S(1)}, f32[2,256,256]{2,1,0:T(8,128)S(1)}, u32[]{:S(2)}, u32[]{:S(2)}) %collective-permute-start.21) | collective-permute-done | bytes 524320 | tf_op jit(solution)/shard_map/ppermute | solution.py:34
  175.6 2.6 collective-permute-done.22
  180.3 7.1 %collective-permute-done.23 = bf16[256,256]{0,1:T(8,128)(2,1)S(1)} collective-permute-done((bf16[256,256]{0,1:T(8,128)(2,1)S(1)}, bf16[256,256]{0,1:T(8,128)(2,1)S(1)}, u32[]{:S(2)}, u32[]{:S(2)}) %collective-permute-start.23) | collective-permute-done | bytes 131104 | tf_op jit(solution)/shard_map/ppermute | solution.py:24
  189.4 5.0 %collective-permute-start.26 = (f32[256,256]{1,0:T(8,128)S(1)}, f32[256,256]{1,0:T(8,128)S(1)}, u32[]{:S(2)}, u32[]{:S(2)}) collective-permute-start(f32[256,256]{1,0:T(8,128)S(1)} %add.221), channel_id=1, source_target_pairs={{0,4},{1,5},{2,6},{3,7},{4,0},{5,1},{6,2},{7,3},{8,12},{9,13},{10,... | collective-permute-start | bytes 786440 | tf_op jit(solution)/shard_map/ppermute | solution.py:34
  194.4 4.2 %collective-permute-done.25 = f32[256,256]{1,0:T(8,128)S(1)} collective-permute-done((f32[256,256]{1,0:T(8,128)S(1)}, f32[256,256]{1,0:T(8,128)S(1)}, u32[]{:S(2)}, u32[]{:S(2)}) %collective-permute-start.25) | collective-permute-done | bytes 262176 | tf_op jit(solution)/shard_map/ppermute | solution.py:34
  198.6 7.9 %collective-permute-done.26 = f32[256,256]{1,0:T(8,128)S(1)} collective-permute-done((f32[256,256]{1,0:T(8,128)S(1)}, f32[256,256]{1,0:T(8,128)S(1)}, u32[]{:S(2)}, u32[]{:S(2)}) %collective-permute-start.26) | collective-permute-done | bytes 262176 | tf_op jit(solution)/shard_map/ppermute | solution.py:34
  211.6 7.6 %collective-permute-done.28 = bf16[256,256]{0,1:T(8,128)(2,1)S(1)} collective-permute-done((bf16[256,256]{0,1:T(8,128)(2,1)}, bf16[256,256]{0,1:T(8,128)(2,1)S(1)}, u32[]{:S(2)}, u32[]{:S(2)}) %collective-permute-start.28) | collective-permute-done | bytes 131104 | tf_op jit(solution)/shard_map/ppermute | solution.py:24
  223.0 4.8 %collective-permute-start.31 = (f32[256,256]{0,1:T(8,128)S(1)}, f32[256,256]{0,1:T(8,128)S(1)}, u32[]{:S(2)}, u32[]{:S(2)}) collective-permute-start(f32[256,256]{0,1:T(8,128)S(1)} %add.226), channel_id=1, source_target_pairs={{0,4},{1,5},{2,6},{3,7},{4,0},{5,1},{6,2},{7,3},{8,12},{9,13},{10,... | collective-permute-start | bytes 786440 | tf_op jit(solution)/shard_map/ppermute | solution.py:34
  232.2 7.7 %collective-permute-done.31 = f32[256,256]{0,1:T(8,128)S(1)} collective-permute-done((f32[256,256]{0,1:T(8,128)S(1)}, f32[256,256]{0,1:T(8,128)S(1)}, u32[]{:S(2)}, u32[]{:S(2)}) %collective-permute-start.31) | collective-permute-done | bytes 262176 | tf_op jit(solution)/shard_map/ppermute | solution.py:34
  239.9 2.6 collective-permute-done.32
  244.4 9.2 %collective-permute-start.33 = (bf16[256,256]{0,1:T(8,128)(2,1)S(1)}, bf16[256,256]{0,1:T(8,128)(2,1)S(1)}, u32[]{:S(2)}, u32[]{:S(2)}) collective-permute-start(bf16[256,256]{0,1:T(8,128)(2,1)S(1)} %get-tuple-element.18), channel_id=1, source_target_pairs={{0,32},{1,24},{2,40},{6,16},{3,48},{7,8},{4,56},{5,0},{9,41},{8,33... | collective-permute-start | bytes 393224 | tf_op jit(solution)/shard_map/ppermute | solution.py:24
  254.5 6.1 %collective-permute-done.33 = bf16[256,256]{0,1:T(8,128)(2,1)S(1)} collective-permute-done((bf16[256,256]{0,1:T(8,128)(2,1)S(1)}, bf16[256,256]{0,1:T(8,128)(2,1)S(1)}, u32[]{:S(2)}, u32[]{:S(2)}) %collective-permute-start.33) | collective-permute-done | bytes 131104 | tf_op jit(solution)/shard_map/ppermute | solution.py:24
  264.4 5.6 %collective-permute-start.36 = (f32[256,256]{0,1:T(8,128)S(1)}, f32[256,256]{0,1:T(8,128)S(1)}, u32[]{:S(2)}, u32[]{:S(2)}) collective-permute-start(f32[256,256]{0,1:T(8,128)S(1)} %add.232), channel_id=1, source_target_pairs={{0,4},{1,5},{2,6},{3,7},{4,0},{5,1},{6,2},{7,3},{8,12},{9,13},{10,... | collective-permute-start | bytes 786440 | tf_op jit(solution)/shard_map/ppermute | solution.py:34
  269.9 3.6 collective-permute-done.35
  273.5 8.4 %collective-permute-done.36 = f32[256,256]{0,1:T(8,128)S(1)} collective-permute-done((f32[256,256]{0,1:T(8,128)S(1)}, f32[256,256]{0,1:T(8,128)S(1)}, u32[]{:S(2)}, u32[]{:S(2)}) %collective-permute-start.36) | collective-permute-done | bytes 262176 | tf_op jit(solution)/shard_map/ppermute | solution.py:34
  285.7 6.9 %collective-permute-done.38 = bf16[256,256]{0,1:T(8,128)(2,1)S(1)} collective-permute-done((bf16[256,256]{0,1:T(8,128)(2,1)S(1)}, bf16[256,256]{0,1:T(8,128)(2,1)S(1)}, u32[]{:S(2)}, u32[]{:S(2)}) %collective-permute-start.38) | collective-permute-done | bytes 131104 | tf_op jit(solution)/shard_map/ppermute | solution.py:24
  295.5 5.3 %collective-permute-start.41 = (f32[256,256]{0,1:T(8,128)S(1)}, f32[256,256]{0,1:T(8,128)S(1)}, u32[]{:S(2)}, u32[]{:S(2)}) collective-permute-start(f32[256,256]{0,1:T(8,128)S(1)} %add.239), channel_id=1, source_target_pairs={{0,4},{1,5},{2,6},{3,7},{4,0},{5,1},{6,2},{7,3},{8,12},{9,13},{10,... | collective-permute-start | bytes 786440 | tf_op jit(solution)/shard_map/ppermute | solution.py:34
  301.0 3.0 collective-permute-done.40
  304.0 8.8 %collective-permute-done.41 = f32[256,256]{0,1:T(8,128)S(1)} collective-permute-done((f32[256,256]{0,1:T(8,128)S(1)}, f32[256,256]{0,1:T(8,128)S(1)}, u32[]{:S(2)}, u32[]{:S(2)}) %collective-permute-start.41) | collective-permute-done | bytes 262176 | tf_op jit(solution)/shard_map/ppermute | solution.py:34
  312.8 2.6 collective-permute-done.42
  316.5 7.0 %collective-permute-done.43 = bf16[256,256]{0,1:T(8,128)(2,1)S(1)} collective-permute-done((bf16[256,256]{0,1:T(8,128)(2,1)S(1)}, bf16[256,256]{0,1:T(8,128)(2,1)S(1)}, u32[]{:S(2)}, u32[]{:S(2)}) %collective-permute-start.43) | collective-permute-done | bytes 131104 | tf_op jit(solution)/shard_map/ppermute | solution.py:24
  327.7 5.0 %collective-permute-start.46 = (f32[256,256]{0,1:T(8,128)S(1)}, f32[256,256]{0,1:T(8,128)S(1)}, u32[]{:S(2)}, u32[]{:S(2)}) collective-permute-start(f32[256,256]{0,1:T(8,128)S(1)} %add.247), channel_id=1, source_target_pairs={{0,4},{1,5},{2,6},{3,7},{4,0},{5,1},{6,2},{7,3},{8,12},{9,13},{10,... | collective-permute-start | bytes 786440 | tf_op jit(solution)/shard_map/ppermute | solution.py:34
  333.1 3.7 collective-permute-done.45
  336.9 7.8 %collective-permute-done.46 = f32[256,256]{0,1:T(8,128)S(1)} collective-permute-done((f32[256,256]{0,1:T(8,128)S(1)}, f32[256,256]{0,1:T(8,128)S(1)}, u32[]{:S(2)}, u32[]{:S(2)}) %collective-permute-start.46) | collective-permute-done | bytes 262176 | tf_op jit(solution)/shard_map/ppermute | solution.py:34
  348.5 6.9 %collective-permute-done.48 = bf16[256,256]{0,1:T(8,128)(2,1)S(1)} collective-permute-done((bf16[256,256]{0,1:T(8,128)(2,1)S(1)}, bf16[256,256]{0,1:T(8,128)(2,1)S(1)}, u32[]{:S(2)}, u32[]{:S(2)}) %collective-permute-start.48) | collective-permute-done | bytes 131104 | tf_op jit(solution)/shard_map/ppermute | solution.py:24
  359.0 4.3 %collective-permute-start.51 = (f32[256,256]{1,0:T(8,128)S(1)}, f32[256,256]{1,0:T(8,128)S(1)}, u32[]{:S(2)}, u32[]{:S(2)}) collective-permute-start(f32[256,256]{1,0:T(8,128)S(1)} %add.252), channel_id=1, source_target_pairs={{0,4},{1,5},{2,6},{3,7},{4,0},{5,1},{6,2},{7,3},{8,12},{9,13},{10,... | collective-permute-start | bytes 786440 | tf_op jit(solution)/shard_map/ppermute | solution.py:34
  365.0 3.1 collective-permute-done.50
  368.1 7.2 %collective-permute-done.51 = f32[256,256]{1,0:T(8,128)S(1)} collective-permute-done((f32[256,256]{1,0:T(8,128)S(1)}, f32[256,256]{1,0:T(8,128)S(1)}, u32[]{:S(2)}, u32[]{:S(2)}) %collective-permute-start.51) | collective-permute-done | bytes 262176 | tf_op jit(solution)/shard_map/ppermute | solution.py:34
  (162 shorter events, 78.4 us)
Async XLA Ops:
  3.3 11.9 %collective-permute-start = (bf16[256,256]{1,0:T(8,128)(2,1)S(1)}, bf16[256,256]{1,0:T(8,128)(2,1)S(1)}, u32[]{:S(2)}, u32[]{:S(2)}) collective-permute-start(bf16[256,256]{1,0:T(8,128)(2,1)S(1)} %get-tuple-element.6), channel_id=1, source_target_pairs={{0,32},{1,24},{2,40},{6,16},{3,48},{7,8},{4,56},{5,0},{9,41},{8,33... | collective-permute-start | bytes 393224 | tf_op jit(solution)/shard_map/ppermute | solution.py:24
  17.1 8.7 %collective-permute-start.2 = (f32[256,256]{1,0:T(8,128)S(1)}, f32[256,256]{1,0:T(8,128)S(1)}, u32[]{:S(2)}, u32[]{:S(2)}) collective-permute-start(f32[256,256]{1,0:T(8,128)S(1)} %add.193), channel_id=1, source_target_pairs={{0,2},{1,3},{2,0},{3,1},{4,6},{5,7},{6,4},{7,5},{8,10},{9,11},{10,... | collective-permute-start | bytes 786440 | tf_op jit(solution)/shard_map/ppermute | solution.py:34
  17.2 19.9 %collective-permute-start.3 = (f32[256,256]{1,0:T(8,128)S(1)}, f32[256,256]{1,0:T(8,128)S(1)}, u32[]{:S(2)}, u32[]{:S(2)}) collective-permute-start(f32[256,256]{1,0:T(8,128)S(1)} %add.193), channel_id=1, source_target_pairs={{0,4},{1,5},{2,6},{3,7},{4,0},{5,1},{6,2},{7,3},{8,12},{9,13},{10,... | collective-permute-start | bytes 786440 | tf_op jit(solution)/shard_map/ppermute | solution.py:34
  25.1 14.6 %collective-permute-start.4 = (f32[256,256]{1,0:T(8,128)S(1)}, f32[256,256]{1,0:T(8,128)S(1)}, u32[]{:S(2)}, u32[]{:S(2)}) collective-permute-start(f32[256,256]{1,0:T(8,128)S(1)} %add.193), channel_id=1, source_target_pairs={{0,6},{1,7},{2,4},{3,5},{4,2},{5,3},{6,0},{7,1},{8,14},{9,15},{10,... | collective-permute-start | bytes 786440 | tf_op jit(solution)/shard_map/ppermute | solution.py:34
  40.9 7.2 %collective-permute-start.5 = (bf16[256,256]{0,1:T(8,128)(2,1)S(1)}, bf16[256,256]{0,1:T(8,128)(2,1)S(1)}, u32[]{:S(2)}, u32[]{:S(2)}) collective-permute-start(bf16[256,256]{0,1:T(8,128)(2,1)S(1)} %get-tuple-element.8), channel_id=1, source_target_pairs={{0,32},{1,24},{2,40},{6,16},{3,48},{7,8},{4,56},{5,0},{9,41},{8,33... | collective-permute-start | bytes 393224 | tf_op jit(solution)/shard_map/ppermute | solution.py:24
  50.2 9.3 %collective-permute-start.7 = (f32[256,256]{1,0:T(8,128)S(1)}, f32[256,256]{1,0:T(8,128)S(1)}, u32[]{:S(2)}, u32[]{:S(2)}) collective-permute-start(f32[256,256]{1,0:T(8,128)S(1)} %add.199), channel_id=1, source_target_pairs={{0,2},{1,3},{2,0},{3,1},{4,6},{5,7},{6,4},{7,5},{8,10},{9,11},{10,... | collective-permute-start | bytes 786440 | tf_op jit(solution)/shard_map/ppermute | solution.py:34
  50.4 19.2 %collective-permute-start.8 = (f32[256,256]{1,0:T(8,128)S(1)}, f32[256,256]{1,0:T(8,128)S(1)}, u32[]{:S(2)}, u32[]{:S(2)}) collective-permute-start(f32[256,256]{1,0:T(8,128)S(1)} %add.199), channel_id=1, source_target_pairs={{0,4},{1,5},{2,6},{3,7},{4,0},{5,1},{6,2},{7,3},{8,12},{9,13},{10,... | collective-permute-start | bytes 786440 | tf_op jit(solution)/shard_map/ppermute | solution.py:34
  57.6 14.6 %collective-permute-start.9 = (f32[256,256]{1,0:T(8,128)S(1)}, f32[256,256]{1,0:T(8,128)S(1)}, u32[]{:S(2)}, u32[]{:S(2)}) collective-permute-start(f32[256,256]{1,0:T(8,128)S(1)} %add.199), channel_id=1, source_target_pairs={{0,6},{1,7},{2,4},{3,5},{4,2},{5,3},{6,0},{7,1},{8,14},{9,15},{10,... | collective-permute-start | bytes 786440 | tf_op jit(solution)/shard_map/ppermute | solution.py:34
  74.1 7.2 %collective-permute-start.10 = (bf16[256,256]{0,1:T(8,128)(2,1)S(1)}, bf16[256,256]{0,1:T(8,128)(2,1)S(1)}, u32[]{:S(2)}, u32[]{:S(2)}) collective-permute-start(bf16[256,256]{0,1:T(8,128)(2,1)S(1)} %get-tuple-element.10), channel_id=1, source_target_pairs={{0,32},{1,24},{2,40},{6,16},{3,48},{7,8},{4,56},{5,0},{9,41},{8,33... | collective-permute-start | bytes 393224 | tf_op jit(solution)/shard_map/ppermute | solution.py:24
  83.7 9.3 %collective-permute-start.12 = (f32[256,256]{1,0:T(8,128)S(1)}, f32[256,256]{1,0:T(8,128)S(1)}, u32[]{:S(2)}, u32[]{:S(2)}) collective-permute-start(f32[256,256]{1,0:T(8,128)S(1)} %add.206), channel_id=1, source_target_pairs={{0,2},{1,3},{2,0},{3,1},{4,6},{5,7},{6,4},{7,5},{8,10},{9,11},{10,... | collective-permute-start | bytes 786440 | tf_op jit(solution)/shard_map/ppermute | solution.py:34
  83.8 18.6 %collective-permute-start.13 = (f32[256,256]{1,0:T(8,128)S(1)}, f32[256,256]{1,0:T(8,128)S(1)}, u32[]{:S(2)}, u32[]{:S(2)}) collective-permute-start(f32[256,256]{1,0:T(8,128)S(1)} %add.206), channel_id=1, source_target_pairs={{0,4},{1,5},{2,6},{3,7},{4,0},{5,1},{6,2},{7,3},{8,12},{9,13},{10,... | collective-permute-start | bytes 786440 | tf_op jit(solution)/shard_map/ppermute | solution.py:34
  90.3 14.6 %collective-permute-start.14 = (f32[256,256]{1,0:T(8,128)S(1)}, f32[256,256]{1,0:T(8,128)S(1)}, u32[]{:S(2)}, u32[]{:S(2)}) collective-permute-start(f32[256,256]{1,0:T(8,128)S(1)} %add.206), channel_id=1, source_target_pairs={{0,6},{1,7},{2,4},{3,5},{4,2},{5,3},{6,0},{7,1},{8,14},{9,15},{10,... | collective-permute-start | bytes 786440 | tf_op jit(solution)/shard_map/ppermute | solution.py:34
  106.8 7.3 %collective-permute-start.15 = (bf16[256,256]{0,1:T(8,128)(2,1)S(1)}, bf16[256,256]{0,1:T(8,128)(2,1)S(1)}, u32[]{:S(2)}, u32[]{:S(2)}) collective-permute-start(bf16[256,256]{0,1:T(8,128)(2,1)S(1)} %get-tuple-element.12), channel_id=1, source_target_pairs={{0,32},{1,24},{2,40},{6,16},{3,48},{7,8},{4,56},{5,0},{9,41},{8,33... | collective-permute-start | bytes 393224 | tf_op jit(solution)/shard_map/ppermute | solution.py:24
  115.1 2.5 collective-permute-start.16
  117.6 14.9 %collective-permute-start.17 = (f32[2,256,256]{2,1,0:T(8,128)S(1)}, f32[2,256,256]{2,1,0:T(8,128)S(1)}, u32[]{:S(2)}, u32[]{:S(2)}) collective-permute-start(f32[2,256,256]{2,1,0:T(8,128)S(1)} %fusion.64), channel_id=1, source_target_pairs={{0,2},{1,3},{2,0},{3,1},{4,6},{5,7},{6,4},{7,5},{8,10},{9,11},{10,... | collective-permute-start | bytes 1572872 | tf_op jit(solution)/shard_map/ppermute | solution.py:34
  117.7 28.7 %collective-permute-start.18 = (f32[2,256,256]{2,1,0:T(8,128)S(1)}, f32[2,256,256]{2,1,0:T(8,128)S(1)}, u32[]{:S(2)}, u32[]{:S(2)}) collective-permute-start(f32[2,256,256]{2,1,0:T(8,128)S(1)} %fusion.64), channel_id=1, source_target_pairs={{0,4},{1,5},{2,6},{3,7},{4,0},{5,1},{6,2},{7,3},{8,12},{9,13},{10,... | collective-permute-start | bytes 1572872 | tf_op jit(solution)/shard_map/ppermute | solution.py:34
  123.1 25.9 %collective-permute-start.19 = (f32[2,256,256]{2,1,0:T(8,128)S(1)}, f32[2,256,256]{2,1,0:T(8,128)S(1)}, u32[]{:S(2)}, u32[]{:S(2)}) collective-permute-start(f32[2,256,256]{2,1,0:T(8,128)S(1)} %fusion.64), channel_id=1, source_target_pairs={{0,6},{1,7},{2,4},{3,5},{4,2},{5,3},{6,0},{7,1},{8,14},{9,15},{10,... | collective-permute-start | bytes 1572872 | tf_op jit(solution)/shard_map/ppermute | solution.py:34
  149.2 14.9 %collective-permute-start.20 = (f32[2,256,256]{2,1,0:T(8,128)S(1)}, f32[2,256,256]{2,1,0:T(8,128)S(1)}, u32[]{:S(2)}, u32[]{:S(2)}) collective-permute-start(f32[2,256,256]{2,1,0:T(8,128)S(1)} %add_add_fusion.1), channel_id=1, source_target_pairs={{0,64},{64,0},{128,192},{192,128},{1,65},{65,1},{129,193},{193,129... | collective-permute-start | bytes 1572872 | tf_op jit(solution)/shard_map/ppermute | solution.py:34
  150.9 24.7 %collective-permute-start.21 = (f32[2,256,256]{2,1,0:T(8,128)S(1)}, f32[2,256,256]{2,1,0:T(8,128)S(1)}, u32[]{:S(2)}, u32[]{:S(2)}) collective-permute-start(f32[2,256,256]{2,1,0:T(8,128)S(1)} %add_add_fusion.1), channel_id=1, source_target_pairs={{0,128},{64,192},{128,0},{192,64},{1,129},{65,193},{129,1},{193,65... | collective-permute-start | bytes 1572872 | tf_op jit(solution)/shard_map/ppermute | solution.py:34
  153.7 24.4 %collective-permute-start.22 = (f32[2,256,256]{2,1,0:T(8,128)S(1)}, f32[2,256,256]{2,1,0:T(8,128)S(1)}, u32[]{:S(2)}, u32[]{:S(2)}) collective-permute-start(f32[2,256,256]{2,1,0:T(8,128)S(1)} %add_add_fusion.1), channel_id=1, source_target_pairs={{0,192},{64,128},{128,64},{192,0},{1,193},{65,129},{129,65},{193,1... | collective-permute-start | bytes 1572872 | tf_op jit(solution)/shard_map/ppermute | solution.py:34
  180.2 7.2 %collective-permute-start.23 = (bf16[256,256]{0,1:T(8,128)(2,1)S(1)}, bf16[256,256]{0,1:T(8,128)(2,1)S(1)}, u32[]{:S(2)}, u32[]{:S(2)}) collective-permute-start(bf16[256,256]{0,1:T(8,128)(2,1)S(1)} %get-tuple-element.14), channel_id=1, source_target_pairs={{0,32},{1,24},{2,40},{6,16},{3,48},{7,8},{4,56},{5,0},{9,41},{8,33... | collective-permute-start | bytes 393224 | tf_op jit(solution)/shard_map/ppermute | solution.py:24
  189.3 9.3 %collective-permute-start.25 = (f32[256,256]{1,0:T(8,128)S(1)}, f32[256,256]{1,0:T(8,128)S(1)}, u32[]{:S(2)}, u32[]{:S(2)}) collective-permute-start(f32[256,256]{1,0:T(8,128)S(1)} %add.221), channel_id=1, source_target_pairs={{0,2},{1,3},{2,0},{3,1},{4,6},{5,7},{6,4},{7,5},{8,10},{9,11},{10,... | collective-permute-start | bytes 786440 | tf_op jit(solution)/shard_map/ppermute | solution.py:34
  189.4 17.0 %collective-permute-start.26 = (f32[256,256]{1,0:T(8,128)S(1)}, f32[256,256]{1,0:T(8,128)S(1)}, u32[]{:S(2)}, u32[]{:S(2)}) collective-permute-start(f32[256,256]{1,0:T(8,128)S(1)} %add.221), channel_id=1, source_target_pairs={{0,4},{1,5},{2,6},{3,7},{4,0},{5,1},{6,2},{7,3},{8,12},{9,13},{10,... | collective-permute-start | bytes 786440 | tf_op jit(solution)/shard_map/ppermute | solution.py:34
  194.4 14.7 %collective-permute-start.27 = (f32[256,256]{1,0:T(8,128)S(1)}, f32[256,256]{1,0:T(8,128)}, u32[]{:S(2)}, u32[]{:S(2)}) collective-permute-start(f32[256,256]{1,0:T(8,128)S(1)} %add.221), channel_id=1, source_target_pairs={{0,6},{1,7},{2,4},{3,5},{4,2},{5,3},{6,0},{7,1},{8,14},{9,15},{10,... | collective-permute-start | bytes 786440 | tf_op jit(solution)/shard_map/ppermute | solution.py:34
  211.6 7.6 %collective-permute-start.28 = (bf16[256,256]{0,1:T(8,128)(2,1)}, bf16[256,256]{0,1:T(8,128)(2,1)S(1)}, u32[]{:S(2)}, u32[]{:S(2)}) collective-permute-start(bf16[256,256]{0,1:T(8,128)(2,1)} %get-tuple-element.16), channel_id=1, source_target_pairs={{0,32},{1,24},{2,40},{6,16},{3,48},{7,8},{4,56},{5,0},{9,41},{8,33... | collective-permute-start | bytes 393224 | tf_op jit(solution)/shard_map/ppermute | solution.py:24
  219.4 3.5 collective-permute-start.29
  222.9 9.3 %collective-permute-start.30 = (f32[256,256]{0,1:T(8,128)S(1)}, f32[256,256]{0,1:T(8,128)S(1)}, u32[]{:S(2)}, u32[]{:S(2)}) collective-permute-start(f32[256,256]{0,1:T(8,128)S(1)} %add.226), channel_id=1, source_target_pairs={{0,2},{1,3},{2,0},{3,1},{4,6},{5,7},{6,4},{7,5},{8,10},{9,11},{10,... | collective-permute-start | bytes 786440 | tf_op jit(solution)/shard_map/ppermute | solution.py:34
  223.0 16.8 %collective-permute-start.31 = (f32[256,256]{0,1:T(8,128)S(1)}, f32[256,256]{0,1:T(8,128)S(1)}, u32[]{:S(2)}, u32[]{:S(2)}) collective-permute-start(f32[256,256]{0,1:T(8,128)S(1)} %add.226), channel_id=1, source_target_pairs={{0,4},{1,5},{2,6},{3,7},{4,0},{5,1},{6,2},{7,3},{8,12},{9,13},{10,... | collective-permute-start | bytes 786440 | tf_op jit(solution)/shard_map/ppermute | solution.py:34
  227.8 14.6 %collective-permute-start.32 = (f32[256,256]{0,1:T(8,128)S(1)}, f32[256,256]{0,1:T(8,128)S(1)}, u32[]{:S(2)}, u32[]{:S(2)}) collective-permute-start(f32[256,256]{0,1:T(8,128)S(1)} %add.226), channel_id=1, source_target_pairs={{0,6},{1,7},{2,4},{3,5},{4,2},{5,3},{6,0},{7,1},{8,14},{9,15},{10,... | collective-permute-start | bytes 786440 | tf_op jit(solution)/shard_map/ppermute | solution.py:34
  244.4 16.3 %collective-permute-start.33 = (bf16[256,256]{0,1:T(8,128)(2,1)S(1)}, bf16[256,256]{0,1:T(8,128)(2,1)S(1)}, u32[]{:S(2)}, u32[]{:S(2)}) collective-permute-start(bf16[256,256]{0,1:T(8,128)(2,1)S(1)} %get-tuple-element.18), channel_id=1, source_target_pairs={{0,32},{1,24},{2,40},{6,16},{3,48},{7,8},{4,56},{5,0},{9,41},{8,33... | collective-permute-start | bytes 393224 | tf_op jit(solution)/shard_map/ppermute | solution.py:24
  261.1 3.2 collective-permute-start.34
  264.3 9.3 %collective-permute-start.35 = (f32[256,256]{0,1:T(8,128)S(1)}, f32[256,256]{0,1:T(8,128)S(1)}, u32[]{:S(2)}, u32[]{:S(2)}) collective-permute-start(f32[256,256]{0,1:T(8,128)S(1)} %add.232), channel_id=1, source_target_pairs={{0,2},{1,3},{2,0},{3,1},{4,6},{5,7},{6,4},{7,5},{8,10},{9,11},{10,... | collective-permute-start | bytes 786440 | tf_op jit(solution)/shard_map/ppermute | solution.py:34
  264.4 17.6 %collective-permute-start.36 = (f32[256,256]{0,1:T(8,128)S(1)}, f32[256,256]{0,1:T(8,128)S(1)}, u32[]{:S(2)}, u32[]{:S(2)}) collective-permute-start(f32[256,256]{0,1:T(8,128)S(1)} %add.232), channel_id=1, source_target_pairs={{0,4},{1,5},{2,6},{3,7},{4,0},{5,1},{6,2},{7,3},{8,12},{9,13},{10,... | collective-permute-start | bytes 786440 | tf_op jit(solution)/shard_map/ppermute | solution.py:34
  269.9 14.6 %collective-permute-start.37 = (f32[256,256]{0,1:T(8,128)S(1)}, f32[256,256]{0,1:T(8,128)S(1)}, u32[]{:S(2)}, u32[]{:S(2)}) collective-permute-start(f32[256,256]{0,1:T(8,128)S(1)} %add.232), channel_id=1, source_target_pairs={{0,6},{1,7},{2,4},{3,5},{4,2},{5,3},{6,0},{7,1},{8,14},{9,15},{10,... | collective-permute-start | bytes 786440 | tf_op jit(solution)/shard_map/ppermute | solution.py:34
  285.5 7.1 %collective-permute-start.38 = (bf16[256,256]{0,1:T(8,128)(2,1)S(1)}, bf16[256,256]{0,1:T(8,128)(2,1)S(1)}, u32[]{:S(2)}, u32[]{:S(2)}) collective-permute-start(bf16[256,256]{0,1:T(8,128)(2,1)S(1)} %get-tuple-element.20), channel_id=1, source_target_pairs={{0,32},{1,24},{2,40},{6,16},{3,48},{7,8},{4,56},{5,0},{9,41},{8,33... | collective-permute-start | bytes 393224 | tf_op jit(solution)/shard_map/ppermute | solution.py:24
  294.7 9.3 %collective-permute-start.40 = (f32[256,256]{0,1:T(8,128)S(1)}, f32[256,256]{0,1:T(8,128)S(1)}, u32[]{:S(2)}, u32[]{:S(2)}) collective-permute-start(f32[256,256]{0,1:T(8,128)S(1)} %add.239), channel_id=1, source_target_pairs={{0,2},{1,3},{2,0},{3,1},{4,6},{5,7},{6,4},{7,5},{8,10},{9,11},{10,... | collective-permute-start | bytes 786440 | tf_op jit(solution)/shard_map/ppermute | solution.py:34
  295.5 17.3 %collective-permute-start.41 = (f32[256,256]{0,1:T(8,128)S(1)}, f32[256,256]{0,1:T(8,128)S(1)}, u32[]{:S(2)}, u32[]{:S(2)}) collective-permute-start(f32[256,256]{0,1:T(8,128)S(1)} %add.239), channel_id=1, source_target_pairs={{0,4},{1,5},{2,6},{3,7},{4,0},{5,1},{6,2},{7,3},{8,12},{9,13},{10,... | collective-permute-start | bytes 786440 | tf_op jit(solution)/shard_map/ppermute | solution.py:34
  300.8 14.6 %collective-permute-start.42 = (f32[256,256]{0,1:T(8,128)S(1)}, f32[256,256]{0,1:T(8,128)S(1)}, u32[]{:S(2)}, u32[]{:S(2)}) collective-permute-start(f32[256,256]{0,1:T(8,128)S(1)} %add.239), channel_id=1, source_target_pairs={{0,6},{1,7},{2,4},{3,5},{4,2},{5,3},{6,0},{7,1},{8,14},{9,15},{10,... | collective-permute-start | bytes 786440 | tf_op jit(solution)/shard_map/ppermute | solution.py:34
  316.3 7.2 %collective-permute-start.43 = (bf16[256,256]{0,1:T(8,128)(2,1)S(1)}, bf16[256,256]{0,1:T(8,128)(2,1)S(1)}, u32[]{:S(2)}, u32[]{:S(2)}) collective-permute-start(bf16[256,256]{0,1:T(8,128)(2,1)S(1)} %get-tuple-element.22), channel_id=1, source_target_pairs={{0,32},{1,24},{2,40},{6,16},{3,48},{7,8},{4,56},{5,0},{9,41},{8,33... | collective-permute-start | bytes 393224 | tf_op jit(solution)/shard_map/ppermute | solution.py:24
  324.0 3.6 collective-permute-start.44
  327.6 9.3 %collective-permute-start.45 = (f32[256,256]{0,1:T(8,128)S(1)}, f32[256,256]{0,1:T(8,128)S(1)}, u32[]{:S(2)}, u32[]{:S(2)}) collective-permute-start(f32[256,256]{0,1:T(8,128)S(1)} %add.247), channel_id=1, source_target_pairs={{0,2},{1,3},{2,0},{3,1},{4,6},{5,7},{6,4},{7,5},{8,10},{9,11},{10,... | collective-permute-start | bytes 786440 | tf_op jit(solution)/shard_map/ppermute | solution.py:34
  327.7 17.0 %collective-permute-start.46 = (f32[256,256]{0,1:T(8,128)S(1)}, f32[256,256]{0,1:T(8,128)S(1)}, u32[]{:S(2)}, u32[]{:S(2)}) collective-permute-start(f32[256,256]{0,1:T(8,128)S(1)} %add.247), channel_id=1, source_target_pairs={{0,4},{1,5},{2,6},{3,7},{4,0},{5,1},{6,2},{7,3},{8,12},{9,13},{10,... | collective-permute-start | bytes 786440 | tf_op jit(solution)/shard_map/ppermute | solution.py:34
  332.7 14.6 %collective-permute-start.47 = (f32[256,256]{0,1:T(8,128)S(1)}, f32[256,256]{0,1:T(8,128)S(1)}, u32[]{:S(2)}, u32[]{:S(2)}) collective-permute-start(f32[256,256]{0,1:T(8,128)S(1)} %add.247), channel_id=1, source_target_pairs={{0,6},{1,7},{2,4},{3,5},{4,2},{5,3},{6,0},{7,1},{8,14},{9,15},{10,... | collective-permute-start | bytes 786440 | tf_op jit(solution)/shard_map/ppermute | solution.py:34
  348.3 7.1 %collective-permute-start.48 = (bf16[256,256]{0,1:T(8,128)(2,1)S(1)}, bf16[256,256]{0,1:T(8,128)(2,1)S(1)}, u32[]{:S(2)}, u32[]{:S(2)}) collective-permute-start(bf16[256,256]{0,1:T(8,128)(2,1)S(1)} %get-tuple-element.24), channel_id=1, source_target_pairs={{0,32},{1,24},{2,40},{6,16},{3,48},{7,8},{4,56},{5,0},{9,41},{8,33... | collective-permute-start | bytes 393224 | tf_op jit(solution)/shard_map/ppermute | solution.py:24
  355.9 3.0 collective-permute-start.49
  358.9 9.3 %collective-permute-start.50 = (f32[256,256]{1,0:T(8,128)S(1)}, f32[256,256]{1,0:T(8,128)S(1)}, u32[]{:S(2)}, u32[]{:S(2)}) collective-permute-start(f32[256,256]{1,0:T(8,128)S(1)} %add.252), channel_id=1, source_target_pairs={{0,2},{1,3},{2,0},{3,1},{4,6},{5,7},{6,4},{7,5},{8,10},{9,11},{10,... | collective-permute-start | bytes 786440 | tf_op jit(solution)/shard_map/ppermute | solution.py:34
  359.0 16.4 %collective-permute-start.51 = (f32[256,256]{1,0:T(8,128)S(1)}, f32[256,256]{1,0:T(8,128)S(1)}, u32[]{:S(2)}, u32[]{:S(2)}) collective-permute-start(f32[256,256]{1,0:T(8,128)S(1)} %add.252), channel_id=1, source_target_pairs={{0,4},{1,5},{2,6},{3,7},{4,0},{5,1},{6,2},{7,3},{8,12},{9,13},{10,... | collective-permute-start | bytes 786440 | tf_op jit(solution)/shard_map/ppermute | solution.py:34
  363.3 14.6 %collective-permute-start.52 = (f32[256,256]{1,0:T(8,128)S(1)}, f32[256,256]{1,0:T(8,128)S(1)}, u32[]{:S(2)}, u32[]{:S(2)}) collective-permute-start(f32[256,256]{1,0:T(8,128)S(1)} %add.252), channel_id=1, source_target_pairs={{0,6},{1,7},{2,4},{3,5},{4,2},{5,3},{6,0},{7,1},{8,14},{9,15},{10,... | collective-permute-start | bytes 786440 | tf_op jit(solution)/shard_map/ppermute | solution.py:34
  (22 other events, 426.7 us)
